TPU v7x, 256 devices: a whole 4x4x8 slice. The times are simulated.
256 devices in a mesh: lat: 32 (over z, x), lon: 8 (over y, core).
Axes of the slice: x: 4, y: 4, z: 8, core: 2. Of those that a mesh axis runs over, the one named last changes fastest.
Arguments:
- fields: bfloat16 [128, 720, 2, 512], P('lat', 'lon'), may hold values from -6 to 6
- coeffs: float32 [1024, 3], replicated, may hold values from -1.2 to 1.2
- entries: int32 [32, 4, 4, 128], replicated, may hold values from -3 to 1023, as said below
- band_info: int32 [32, 3], replicated, may hold values from 0 to 4, as said below
- conv_weight: bfloat16 [1536, 512], replicated, may hold values from -0.15625 to 0.15625
- mix_weight: bfloat16 [512, 512], replicated, may hold values from -0.25 to 0.25
Outputs:
- mixed: bfloat16 [128, 720, 2, 512], P('lat', 'lon')
Inputs may be any that keep to these rules, and one draw needn't show every extreme that they name: `entries`: in band b's list every in row lies in b's own rows b * 4 to (b + 1) * 4 - 1, every out row differs from its in row by at most 3, shifts are 0 to 6 and filter rows 0 to 1023. `band_info`: count is 1 to 4 and equals 4 in the first and the last band; ext_lo and ext_hi are 0 to 3 and both equal 3 in bands 0, 1 and the last band.
All inputs are finite; a program needn't handle non-finite values.
Results may differ from a plain program's by a relative error of at most 0.0065.
Values may be sent and summed in bfloat16 or wider, within the bound.
No kernel may reach another device: no remote copies, remote signals or barrier semaphores. Data moves between devices by JAX's collectives and lax.ppermute only.
A program may use at most 128 MiB of HBM per device.

v0:
```python
import jax
import jax.numpy as jnp
from jax import lax
from jax.sharding import PartitionSpec as P

CHANNELS = 512
BASIS = 3
SHIFTS = 7
OVERHANG = 3
LAT_DEV = 4


def shifted(value, axis, steps):
    count = lax.axis_size(axis)
    leading, last = (max(0, -steps), min(count, count - steps))
    return lax.ppermute(value, axis, [(source, source + steps) for source in range(leading, last)])


def band_coupling(
    entries,
    band_meta,
    coeffs,
    band_index,
    out_start,
    out_count,
    in_start,
    in_count,
    band_rows,
    grid_rows,
):
    nbands = entries.shape[0]
    clamped = jnp.clip(band_index, 0, nbands - 1)
    listed = lax.dynamic_index_in_dim(entries, clamped, 0, keepdims=False)
    meta = lax.dynamic_index_in_dim(band_meta, clamped, 0, keepdims=False)
    blocks = listed.shape[0]
    flattened = jnp.transpose(listed, (1, 0, 2)).reshape(4, blocks * 128)
    out_rows = flattened[0]
    in_rows = flattened[1]
    shifts = flattened[2]
    filter_rows = flattened[3]
    block_ids = jnp.arange(blocks * 128, dtype=jnp.int32) // 128
    own_rel = out_rows - clamped * band_rows
    usable = (band_index >= 0) & (band_index < nbands) & (block_ids < meta[0])
    usable = usable & (own_rel >= -meta[1]) & (own_rel < band_rows + meta[2])
    usable = usable & (out_rows >= 0) & (out_rows < grid_rows)
    filter_pick = (
        filter_rows[:, None] == jnp.arange(coeffs.shape[0], dtype=jnp.int32)[None, :]
    ).astype(jnp.float32)
    values = jnp.dot(
        filter_pick, coeffs, precision=lax.Precision.HIGHEST, preferred_element_type=jnp.float32
    )
    values = values * usable[:, None].astype(jnp.float32)
    out_hit = (
        (out_rows - out_start)[:, None] == jnp.arange(out_count, dtype=jnp.int32)[None, :]
    ).astype(jnp.float32)
    basis = coeffs.shape[1]
    left_side = (out_hit[:, :, None] * values[:, None, :]).reshape(blocks * 128, out_count * basis)
    in_hit = (
        (shifts * in_count + in_rows - in_start)[:, None]
        == jnp.arange(SHIFTS * in_count, dtype=jnp.int32)[None, :]
    ).astype(jnp.float32)
    return jnp.dot(
        left_side.T, in_hit, precision=lax.Precision.HIGHEST, preferred_element_type=jnp.float32
    )


def apply_filter(coupling, rows_in):
    row_count, nlon, members, pieces = rows_in.shape
    flattened = rows_in.reshape(row_count, nlon, members * pieces)
    stacked = jnp.concatenate(
        [jnp.roll(flattened, offset, axis=1) for offset in range(SHIFTS)], axis=0
    )
    stacked = stacked.reshape(SHIFTS * row_count, nlon * members * pieces)
    result = jnp.dot(coupling, stacked, preferred_element_type=jnp.float32)
    return result.reshape(-1, BASIS, nlon, members, pieces)


def mix_local(features, conv_weight, mix_weight):
    kernel = conv_weight.reshape(BASIS, CHANNELS, CHANNELS)
    combined = jnp.einsum("lkomc,kcd->lomd", features, kernel, preferred_element_type=jnp.float32)
    activated = jax.nn.gelu(combined, approximate=True).astype(jnp.bfloat16)
    return jnp.einsum(
        "lomc,cd->lomd", activated, mix_weight, preferred_element_type=jnp.float32
    ).astype(jnp.bfloat16)


def shards(fields, coeffs, entries, band_info, conv_weight, mix_weight):
    band_index = lax.axis_index("lat")
    grid_rows = LAT_DEV * lax.axis_size("lat")
    band_start = band_index * LAT_DEV
    coupling = band_coupling(
        entries,
        band_info,
        coeffs,
        band_index,
        band_start - OVERHANG,
        LAT_DEV + 2 * OVERHANG,
        band_start,
        LAT_DEV,
        LAT_DEV,
        grid_rows,
    ).astype(jnp.bfloat16)
    extended = apply_filter(
        coupling, lax.all_to_all(fields, "lon", split_axis=3, concat_axis=1, tiled=True)
    )
    bottom_part = extended[:OVERHANG]
    middle = extended[OVERHANG : OVERHANG + LAT_DEV]
    top_part = extended[OVERHANG + LAT_DEV :]
    from_below = shifted(top_part, "lat", 1)
    from_above = shifted(bottom_part, "lat", -1)
    padding_low = ((0, LAT_DEV - OVERHANG), (0, 0), (0, 0), (0, 0), (0, 0))
    padding_high = ((LAT_DEV - OVERHANG, 0), (0, 0), (0, 0), (0, 0), (0, 0))
    middle = middle + jnp.pad(from_below, padding_low) + jnp.pad(from_above, padding_high)
    gathered = lax.all_to_all(
        middle.astype(jnp.bfloat16), "lon", split_axis=2, concat_axis=4, tiled=True
    )
    return mix_local(gathered, conv_weight, mix_weight)


def solution(mesh):
    in_specs = (P("lat", "lon", None, None), P(), P(), P(), P(), P())
    out_specs = P("lat", "lon", None, None)
    return jax.shard_map(shards, mesh=mesh, in_specs=in_specs, out_specs=out_specs, check_vma=False)
```

profile of v0, /device:TPU:102, one launch (start us, length us, event | category | flops | bytes accessed | tf_op | source)
XLA Modules:
  0.0 330.1 jit_solution(4340543974053770961)
XLA Ops:
  0.0 5.7 %copy.34 = bf16[4,90,2,512]{1,2,0,3:T(2,128)(2,1)} copy(bf16[4,90,2,512]{3,2,1,0:T(2,128)(2,1)} %param.6) | data formatting | bytes 1474560 | tf_op args[0]
  5.7 4.5 %all-to-all-start = ((bf16[4,90,2,512]{1,2,0,3:T(2,128)(2,1)}), bf16[4,90,2,512]{1,2,0,3:T(2,128)(2,1)}, u32[]{:S(2)}, u32[]{:S(2)}) async-start(bf16[4,90,2,512]{1,2,0,3:T(2,128)(2,1)} %copy.34), calls=%async_computation | async-start | bytes 2097152 | tf_op jit(solution)/shard_map/all_to_all | solution.py:104
  14.9 11.3 %all-to-all-done = bf16[4,90,2,512]{1,2,0,3:T(2,128)(2,1)} async-done(((bf16[4,90,2,512]{1,2,0,3:T(2,128)(2,1)}), bf16[4,90,2,512]{1,2,0,3:T(2,128)(2,1)}, u32[]{:S(2)}, u32[]{:S(2)}) %all-to-all-start) | async-done | bytes 737312 | tf_op jit(solution)/shard_map/all_to_all | solution.py:104
  27.6 1.7 copy.37
  29.3 2.0 reshape.134
  35.2 3.2 copy.36
  38.4 3.2 concatenate.42
  51.0 2.8 copy_bitcast_fusion.4
  53.8 1.7 copy_bitcast_fusion.2
  55.6 1.7 copy_bitcast_fusion
  57.3 28.8 %concatenate.55 = bf16[28,92160]{1,0:T(8,128)(2,1)} concatenate(bf16[4,92160]{1,0:T(4,128)(2,1)S(1)} %copy-done.5, bf16[4,92160]{1,0:T(4,128)(2,1)} %get-tuple-element.22, bf16[4,92160]{1,0:T(4,128)(2,1)S(1)} %get-tuple-element.21, bf16[4,92160]{1,0:T(4,128)(2,1)} %get-tuple-element.20, bf16[4,92160]{1,0:T(4,128)(2,1)} %get-tuple-element.19, bf16[4,92160]{1,0:T(4,128)(2,1)} %get-tuple-element.18, ...), dimensions={0} | concatenate | bytes 10321920 | tf_op jit(solution)/shard_map/concatenate | solution.py:70
  86.1 8.7 %fusion.34 = f32[30,92160]{1,0:T(8,128)} fusion(bf16[30,28]{1,0:T(8,128)(2,1)S(1)} %convolution_convert_fusion.1, bf16[28,92160]{1,0:T(8,128)(2,1)} %concatenate.55), kind=kOutput, calls=%fused_computation.69 | convolution fusion | flops 154828800 | bytes 16221840 | tf_op jit(solution)/shard_map/dot_general | solution.py:74
  94.8 9.5 %fusion.32 = (f32[9,92160]{1,0:T(8,128)}, f32[9,92160]{1,0:T(8,128)}) fusion(f32[30,92160]{1,0:T(8,128)} %fusion.34), kind=kLoop, calls=%fused_computation.66 | loop fusion | bytes 13271040 | tf_op jit(solution)/shard_map/slice | solution.py:108
  104.3 12.1 %slice.116 = f32[3,3,720,2,64]{4,3,2,1,0:T(2,128)} reshape(f32[9,92160]{1,0:T(8,128)} %get-tuple-element.9) | data formatting | bytes 6635520 | tf_op jit(solution)/shard_map/slice | solution.py:108
  116.3 12.5 %copy.44 = f32[3,3,720,2,64]{2,4,3,1,0:T(8,128)} copy(f32[3,3,720,2,64]{4,3,2,1,0:T(2,128)} %slice.116) | data formatting | bytes 6635520 | tf_op jit(solution)/shard_map/slice | solution.py:108
  128.8 4.9 %collective-permute-start = (f32[3,3,720,2,64]{2,4,3,1,0:T(8,128)}, f32[3,3,720,2,64]{2,4,3,1,0:T(8,128)}, u32[]{:S(2)}, u32[]{:S(2)}) collective-permute-start(f32[3,3,720,2,64]{2,4,3,1,0:T(8,128)} %copy.44), channel_id=1, source_target_pairs={{0,8},{8,16},{16,24},{24,32},{32,40},{40,48},{48,56},{56,64},{64,7... | collective-permute-start | bytes 9953288 | tf_op jit(solution)/shard_map/ppermute | solution.py:16
  133.8 12.1 %slice.118 = f32[3,3,720,2,64]{4,3,2,1,0:T(2,128)} reshape(f32[9,92160]{1,0:T(8,128)} %get-tuple-element.10) | data formatting | bytes 6635520 | tf_op jit(solution)/shard_map/slice | solution.py:106
  145.8 12.5 %copy.46 = f32[3,3,720,2,64]{2,4,3,1,0:T(8,128)} copy(f32[3,3,720,2,64]{4,3,2,1,0:T(2,128)} %slice.118) | data formatting | bytes 6635520 | tf_op jit(solution)/shard_map/slice | solution.py:106
  158.4 1.9 collective-permute-start.1
  160.3 6.6 %slice.135 = f32[12,92160]{1,0:T(8,128)} slice(f32[30,92160]{1,0:T(8,128)} %fusion.34), slice={[9:21], [0:92160]} | slice | bytes 8847360 | tf_op jit(solution)/shard_map/slice | solution.py:107
  166.9 14.5 %slice.114 = f32[4,3,720,2,64]{4,3,2,1,0:T(2,128)} reshape(f32[12,92160]{1,0:T(8,128)} %slice.135) | data formatting | bytes 8847360 | tf_op jit(solution)/shard_map/slice | solution.py:107
  181.4 28.2 %collective-permute-done = f32[3,3,720,2,64]{2,4,3,1,0:T(8,128)} collective-permute-done((f32[3,3,720,2,64]{2,4,3,1,0:T(8,128)}, f32[3,3,720,2,64]{2,4,3,1,0:T(8,128)}, u32[]{:S(2)}, u32[]{:S(2)}) %collective-permute-start) | collective-permute-done | bytes 3317792 | tf_op jit(solution)/shard_map/ppermute | solution.py:16
  209.7 12.7 %copy.45 = f32[3,3,720,2,64]{4,3,2,1,0:T(2,128)} copy(f32[3,3,720,2,64]{2,4,3,1,0:T(8,128)} %collective-permute-done) | data formatting | bytes 6635520 | tf_op jit(solution)/shard_map/ppermute | solution.py:16
  222.4 19.3 %collective-permute-done.1 = f32[3,3,720,2,64]{2,4,3,1,0:T(8,128)} collective-permute-done((f32[3,3,720,2,64]{2,4,3,1,0:T(8,128)}, f32[3,3,720,2,64]{2,4,3,1,0:T(8,128)}, u32[]{:S(2)}, u32[]{:S(2)}) %collective-permute-start.1) | collective-permute-done | bytes 3317792 | tf_op jit(solution)/shard_map/ppermute | solution.py:16
  241.7 12.7 %copy.47 = f32[3,3,720,2,64]{4,3,2,1,0:T(2,128)} copy(f32[3,3,720,2,64]{2,4,3,1,0:T(8,128)} %collective-permute-done.1) | data formatting | bytes 6635520 | tf_op jit(solution)/shard_map/ppermute | solution.py:16
  254.4 10.8 %copy_bitcast_fusion.6 = bf16[720,4,3,2,64]{4,3,2,1,0:T(2,128)(2,1)} fusion(f32[3,3,720,2,64]{4,3,2,1,0:T(2,128)} %copy.47, f32[4,3,720,2,64]{4,3,2,1,0:T(2,128)} %slice.114, f32[3,3,720,2,64]{4,3,2,1,0:T(2,128)} %copy.45), kind=kLoop, calls=%fused_computation.68 | loop fusion | flops 3317760 | bytes 13271040
  265.2 7.6 %reshape.143 = bf16[8,2,69120]{2,1,0:T(2,128)(2,1)} reshape(bf16[720,4,3,2,64]{4,3,2,1,0:T(2,128)(2,1)} %copy_bitcast_fusion.6) | data formatting | bytes 4423680
  272.8 33.1 %all_to_all.33 = bf16[8,2,69120]{2,1,0:T(2,128)(2,1)} all-to-all(bf16[8,2,69120]{2,1,0:T(2,128)(2,1)} %reshape.143), channel_id=1, replica_groups=mesh['lat'=32,'lon'=8] {'lon'}, dimensions={0} | all-to-all | bytes 4423680 | tf_op jit(solution)/shard_map/all_to_all | solution.py:114
  305.9 7.4 %reshape.144 = bf16[720,4,3,2,64]{4,3,2,1,0:T(2,128)(2,1)} reshape(bf16[8,2,69120]{2,1,0:T(2,128)(2,1)} %all_to_all.33) | data formatting | bytes 4423680
  313.3 11.3 %copy.57 = bf16[4,3,8,90,2,64]{3,5,2,1,4,0:T(8,128)(2,1)} copy(bf16[4,3,8,90,2,64]{5,4,1,0,3,2:T(2,128)(2,1)} %bitcast.91) | data formatting | bytes 4423680 | tf_op jit(solution)/shard_map/all_to_all | solution.py:114
  324.6 3.9 %convolution_convert_fusion = bf16[4,90,2,512]{3,1,2,0:T(8,128)(2,1)S(1)} fusion(bf16[4,3,90,2,512]{2,4,1,3,0:T(8,128)(2,1)} %bitcast.94, bf16[3,512,512,1,1]{2,1,0,4,3:T(8,128)(2,1)S(1)} %bitcast.84, bf16[512,512]{1,0:T(8,128)(2,1)S(1)} %copy-done.12), kind=kOutput, calls=%fused_computation.12 | convolution fusion | flops 1513635840 | bytes 5046272 | tf_op jit(solution)/shard_map/lomc,cd->lomd/dot_general | solution.py:82
  328.5 1.6 copy.51
  (58 shorter events, 18.0 us)
Async XLA Ops:
  0.0 324.6 %copy-start = (bf16[1536,512]{1,0:T(8,128)(2,1)S(1)}, bf16[1536,512]{1,0:T(8,128)(2,1)}, u32[]{:S(2)}) copy-start(bf16[1536,512]{1,0:T(8,128)(2,1)} %param.10) | copy-start | bytes 4718596
  0.0 10.2 %copy-start.11 = (s32[32,3]{0,1:T(4,128)S(1)}, s32[32,3]{0,1:T(4,128)}, u32[]{:S(2)}) copy-start(s32[32,3]{0,1:T(4,128)} %param.9) | copy-start | bytes 1156
  0.0 13.4 %copy-start.13 = (f32[1024,3]{0,1:T(4,128)S(1)}, f32[1024,3]{0,1:T(4,128)}, u32[]{:S(2)}) copy-start(f32[1024,3]{0,1:T(4,128)} %param.7) | copy-start | bytes 36868
  5.7 20.5 %all-to-all-start = ((bf16[4,90,2,512]{1,2,0,3:T(2,128)(2,1)}), bf16[4,90,2,512]{1,2,0,3:T(2,128)(2,1)}, u32[]{:S(2)}, u32[]{:S(2)}) async-start(bf16[4,90,2,512]{1,2,0,3:T(2,128)(2,1)} %copy.34), calls=%async_computation | async-start | bytes 2097152 | tf_op jit(solution)/shard_map/all_to_all | solution.py:104
  38.4 3.2 copy-start.10
  38.4 4.8 %copy-start.9 = (bf16[4,2,128]{1,2,0:T(8,128)(2,1)S(1)}, bf16[4,2,128]{1,2,0:T(8,128)(2,1)}, u32[]{:S(2)}) copy-start(bf16[4,2,128]{1,2,0:T(8,128)(2,1)} %slice.125) | copy-start | bytes 6148
  42.1 2.8 copy-start.8
  43.6 2.7 copy-start.7
  45.2 2.7 copy-start.6
  49.8 4.0 %copy-start.1 = (bf16[4,720,128]{2,1,0:T(8,128)(2,1)S(1)}, bf16[4,720,128]{2,1,0:T(8,128)(2,1)}, u32[]{:S(2)}) copy-start(bf16[4,720,128]{2,1,0:T(8,128)(2,1)} %copy.40) | copy-start | bytes 2211844
  51.0 2.9 copy-start.2
  53.8 1.7 copy-start.3
  53.8 1.7 copy-start.4
  55.5 1.7 copy-start.5
  128.8 80.8 %collective-permute-start = (f32[3,3,720,2,64]{2,4,3,1,0:T(8,128)}, f32[3,3,720,2,64]{2,4,3,1,0:T(8,128)}, u32[]{:S(2)}, u32[]{:S(2)}) collective-permute-start(f32[3,3,720,2,64]{2,4,3,1,0:T(8,128)} %copy.44), channel_id=1, source_target_pairs={{0,8},{8,16},{16,24},{24,32},{32,40},{40,48},{48,56},{56,64},{64,7... | collective-permute-start | bytes 9953288 | tf_op jit(solution)/shard_map/ppermute | solution.py:16
  158.4 83.3 %collective-permute-start.1 = (f32[3,3,720,2,64]{2,4,3,1,0:T(8,128)}, f32[3,3,720,2,64]{2,4,3,1,0:T(8,128)}, u32[]{:S(2)}, u32[]{:S(2)}) collective-permute-start(f32[3,3,720,2,64]{2,4,3,1,0:T(8,128)} %copy.46), channel_id=1, source_target_pairs={{8,0},{16,8},{24,16},{32,24},{40,32},{48,40},{56,48},{64,56},{72,6... | collective-permute-start | bytes 9953288 | tf_op jit(solution)/shard_map/ppermute | solution.py:16
  313.3 11.3 %copy-start.12 = (bf16[512,512]{1,0:T(8,128)(2,1)S(1)}, bf16[512,512]{1,0:T(8,128)(2,1)}, u32[]{:S(2)}) copy-start(bf16[512,512]{1,0:T(8,128)(2,1)} %param.11) | copy-start | bytes 1572868
where the time goes:
time: 335 us; the launch traced here: 330 us
  local copies, waits for them, and re-layouts  197 us (59%)
  waiting for transfers between devices  58.9 us (18%)
  blocking collectives  33.1 us (10%)
  other arithmetic  14 us (4%)
  matrix products  14 us (4%)
  starting transfers between devices  11.3 us (3%)
    ppermute x2, waiting for transfers between devices, shifted(): lax.ppermute(value, axis, [(source, source + steps) for source in range(l...  47.6 us
    concatenate x5, local copies, waits for them, and re-layouts, apply_filter(): jnp.concatenate([jnp.roll(flattened, offset, axis=1) for offset in range(...  38.3 us
    slice x3, local copies, waits for them, and re-layouts, shards(): top_part = extended[OVERHANG + LAT_DEV:]  34.1 us
    all_to_all x1, blocking collectives, shards(): lax.all_to_all(middle.astype(jnp.bfloat16), 'lon', split_axis=2, concat_a...  33.1 us
    ppermute x2, local copies, waits for them, and re-layouts, shifted(): lax.ppermute(value, axis, [(source, source + steps) for source in range(l...  25.4 us
    slice x2, local copies, waits for them, and re-layouts, shards(): bottom_part = extended[:OVERHANG]  24.6 us
    slice x2, local copies, waits for them, and re-layouts, shards(): middle = extended[OVERHANG:OVERHANG + LAT_DEV]  21.1 us
    unnamed x31, local copies, waits for them, and re-layouts  20.7 us
  transfers between devices with their start and end apart: 3, of which 3 were waited for; matrix products, arithmetic and copies ran while one was open for 19% of the time, Pallas kernels for 0%

commit v1 on v0

v1 whole, which is shorter than its diff:
```python
import jax
import jax.numpy as jnp
from jax import lax
from jax.sharding import PartitionSpec as P

CHANNELS = 512
BASIS = 3
SHIFTS = 7
OVERHANG = 3
LAT_DEV = 4


def band_coupling(entries, band_meta, coeffs, band_index, grid_rows):
    nbands = entries.shape[0]
    blocks = entries.shape[1]
    ids = band_index + jnp.arange(-1, 2, dtype=jnp.int32)
    known = (ids >= 0) & (ids < nbands)
    clamped = jnp.clip(ids, 0, nbands - 1)
    listed = jnp.take(entries, clamped, axis=0)
    meta = jnp.take(band_meta, clamped, axis=0)
    out_rows = listed[:, :, 0, :]
    in_rows = listed[:, :, 1, :]
    shifts = listed[:, :, 2, :]
    filter_rows = listed[:, :, 3, :]
    block_ids = jnp.arange(blocks, dtype=jnp.int32)[None, :, None]
    own_rel = out_rows - clamped[:, None, None] * LAT_DEV
    usable = known[:, None, None] & (block_ids < meta[:, 0, None, None])
    usable = usable & (own_rel >= -meta[:, 1, None, None])
    usable = usable & (own_rel < LAT_DEV + meta[:, 2, None, None])
    usable = usable & (out_rows >= 0) & (out_rows < grid_rows)
    band_start = band_index * LAT_DEV
    q = (out_rows - band_start).reshape(-1)
    r = (in_rows - (band_start - OVERHANG)).reshape(-1)
    s = shifts.reshape(-1)
    values = jnp.take(coeffs, filter_rows.reshape(-1), axis=0)
    values = values * usable.reshape(-1)[:, None].astype(jnp.float32)
    out_hit = (q[:, None] == jnp.arange(LAT_DEV, dtype=jnp.int32)[None, :]).astype(jnp.float32)
    left_side = (out_hit[:, :, None] * values[:, None, :]).reshape(-1, LAT_DEV * BASIS)
    rows_in = LAT_DEV + 2 * OVERHANG
    in_hit = (
        (s * rows_in + r)[:, None] == jnp.arange(SHIFTS * rows_in, dtype=jnp.int32)[None, :]
    ).astype(jnp.float32)
    coupling = jnp.dot(
        left_side.T, in_hit, precision=lax.Precision.HIGHEST, preferred_element_type=jnp.float32
    )
    return coupling.reshape(LAT_DEV * BASIS, SHIFTS, rows_in)


def gather_rows(x):
    nlat = lax.axis_size("lat")
    nlon = lax.axis_size("lon")
    lo = SHIFTS - 1
    tail = x[:, x.shape[1] - lo :]

    def move(value, dlat, dlon):
        pairs = []
        for b in range(nlat):
            if 0 <= b + dlat < nlat:
                for j in range(nlon):
                    pairs.append((b * nlon + j, (b + dlat) * nlon + (j + dlon) % nlon))
        return lax.ppermute(value, ("lat", "lon"), pairs)

    below = move(x[LAT_DEV - OVERHANG :], 1, 0)
    above = move(x[:OVERHANG], -1, 0)
    left = move(tail, 0, 1)
    below_left = move(tail[LAT_DEV - OVERHANG :], 1, 1)
    above_left = move(tail[:OVERHANG], -1, 1)
    rows_below = jnp.concatenate([below_left, below], axis=1)
    rows_mid = jnp.concatenate([left, x], axis=1)
    rows_above = jnp.concatenate([above_left, above], axis=1)
    return jnp.concatenate([rows_below, rows_mid, rows_above], axis=0)


def shards(fields, coeffs, entries, band_info, conv_weight, mix_weight):
    band_index = lax.axis_index("lat")
    grid_rows = LAT_DEV * lax.axis_size("lat")
    nrows, nlon, members, channels = fields.shape
    coupling = band_coupling(entries, band_info, coeffs, band_index, grid_rows).astype(jnp.bfloat16)
    rows = gather_rows(fields)
    ext = rows.shape[1]
    lo = SHIFTS - 1
    pick = (
        jnp.arange(ext, dtype=jnp.int32)[None, None, :]
        == jnp.arange(nlon, dtype=jnp.int32)[None, :, None]
        + lo
        - jnp.arange(SHIFTS, dtype=jnp.int32)[:, None, None]
    ).astype(jnp.bfloat16)
    toeplitz = jnp.einsum(
        "asr,slt->alrt", coupling, pick, preferred_element_type=jnp.float32
    ).astype(jnp.bfloat16)
    rows_in = rows.shape[0]
    toeplitz = toeplitz.reshape(LAT_DEV * BASIS * nlon, rows_in * ext)
    conv = jnp.dot(
        toeplitz, rows.reshape(rows_in * ext, members * channels), preferred_element_type=jnp.float32
    )
    features = conv.astype(jnp.bfloat16).reshape(LAT_DEV, BASIS, nlon, members, channels)
    kernel = conv_weight.reshape(BASIS, CHANNELS, CHANNELS)
    combined = jnp.einsum("qklmc,kcd->qlmd", features, kernel, preferred_element_type=jnp.float32)
    activated = jax.nn.gelu(combined, approximate=True).astype(jnp.bfloat16)
    return jnp.einsum(
        "qlmc,cd->qlmd", activated, mix_weight, preferred_element_type=jnp.float32
    ).astype(jnp.bfloat16)


def solution(mesh):
    in_specs = (P("lat", "lon", None, None), P(), P(), P(), P(), P())
    out_specs = P("lat", "lon", None, None)
    return jax.shard_map(shards, mesh=mesh, in_specs=in_specs, out_specs=out_specs, check_vma=False)
```

time: 335 us -> 80.3 us (0.24)
  the two profiles are of different devices: /device:TPU:102 before, /device:TPU:129 now
where the time goes in v1:
time: 80.3 us; the launch traced here: 79.3 us
  local copies, waits for them, and re-layouts  39 us (49%)
  starting transfers between devices  20.9 us (26%)
  matrix products  11.7 us (15%)
  other arithmetic  7.47 us (9%)
    ppermute x5, starting transfers between devices, move(): return lax.ppermute(value, ('lat', 'lon'), pairs)  20.9 us
    convert_element_type x1, local copies, waits for them, and re-layouts, shards(): toeplitz = jnp.einsum('asr,slt->alrt', coupling, pick, preferred_element_...  8.4 us
    reshape x1, local copies, waits for them, and re-layouts, shards(): toeplitz = toeplitz.reshape(LAT_DEV * BASIS * nlon, rows_in * ext)  6.65 us
    reshape x1, local copies, waits for them, and re-layouts, shards(): conv.astype(jnp.bfloat16).reshape(LAT_DEV, BASIS, nlon, members, channels)  6.23 us
    gather x2, local copies, waits for them, and re-layouts, band_coupling(): values = jnp.take(coeffs, filter_rows.reshape(-1), axis=0)  5.38 us
    concatenate x1, other arithmetic, gather_rows(): return jnp.concatenate([rows_below, rows_mid, rows_above], axis=0)  4.33 us
    dot_general x1, matrix products, shards(): jnp.dot(toeplitz, rows.reshape(rows_in * ext, members * channels), prefer...  3.92 us
    dot_general x1, matrix products, shards(): jnp.einsum('qlmc,cd->qlmd', activated, mix_weight, preferred_element_type...  3.61 us
  transfers between devices with their start and end apart: 5, of which 0 were waited for; matrix products, arithmetic and copies ran while one was open for 43% of the time, Pallas kernels for 0%

profile of v1, /device:TPU:129, one launch (start us, length us, event | category | flops | bytes accessed | tf_op | source)
XLA Modules:
  0.0 79.3 jit_solution(2155777504211576497)
XLA Ops:
  0.0 2.9 %fusion.38 = (bf16[3,90,2,512]{3,2,1,0:T(2,128)(2,1)}, bf16[3,90,2,512]{3,2,1,0:T(2,128)(2,1)S(1)}) fusion(bf16[4,90,2,512]{3,2,1,0:T(2,128)(2,1)} %param.6), kind=kLoop, calls=%fused_computation.72 | loop fusion | bytes 2211840 | tf_op jit(solution)/shard_map/slice | solution.py:63
  2.9 3.1 %collective-permute-start.1 = (bf16[3,90,2,512]{3,2,1,0:T(2,128)(2,1)}, bf16[3,90,2,512]{3,2,1,0:T(2,128)(2,1)}, u32[]{:S(2)}, u32[]{:S(2)}) collective-permute-start(bf16[3,90,2,512]{3,2,1,0:T(2,128)(2,1)} %get-tuple-element.13), channel_id=1, source_target_pairs={{0,8},{1,9},{2,10},{3,11},{4,12},{5,13},{6,14},{7,15},{8,16},{9,17... | collective-permute-start | bytes 1658888 | tf_op jit(solution)/shard_map/ppermute | solution.py:61
  6.1 5.5 %collective-permute-start.4 = (bf16[3,90,2,512]{3,2,1,0:T(2,128)(2,1)S(1)}, bf16[3,90,2,512]{3,2,1,0:T(2,128)(2,1)}, u32[]{:S(2)}, u32[]{:S(2)}) collective-permute-start(bf16[3,90,2,512]{3,2,1,0:T(2,128)(2,1)S(1)} %get-tuple-element.14), channel_id=1, source_target_pairs={{8,0},{9,1},{10,2},{11,3},{12,4},{13,5},{14,6},{15,7},{16,8},{17,9... | collective-permute-start | bytes 1658888 | tf_op jit(solution)/shard_map/ppermute | solution.py:61
  11.6 0.7 fusion.37
  12.2 1.9 %collective-permute-start = (bf16[3,6,2,512]{3,2,1,0:T(2,128)(2,1)}, bf16[3,6,2,512]{3,2,1,0:T(2,128)(2,1)}, u32[]{:S(2)}, u32[]{:S(2)}) collective-permute-start(bf16[3,6,2,512]{3,2,1,0:T(2,128)(2,1)} %get-tuple-element.11), channel_id=1, source_target_pairs={{0,9},{1,10},{2,11},{3,12},{4,13},{5,14},{6,15},{7,8},{8,17},{9,18... | collective-permute-start | bytes 110600 | tf_op jit(solution)/shard_map/ppermute | solution.py:61
  14.2 8.0 %collective-permute-start.3 = (bf16[3,6,2,512]{3,2,1,0:T(2,128)(2,1)S(1)}, bf16[3,6,2,512]{3,2,1,0:T(2,128)(2,1)}, u32[]{:S(2)}, u32[]{:S(2)}) collective-permute-start(bf16[3,6,2,512]{3,2,1,0:T(2,128)(2,1)S(1)} %get-tuple-element.12), channel_id=1, source_target_pairs={{8,1},{9,2},{10,3},{11,4},{12,5},{13,6},{14,7},{15,0},{16,9},{17,1... | collective-permute-start | bytes 110600 | tf_op jit(solution)/shard_map/ppermute | solution.py:61
  22.2 2.4 %collective-permute-start.2 = (bf16[4,6,2,512]{3,2,1,0:T(2,128)(2,1)S(1)}, bf16[4,6,2,512]{3,2,1,0:T(2,128)(2,1)S(1)}, u32[]{:S(2)}, u32[]{:S(2)}) collective-permute-start(bf16[4,6,2,512]{3,2,1,0:T(2,128)(2,1)S(1)} %slice.50), channel_id=1, source_target_pairs={{0,1},{1,2},{2,3},{3,4},{4,5},{5,6},{6,7},{7,0},{8,9},{9,10},{10,1... | collective-permute-start | bytes 147464 | tf_op jit(solution)/shard_map/ppermute | solution.py:61
  24.6 0.6 multiply_add_fusion
  25.2 1.5 %gather_fusion = s32[3,4,4,128]{3,2,1,0:T(4,128)S(1)} fusion(s32[32,4,4,128]{3,2,1,0:T(4,128)} %param.8, s32[1024]{0:T(1024)S(1)} %pad_clamp_fusion.1), kind=kCustom, calls=%fused_computation | custom fusion | bytes 49164 | tf_op jit(solution)/shard_map/jit(_take)/gather | solution.py:19
  26.8 0.6 fusion.29
  27.5 0.1 copy.19
  27.6 0.6 gather_fusion.2
  28.2 0.2 negate_reduce_fusion
  28.6 0.6 and.82
  29.5 0.6 pad_clamp_fusion
  30.1 0.9 %copy.17 = f32[1024,3]{1,0:T(8,128)S(1)} copy(f32[1024,3]{0,1:T(4,128)} %param.7) | data formatting | bytes 24576 | tf_op args[1]
  31.0 4.0 %gather_fusion.1 = f32[1536,3]{1,0:T(8,128)} fusion(f32[1024,3]{1,0:T(8,128)S(1)} %copy.17, s32[2048]{0:T(1024)} %pad_clamp_fusion), kind=kCustom, calls=%fused_computation.1 | custom fusion | bytes 43008 | tf_op jit(solution)/shard_map/jit(_take)/gather | solution.py:35
  35.0 1.4 %copy.18 = f32[1536,3]{0,1:T(4,128)S(1)} copy(f32[1536,3]{1,0:T(8,128)} %gather_fusion.1) | data formatting | bytes 36864 | tf_op jit(solution)/shard_map/jit(_take)/gather | solution.py:35
  36.4 0.7 reshape_squeeze.6
  37.1 0.7 and_convert_fusion
  37.9 0.7 add.148
  38.6 1.1 %fusion.12 = bf16[12,7,10,1]{0,1,2,3:T(8,128)(2,1)S(1)} fusion(f32[1536,12,1]{0,1,2:T(8,128)S(1)} %reshape.343, s32[7,10]{0,1:T(8,128)} %multiply_add_fusion, s32[1536]{0:T(1024)S(1)} %add.148), kind=kOutput, calls=%fused_computation.19 | convolution fusion | flops 15591240 | bytes 81832 | tf_op jit(solution)/shard_map/dot_general | solution.py:43
  39.8 3.0 %convert_bitcast_fusion = bf16[12,90,10,96]{3,0,2,1:T(8,128)(2,1)} fusion(bf16[12,7,10,1]{0,1,2,3:T(8,128)(2,1)S(1)} %fusion.12, s32[7,90]{0,1:T(8,128)S(1)} %iota_subtract_fusion), kind=kOutput, calls=%fused_computation.4 | convolution fusion | flops 15612480 | bytes 2077800 | tf_op jit(solution)/shard_map/asr,slt->alrt/dot_general | solution.py:88
  42.8 8.4 %copy.20 = bf16[12,90,10,96]{1,0,3,2:T(8,128)(2,1)} copy(bf16[12,90,10,96]{3,0,2,1:T(8,128)(2,1)} %convert_bitcast_fusion) | data formatting | bytes 4147200 | tf_op jit(solution)/shard_map/convert_element_type | solution.py:90
  51.2 6.7 %reshape.315 = bf16[1080,960]{0,1:T(8,128)(2,1)} reshape(bf16[12,90,10,96]{1,0,3,2:T(8,128)(2,1)} %copy.20) | data formatting | bytes 4147200 | tf_op jit(solution)/shard_map/reshape | solution.py:92
  57.9 4.3 %maximum_maximum_fusion = bf16[10,96,2,512]{3,2,1,0:T(2,128)(2,1)S(1)} fusion(bf16[3,90,2,512]{3,2,1,0:T(2,128)(2,1)} %collective-permute-done.4, bf16[3,6,2,512]{3,2,1,0:T(2,128)(2,1)} %collective-permute-done.3, bf16[4,90,2,512]{3,2,1,0:T(2,128)(2,1)S(1)} %copy-done.1, bf16[4,6,2,512]{3,2,1,0:T(2,128)(2,1)S(1)} %collective-permute-done.2, ...), kind=kLoop, calls=%fused_computation.8 | loop fusion | flops 4915200 | bytes 3932160 | tf_op jit(solution)/shard_map/concatenate | solution.py:71
  62.3 0.5 copy.33
  62.8 1.1 %copy-done.2 = bf16[1080,960]{0,1:T(8,128)(2,1)S(1)} copy-done((bf16[1080,960]{0,1:T(8,128)(2,1)S(1)}, bf16[1080,960]{0,1:T(8,128)(2,1)}, u32[]{:S(2)}) %copy-start.2) | copy-done | bytes 2073624
  63.9 3.9 %convolution_convert_fusion = bf16[1080,1024]{1,0:T(8,128)(2,1)} fusion(bf16[1080,960]{0,1:T(8,128)(2,1)S(1)} %copy-done.2, bf16[960,1024]{1,0:T(8,128)(2,1)S(1)} %bitcast.53), kind=kOutput, calls=%fused_computation.3 | convolution fusion | flops 2124472320 | bytes 6251520 | tf_op jit(solution)/shard_map/dot_general | solution.py:93
  67.8 6.2 %reshape.317 = bf16[4,3,90,2,512]{4,3,2,1,0:T(2,128)(2,1)} reshape(bf16[1080,1024]{1,0:T(8,128)(2,1)} %convolution_convert_fusion) | data formatting | bytes 4423680 | tf_op jit(solution)/shard_map/reshape | solution.py:96
  74.0 3.6 %convolution_convert_fusion.1 = bf16[4,90,2,512]{3,1,2,0:T(8,128)(2,1)S(1)} fusion(bf16[3,512,512,1,1]{2,1,0,4,3:T(8,128)(2,1)S(1)} %bitcast.51, bf16[4,3,90,2,512]{4,3,2,1,0:T(2,128)(2,1)} %reshape.317, bf16[512,512]{1,0:T(8,128)(2,1)S(1)} %copy-done.4), kind=kOutput, calls=%fused_computation.17 | convolution fusion | flops 1513635840 | bytes 5046272 | tf_op jit(solution)/shard_map/qlmc,cd->qlmd/dot_general | solution.py:100
  77.7 1.6 %copy.22 = bf16[4,90,2,512]{3,2,1,0:T(2,128)(2,1)} copy(bf16[4,90,2,512]{3,1,2,0:T(8,128)(2,1)S(1)} %convolution_convert_fusion.1) | data formatting | bytes 1474560 | tf_op jit(solution)/shard_map/convert_element_type | solution.py:102
  (39 shorter events, 0.8 us)
Async XLA Ops:
  0.0 74.0 %copy-start = (bf16[1536,512]{1,0:T(8,128)(2,1)S(1)}, bf16[1536,512]{1,0:T(8,128)(2,1)}, u32[]{:S(2)}) copy-start(bf16[1536,512]{1,0:T(8,128)(2,1)} %param.10) | copy-start | bytes 4718596
  0.0 11.6 %copy-start.1 = (bf16[4,90,2,512]{3,2,1,0:T(2,128)(2,1)S(1)}, bf16[4,90,2,512]{3,2,1,0:T(2,128)(2,1)}, u32[]{:S(2)}) copy-start(bf16[4,90,2,512]{3,2,1,0:T(2,128)(2,1)} %param.6) | copy-start | bytes 2211844
  0.0 27.5 %copy-start.3 = (s32[32,3]{0,1:T(4,128)S(1)}, s32[32,3]{0,1:T(4,128)}, u32[]{:S(2)}) copy-start(s32[32,3]{0,1:T(4,128)} %param.9) | copy-start | bytes 1156
  2.9 55.0 %collective-permute-start.1 = (bf16[3,90,2,512]{3,2,1,0:T(2,128)(2,1)}, bf16[3,90,2,512]{3,2,1,0:T(2,128)(2,1)}, u32[]{:S(2)}, u32[]{:S(2)}) collective-permute-start(bf16[3,90,2,512]{3,2,1,0:T(2,128)(2,1)} %get-tuple-element.13), channel_id=1, source_target_pairs={{0,8},{1,9},{2,10},{3,11},{4,12},{5,13},{6,14},{7,15},{8,16},{9,17... | collective-permute-start | bytes 1658888 | tf_op jit(solution)/shard_map/ppermute | solution.py:61
  6.1 51.8 %collective-permute-start.4 = (bf16[3,90,2,512]{3,2,1,0:T(2,128)(2,1)S(1)}, bf16[3,90,2,512]{3,2,1,0:T(2,128)(2,1)}, u32[]{:S(2)}, u32[]{:S(2)}) collective-permute-start(bf16[3,90,2,512]{3,2,1,0:T(2,128)(2,1)S(1)} %get-tuple-element.14), channel_id=1, source_target_pairs={{8,0},{9,1},{10,2},{11,3},{12,4},{13,5},{14,6},{15,7},{16,8},{17,9... | collective-permute-start | bytes 1658888 | tf_op jit(solution)/shard_map/ppermute | solution.py:61
  12.2 45.7 %collective-permute-start = (bf16[3,6,2,512]{3,2,1,0:T(2,128)(2,1)}, bf16[3,6,2,512]{3,2,1,0:T(2,128)(2,1)}, u32[]{:S(2)}, u32[]{:S(2)}) collective-permute-start(bf16[3,6,2,512]{3,2,1,0:T(2,128)(2,1)} %get-tuple-element.11), channel_id=1, source_target_pairs={{0,9},{1,10},{2,11},{3,12},{4,13},{5,14},{6,15},{7,8},{8,17},{9,18... | collective-permute-start | bytes 110600 | tf_op jit(solution)/shard_map/ppermute | solution.py:61
  14.2 43.7 %collective-permute-start.3 = (bf16[3,6,2,512]{3,2,1,0:T(2,128)(2,1)S(1)}, bf16[3,6,2,512]{3,2,1,0:T(2,128)(2,1)}, u32[]{:S(2)}, u32[]{:S(2)}) collective-permute-start(bf16[3,6,2,512]{3,2,1,0:T(2,128)(2,1)S(1)} %get-tuple-element.12), channel_id=1, source_target_pairs={{8,1},{9,2},{10,3},{11,4},{12,5},{13,6},{14,7},{15,0},{16,9},{17,1... | collective-permute-start | bytes 110600 | tf_op jit(solution)/shard_map/ppermute | solution.py:61
  22.2 35.7 %collective-permute-start.2 = (bf16[4,6,2,512]{3,2,1,0:T(2,128)(2,1)S(1)}, bf16[4,6,2,512]{3,2,1,0:T(2,128)(2,1)S(1)}, u32[]{:S(2)}, u32[]{:S(2)}) collective-permute-start(bf16[4,6,2,512]{3,2,1,0:T(2,128)(2,1)S(1)} %slice.50), channel_id=1, source_target_pairs={{0,1},{1,2},{2,3},{3,4},{4,5},{5,6},{6,7},{7,0},{8,9},{9,10},{10,1... | collective-permute-start | bytes 147464 | tf_op jit(solution)/shard_map/ppermute | solution.py:61
  62.3 1.6 %copy-start.2 = (bf16[1080,960]{0,1:T(8,128)(2,1)S(1)}, bf16[1080,960]{0,1:T(8,128)(2,1)}, u32[]{:S(2)}) copy-start(bf16[1080,960]{0,1:T(8,128)(2,1)} %reshape.315) | copy-start | bytes 6220804
  67.8 6.2 %copy-start.4 = (bf16[512,512]{1,0:T(8,128)(2,1)S(1)}, bf16[512,512]{1,0:T(8,128)(2,1)}, u32[]{:S(2)}) copy-start(bf16[512,512]{1,0:T(8,128)(2,1)} %param.11) | copy-start | bytes 1572868

commit v2 on v1

v2 whole, which is shorter than its diff:
```python
import jax
import jax.numpy as jnp
from jax import lax
from jax.experimental import pallas as pl
from jax.experimental.pallas import tpu as pltpu
from jax.sharding import PartitionSpec as P

CHANNELS = 512
BASIS = 3
SHIFTS = 7
OVERHANG = 3
LAT_DEV = 4


def band_coupling(entries, band_meta, coeffs, band_index, grid_rows):
    nbands = entries.shape[0]
    blocks = entries.shape[1]
    ids = band_index + jnp.arange(-1, 2, dtype=jnp.int32)
    known = (ids >= 0) & (ids < nbands)
    clamped = jnp.clip(ids, 0, nbands - 1)
    listed = jnp.take(entries, clamped, axis=0)
    meta = jnp.take(band_meta, clamped, axis=0)
    out_rows = listed[:, :, 0, :]
    in_rows = listed[:, :, 1, :]
    shifts = listed[:, :, 2, :]
    filter_rows = listed[:, :, 3, :]
    block_ids = jnp.arange(blocks, dtype=jnp.int32)[None, :, None]
    own_rel = out_rows - clamped[:, None, None] * LAT_DEV
    usable = known[:, None, None] & (block_ids < meta[:, 0, None, None])
    usable = usable & (own_rel >= -meta[:, 1, None, None])
    usable = usable & (own_rel < LAT_DEV + meta[:, 2, None, None])
    usable = usable & (out_rows >= 0) & (out_rows < grid_rows)
    band_start = band_index * LAT_DEV
    rows_in = LAT_DEV + 2 * OVERHANG
    q = out_rows - band_start
    r = in_rows - (band_start - OVERHANG)
    usable = usable & (q >= 0) & (q < LAT_DEV) & (r >= 0) & (r < rows_in)
    slot = jnp.where(usable, (q * SHIFTS + shifts) * rows_in + r, -1).reshape(-1)
    nslots = LAT_DEV * SHIFTS * rows_in
    slot_hit = (slot[:, None] == jnp.arange(nslots, dtype=jnp.int32)[None, :]).astype(jnp.bfloat16)
    nfilters = coeffs.shape[0]
    filter_hit = (
        filter_rows.reshape(-1)[:, None] == jnp.arange(nfilters, dtype=jnp.int32)[None, :]
    ).astype(jnp.bfloat16)
    counts = lax.dot_general(
        filter_hit, slot_hit, (((0,), (0,)), ((), ())), preferred_element_type=jnp.float32
    )
    coupling = jnp.dot(
        coeffs.T, counts, precision=lax.Precision.HIGHEST, preferred_element_type=jnp.float32
    )
    return coupling.reshape(BASIS, LAT_DEV, SHIFTS, rows_in)


def gather_rows(x):
    nlat = lax.axis_size("lat")
    nlon = lax.axis_size("lon")
    lo = SHIFTS - 1
    tail = x[:, x.shape[1] - lo :]

    def move(value, dlat, dlon):
        pairs = []
        for b in range(nlat):
            if 0 <= b + dlat < nlat:
                for j in range(nlon):
                    pairs.append((b * nlon + j, (b + dlat) * nlon + (j + dlon) % nlon))
        return lax.ppermute(value, ("lat", "lon"), pairs)

    below = move(x[LAT_DEV - OVERHANG :], 1, 0)
    above = move(x[:OVERHANG], -1, 0)
    left = move(tail, 0, 1)
    below_left = move(tail[LAT_DEV - OVERHANG :], 1, 1)
    above_left = move(tail[:OVERHANG], -1, 1)
    rows_below = jnp.concatenate([below_left, below], axis=1)
    rows_mid = jnp.concatenate([left, x], axis=1)
    rows_above = jnp.concatenate([above_left, above], axis=1)
    return jnp.concatenate([rows_below, rows_mid, rows_above], axis=0)


WINDOW = 30
ROW_PAD = 16


def conv_mix_kernel(toeplitz_ref, rows_ref, weight_ref, mix_ref, out_ref):
    nwin = out_ref.shape[0] // (2 * WINDOW * LAT_DEV)
    span = WINDOW * LAT_DEV
    pieces = [[[] for _ in range(2)] for _ in range(BASIS)]
    for j in range(nwin):
        window = rows_ref[pl.ds(j * WINDOW * ROW_PAD, (WINDOW + SHIFTS - 1) * ROW_PAD), :]
        conv = jnp.dot(toeplitz_ref[...], window, preferred_element_type=jnp.float32)
        for k in range(BASIS):
            for m in range(2):
                pieces[k][m].append(conv[k * span : (k + 1) * span, m * CHANNELS : (m + 1) * CHANNELS])
    combined = None
    for k in range(BASIS):
        features = jnp.concatenate(pieces[k][0] + pieces[k][1], axis=0).astype(jnp.bfloat16)
        term = jnp.dot(
            features,
            weight_ref[k * CHANNELS : (k + 1) * CHANNELS, :],
            preferred_element_type=jnp.float32,
        )
        combined = term if combined is None else combined + term
    activated = jax.nn.gelu(combined, approximate=True).astype(jnp.bfloat16)
    out_ref[...] = jnp.dot(activated, mix_ref[...], preferred_element_type=jnp.float32).astype(
        out_ref.dtype
    )


def shards(fields, coeffs, entries, band_info, conv_weight, mix_weight):
    band_index = lax.axis_index("lat")
    grid_rows = LAT_DEV * lax.axis_size("lat")
    nrows, nlon, members, channels = fields.shape
    lo = SHIFTS - 1
    coupling = band_coupling(entries, band_info, coeffs, band_index, grid_rows).astype(jnp.bfloat16)
    rows = gather_rows(fields)
    rows_in, ext = rows.shape[0], rows.shape[1]
    rows = jnp.pad(rows, ((0, ROW_PAD - rows_in), (0, 0), (0, 0), (0, 0)))
    rows = jnp.transpose(rows, (1, 0, 2, 3)).reshape(ext * ROW_PAD, members * channels)
    pick = (
        jnp.arange(WINDOW + lo, dtype=jnp.int32)[None, None, :]
        == jnp.arange(WINDOW, dtype=jnp.int32)[None, :, None]
        + lo
        - jnp.arange(SHIFTS, dtype=jnp.int32)[:, None, None]
    ).astype(jnp.bfloat16)
    toeplitz = jnp.einsum("kqsr,slt->klqtr", coupling, pick, preferred_element_type=jnp.float32)
    toeplitz = jnp.pad(toeplitz, ((0, 0),) * 4 + ((0, ROW_PAD - rows_in),)).astype(jnp.bfloat16)
    toeplitz = toeplitz.reshape(BASIS * WINDOW * LAT_DEV, (WINDOW + lo) * ROW_PAD)
    out_rows = members * nlon * LAT_DEV
    mixed = pl.pallas_call(
        conv_mix_kernel,
        out_shape=jax.ShapeDtypeStruct((out_rows, CHANNELS), jnp.bfloat16),
        in_specs=[pl.BlockSpec(memory_space=pltpu.VMEM)] * 4,
        out_specs=pl.BlockSpec(memory_space=pltpu.VMEM),
        cost_estimate=pl.CostEstimate(
            flops=2 * toeplitz.shape[0] * toeplitz.shape[1] * 1024 * (nlon // WINDOW)
            + 2 * out_rows * CHANNELS * CHANNELS * (BASIS + 1),
            transcendentals=out_rows * CHANNELS,
            bytes_accessed=rows.size * 2 + toeplitz.size * 2 + (BASIS + 2) * CHANNELS * CHANNELS * 2,
        ),
    )(toeplitz, rows, conv_weight, mix_weight)
    return jnp.transpose(mixed.reshape(members, nlon, LAT_DEV, CHANNELS), (2, 1, 0, 3))


def solution(mesh):
    in_specs = (P("lat", "lon", None, None), P(), P(), P(), P(), P())
    out_specs = P("lat", "lon", None, None)
    return jax.shard_map(shards, mesh=mesh, in_specs=in_specs, out_specs=out_specs, check_vma=False)
```

time: 80.3 us -> 69.1 us (0.86)
  local copies, waits for them, and re-layouts: 39 us -> 30.7 us
  matrix products: 11.7 us -> 3.87 us
  Pallas kernels: 0 us -> 7.11 us
  other arithmetic: 7.47 us -> 5.74 us
    convert_element_type x2 -> x1, local copies, waits for them, and re-layouts: 10 us -> 0.14 us  [shards(): band_coupling(entries, band_info, coeffs, band_index, grid_rows)]
    dot_general x4 -> x3, matrix products: 11.7 us -> 3.87 us  [the longest x1 2.35 us: band_coupling(): lax.dot_general(filter_hit, slot_hit, (((0,), (0,)), ((), ())), preferred...]
    pallas_call x0 -> x1, Pallas kernels: none -> 7.11 us  [shards(): pl.pallas_call(conv_mix_kernel, out_shape=jax.ShapeDtypeStruct((out_rows,...]
    gather x2 -> x0, local copies, waits for them, and re-layouts: 5.38 us -> none  [band_coupling(): values = jnp.take(coeffs, filter_rows.reshape(-1), axis=0)]
    transpose x0 -> x1, other arithmetic: none -> 5.09 us  [shards(): jnp.transpose(rows, (1, 0, 2, 3)).reshape(ext * ROW_PAD, members * channels)]
    unnamed x13 -> x9, local copies, waits for them, and re-layouts: 2.64 us -> 7.63 us
    reshape x2 -> x3, local copies, waits for them, and re-layouts: 12.9 us -> 8.09 us  [the longest x1 5.02 us: shards(): toeplitz.reshape(BASIS * WINDOW * LAT_DEV, (WINDOW + lo) * ROW_PAD)]
    pad x0 -> x1, local copies, waits for them, and re-layouts: none -> 4.62 us  [shards(): jnp.pad(toeplitz, ((0, 0),) * 4 + ((0, ROW_PAD - rows_in),))]
  transfers between devices with their start and end apart: 5 -> 5, of which waited for: 0 -> 0; matrix products, arithmetic and copies ran while one was open for 43% -> 34% of each run, Pallas kernels for 0% -> 0%
where the time goes in v2:
time: 69.1 us; the launch traced here: 68.5 us
  local copies, waits for them, and re-layouts  30.7 us (44%)
  starting transfers between devices  20.9 us (30%)
  Pallas kernels  7.11 us (10%)
  other arithmetic  5.74 us (8%)
  matrix products  3.87 us (6%)
    ppermute x5, starting transfers between devices, move(): return lax.ppermute(value, ('lat', 'lon'), pairs)  20.9 us
    unnamed x9, local copies, waits for them, and re-layouts  7.63 us
    pallas_call x1, Pallas kernels, shards(): pl.pallas_call(conv_mix_kernel, out_shape=jax.ShapeDtypeStruct((out_rows,...  7.11 us
    transpose x1, other arithmetic, shards(): jnp.transpose(rows, (1, 0, 2, 3)).reshape(ext * ROW_PAD, members * channels)  5.09 us
    reshape x1, local copies, waits for them, and re-layouts, shards(): toeplitz.reshape(BASIS * WINDOW * LAT_DEV, (WINDOW + lo) * ROW_PAD)  5.02 us
    pad x1, local copies, waits for them, and re-layouts, shards(): jnp.pad(toeplitz, ((0, 0),) * 4 + ((0, ROW_PAD - rows_in),))  4.62 us
    transpose x1, local copies, waits for them, and re-layouts, shards(): jnp.transpose(rows, (1, 0, 2, 3)).reshape(ext * ROW_PAD, members * channels)  3.49 us
    reshape x2, local copies, waits for them, and re-layouts, shards(): mixed.reshape(members, nlon, LAT_DEV, CHANNELS)  3.07 us
  transfers between devices with their start and end apart: 5, of which 0 were waited for; matrix products, arithmetic and copies ran while one was open for 34% of the time, Pallas kernels for 0%

profile of v2, /device:TPU:129, one launch (start us, length us, event | category | flops | bytes accessed | tf_op | source)
XLA Modules:
  0.0 68.5 jit_solution(16526244467361591856)
XLA Ops:
  0.0 2.8 %fusion.25 = (bf16[3,90,2,512]{3,2,1,0:T(2,128)(2,1)}, bf16[3,90,2,512]{3,2,1,0:T(2,128)(2,1)S(1)}) fusion(bf16[4,90,2,512]{3,2,1,0:T(2,128)(2,1)} %param.6), kind=kLoop, calls=%fused_computation.53 | loop fusion | bytes 2211840 | tf_op jit(solution)/shard_map/slice | solution.py:68
  2.8 3.1 %collective-permute-start.1 = (bf16[3,90,2,512]{3,2,1,0:T(2,128)(2,1)}, bf16[3,90,2,512]{3,2,1,0:T(2,128)(2,1)S(1)}, u32[]{:S(2)}, u32[]{:S(2)}) collective-permute-start(bf16[3,90,2,512]{3,2,1,0:T(2,128)(2,1)} %get-tuple-element.14), channel_id=1, source_target_pairs={{0,8},{1,9},{2,10},{3,11},{4,12},{5,13},{6,14},{7,15},{8,16},{9,17... | collective-permute-start | bytes 1658888 | tf_op jit(solution)/shard_map/ppermute | solution.py:66
  5.9 5.5 %collective-permute-start.4 = (bf16[3,90,2,512]{3,2,1,0:T(2,128)(2,1)S(1)}, bf16[3,90,2,512]{3,2,1,0:T(2,128)(2,1)S(1)}, u32[]{:S(2)}, u32[]{:S(2)}) collective-permute-start(bf16[3,90,2,512]{3,2,1,0:T(2,128)(2,1)S(1)} %get-tuple-element.15), channel_id=1, source_target_pairs={{8,0},{9,1},{10,2},{11,3},{12,4},{13,5},{14,6},{15,7},{16,8},{17,9... | collective-permute-start | bytes 1658888 | tf_op jit(solution)/shard_map/ppermute | solution.py:66
  11.4 1.5 %fusion.24 = (bf16[3,6,2,512]{3,2,1,0:T(2,128)(2,1)}, bf16[3,6,2,512]{3,2,1,0:T(2,128)(2,1)}) fusion(bf16[4,90,2,512]{3,2,1,0:T(2,128)(2,1)} %param.6), kind=kLoop, calls=%fused_computation.52 | loop fusion | bytes 147456 | tf_op jit(solution)/shard_map/slice | solution.py:71
  13.0 1.9 %collective-permute-start = (bf16[3,6,2,512]{3,2,1,0:T(2,128)(2,1)}, bf16[3,6,2,512]{3,2,1,0:T(2,128)(2,1)S(1)}, u32[]{:S(2)}, u32[]{:S(2)}) collective-permute-start(bf16[3,6,2,512]{3,2,1,0:T(2,128)(2,1)} %get-tuple-element.12), channel_id=1, source_target_pairs={{0,9},{1,10},{2,11},{3,12},{4,13},{5,14},{6,15},{7,8},{8,17},{9,18... | collective-permute-start | bytes 110600 | tf_op jit(solution)/shard_map/ppermute | solution.py:66
  14.9 8.0 %collective-permute-start.3 = (bf16[3,6,2,512]{3,2,1,0:T(2,128)(2,1)}, bf16[3,6,2,512]{3,2,1,0:T(2,128)(2,1)}, u32[]{:S(2)}, u32[]{:S(2)}) collective-permute-start(bf16[3,6,2,512]{3,2,1,0:T(2,128)(2,1)} %get-tuple-element.13), channel_id=1, source_target_pairs={{8,1},{9,2},{10,3},{11,4},{12,5},{13,6},{14,7},{15,0},{16,9},{17,1... | collective-permute-start | bytes 110600 | tf_op jit(solution)/shard_map/ppermute | solution.py:66
  22.9 0.8 %slice.50 = bf16[4,6,2,512]{3,2,1,0:T(2,128)(2,1)S(1)} slice(bf16[4,90,2,512]{3,2,1,0:T(2,128)(2,1)} %param.6), slice={[0:4], [84:90], [0:2], [0:512]} | slice | bytes 98304 | tf_op jit(solution)/shard_map/slice | solution.py:58
  23.7 2.4 %collective-permute-start.2 = (bf16[4,6,2,512]{3,2,1,0:T(2,128)(2,1)S(1)}, bf16[4,6,2,512]{3,2,1,0:T(2,128)(2,1)S(1)}, u32[]{:S(2)}, u32[]{:S(2)}) collective-permute-start(bf16[4,6,2,512]{3,2,1,0:T(2,128)(2,1)S(1)} %slice.50), channel_id=1, source_target_pairs={{0,1},{1,2},{2,3},{3,4},{4,5},{5,6},{6,7},{7,0},{8,9},{9,10},{10,1... | collective-permute-start | bytes 147464 | tf_op jit(solution)/shard_map/ppermute | solution.py:66
  26.2 0.6 gather_fusion
  26.8 0.1 broadcast_select_fusion
  26.9 0.1 slice_reduce_fusion.1
  27.0 0.8 %copy.11 = s32[32,3]{1,0:T(8,128)S(1)} copy(s32[32,3]{0,1:T(4,128)} %param.9) | data formatting | bytes 768 | tf_op args[3]
  27.7 0.6 gather_fusion.1
  28.3 0.1 broadcast_select_fusion.1
  28.4 0.2 negate_reduce_fusion
  28.6 0.1 fusion.21
  28.7 0.1 and.97
  28.8 0.1 ge.53
  29.1 2.4 %fusion.6 = f32[1024,280]{1,0:T(8,128)S(1)} fusion(s32[1536]{0:T(1024)S(1)} %eq.44, s32[1536]{0:T(1024)S(1)} %add_select_fusion), kind=kOutput, calls=%fused_computation.10 | convolution fusion | flops 882806784 | bytes 1159168 | tf_op jit(solution)/shard_map/dot_general | solution.py:45
  31.4 0.9 %fusion.16 = bf16[3,280]{1,0:T(4,128)(2,1)S(1)} fusion(f32[1024,280]{1,0:T(8,128)S(1)} %fusion.6, f32[1024,3]{0,1:T(4,128)S(1)} %copy-done.2), kind=kOutput, calls=%fused_computation.23 | convolution fusion | flops 10322760 | bytes 1160848 | tf_op jit(solution)/shard_map/dot_general | solution.py:48
  32.3 0.1 reshape.233
  32.5 0.1 iota_subtract_fusion
  32.6 0.6 fusion.14
  33.2 4.3 %copy.16 = bf16[3,30,4,36,10]{4,3,2,1,0:T(8,128)(2,1)} copy(bf16[3,30,4,36,10]{3,4,2,0,1:T(8,128)(2,1)S(1)} %fusion.14) | data formatting | bytes 518400
  37.5 4.6 %pad.9.clone = bf16[3,30,4,36,16]{4,3,2,1,0:T(8,128)(2,1)} pad(bf16[3,30,4,36,10]{4,3,2,1,0:T(8,128)(2,1)} %copy.16, bf16[]{:T(256)} %constant.60.clone.1), padding=0_0x0_0x0_0x0_0x0_6 | pad | bytes 673922 | tf_op jit(solution)/shard_map/jit(_pad)/pad | solution.py:125
  42.1 5.0 %reshape.213.toeplitz_ref = bf16[360,576]{1,0:T(8,128)(2,1)} reshape(bf16[3,30,4,36,16]{4,3,2,1,0:T(8,128)(2,1)} %pad.9.clone) | data formatting | bytes 829440 | tf_op jit(solution)/shard_map/reshape | solution.py:126
  47.2 5.1 %fusion.12 = bf16[96,16,2,512]{3,2,0,1:T(2,128)(2,1)S(1)} fusion(bf16[3,90,2,512]{3,2,1,0:T(2,128)(2,1)S(1)} %collective-permute-done.4, bf16[3,6,2,512]{3,2,1,0:T(2,128)(2,1)} %collective-permute-done.3, bf16[4,90,2,512]{3,2,1,0:T(2,128)(2,1)S(1)} %copy-done.1, bf16[4,6,2,512]{3,2,1,0:T(2,128)(2,1)S(1)} %collective-permute-done.2, ...), kind=kLoop, calls=%fused_computation.16 | loop fusion | flops 29884416 | bytes 5111808 | tf_op jit(solution)/shard_map/transpose | solution.py:117
  52.3 3.5 %copy.13 = bf16[96,16,2,512]{3,2,1,0:T(2,128)(2,1)S(1)} copy(bf16[96,16,2,512]{3,2,0,1:T(2,128)(2,1)S(1)} %fusion.12) | data formatting | bytes 6291456 | tf_op jit(solution)/shard_map/transpose | solution.py:117
  55.8 2.5 %copy.24 = bf16[192,8,2,512]{3,1,2,0:T(8,128)(2,1)} copy(bf16[192,8,2,512]{3,2,1,0:T(2,128)(2,1)S(1)} %bitcast.36) | data formatting | bytes 6291456
  58.3 7.1 %shard_map.64 = bf16[720,512]{1,0:T(8,128)(2,1)} custom-call(bf16[360,576]{1,0:T(8,128)(2,1)} %reshape.213.toeplitz_ref, bf16[1536,1024]{1,0:T(8,128)(2,1)} %bitcast.37, bf16[1536,512]{1,0:T(8,128)(2,1)} %weight_ref.1, bf16[512,512]{1,0:T(8,128)(2,1)} %mix_ref.1), custom_call_target="tpu_custom_call" | custom-call | flops 2783969280 | bytes 6181888 | tf_op jit(solution)/shard_map/pallas_call | solution.py:128
  65.4 1.6 %reshape.215 = bf16[2,90,4,512]{3,2,1,0:T(4,128)(2,1)S(1)} reshape(bf16[720,512]{1,0:T(8,128)(2,1)} %shard_map.64) | data formatting | bytes 1474560 | tf_op jit(solution)/shard_map/reshape | solution.py:140
  67.1 1.4 %copy.33 = bf16[2,90,4,512]{3,0,1,2:T(2,128)(2,1)} copy(bf16[2,90,4,512]{3,2,1,0:T(4,128)(2,1)S(1)} %reshape.215) | data formatting | bytes 1474560 | tf_op jit(solution)/shard_map/reshape | solution.py:140
  (27 shorter events, 0.3 us)
Async XLA Ops:
  0.0 26.2 %copy-start = (s32[32,4,4,128]{3,2,1,0:T(4,128)S(1)}, s32[32,4,4,128]{3,2,1,0:T(4,128)}, u32[]{:S(2)}) copy-start(s32[32,4,4,128]{3,2,1,0:T(4,128)} %param.8) | copy-start | bytes 786436
  2.8 44.3 %collective-permute-start.1 = (bf16[3,90,2,512]{3,2,1,0:T(2,128)(2,1)}, bf16[3,90,2,512]{3,2,1,0:T(2,128)(2,1)S(1)}, u32[]{:S(2)}, u32[]{:S(2)}) collective-permute-start(bf16[3,90,2,512]{3,2,1,0:T(2,128)(2,1)} %get-tuple-element.14), channel_id=1, source_target_pairs={{0,8},{1,9},{2,10},{3,11},{4,12},{5,13},{6,14},{7,15},{8,16},{9,17... | collective-permute-start | bytes 1658888 | tf_op jit(solution)/shard_map/ppermute | solution.py:66
  5.9 41.2 %collective-permute-start.4 = (bf16[3,90,2,512]{3,2,1,0:T(2,128)(2,1)S(1)}, bf16[3,90,2,512]{3,2,1,0:T(2,128)(2,1)S(1)}, u32[]{:S(2)}, u32[]{:S(2)}) collective-permute-start(bf16[3,90,2,512]{3,2,1,0:T(2,128)(2,1)S(1)} %get-tuple-element.15), channel_id=1, source_target_pairs={{8,0},{9,1},{10,2},{11,3},{12,4},{13,5},{14,6},{15,7},{16,8},{17,9... | collective-permute-start | bytes 1658888 | tf_op jit(solution)/shard_map/ppermute | solution.py:66
  13.0 34.2 %collective-permute-start = (bf16[3,6,2,512]{3,2,1,0:T(2,128)(2,1)}, bf16[3,6,2,512]{3,2,1,0:T(2,128)(2,1)S(1)}, u32[]{:S(2)}, u32[]{:S(2)}) collective-permute-start(bf16[3,6,2,512]{3,2,1,0:T(2,128)(2,1)} %get-tuple-element.12), channel_id=1, source_target_pairs={{0,9},{1,10},{2,11},{3,12},{4,13},{5,14},{6,15},{7,8},{8,17},{9,18... | collective-permute-start | bytes 110600 | tf_op jit(solution)/shard_map/ppermute | solution.py:66
  14.9 32.3 %collective-permute-start.3 = (bf16[3,6,2,512]{3,2,1,0:T(2,128)(2,1)}, bf16[3,6,2,512]{3,2,1,0:T(2,128)(2,1)}, u32[]{:S(2)}, u32[]{:S(2)}) collective-permute-start(bf16[3,6,2,512]{3,2,1,0:T(2,128)(2,1)} %get-tuple-element.13), channel_id=1, source_target_pairs={{8,1},{9,2},{10,3},{11,4},{12,5},{13,6},{14,7},{15,0},{16,9},{17,1... | collective-permute-start | bytes 110600 | tf_op jit(solution)/shard_map/ppermute | solution.py:66
  23.7 23.5 %collective-permute-start.2 = (bf16[4,6,2,512]{3,2,1,0:T(2,128)(2,1)S(1)}, bf16[4,6,2,512]{3,2,1,0:T(2,128)(2,1)S(1)}, u32[]{:S(2)}, u32[]{:S(2)}) collective-permute-start(bf16[4,6,2,512]{3,2,1,0:T(2,128)(2,1)S(1)} %slice.50), channel_id=1, source_target_pairs={{0,1},{1,2},{2,3},{3,4},{4,5},{5,6},{6,7},{7,0},{8,9},{9,10},{10,1... | collective-permute-start | bytes 147464 | tf_op jit(solution)/shard_map/ppermute | solution.py:66
  29.0 2.4 %copy-start.2 = (f32[1024,3]{0,1:T(4,128)S(1)}, f32[1024,3]{0,1:T(4,128)}, u32[]{:S(2)}) copy-start(f32[1024,3]{0,1:T(4,128)} %param.7) | copy-start | bytes 36868
  42.1 5.1 %copy-start.1 = (bf16[4,90,2,512]{3,2,1,0:T(2,128)(2,1)S(1)}, bf16[4,90,2,512]{3,2,1,0:T(2,128)(2,1)}, u32[]{:S(2)}) copy-start(bf16[4,90,2,512]{3,2,1,0:T(2,128)(2,1)} %param.6) | copy-start | bytes 2211844

commit v3 on v2

--- a/solution.py
+++ b/solution.py
@@ -10,6 +10,7 @@
 SHIFTS = 7
 OVERHANG = 3
 LAT_DEV = 4
+ROW_PAD = 16
 
 
 def band_coupling(entries, band_meta, coeffs, band_index, grid_rows):
@@ -35,8 +36,8 @@
     q = out_rows - band_start
     r = in_rows - (band_start - OVERHANG)
     usable = usable & (q >= 0) & (q < LAT_DEV) & (r >= 0) & (r < rows_in)
-    slot = jnp.where(usable, (q * SHIFTS + shifts) * rows_in + r, -1).reshape(-1)
-    nslots = LAT_DEV * SHIFTS * rows_in
+    slot = jnp.where(usable, q * 128 + (SHIFTS - 1 - shifts) * ROW_PAD + r, -1).reshape(-1)
+    nslots = LAT_DEV * 128
     slot_hit = (slot[:, None] == jnp.arange(nslots, dtype=jnp.int32)[None, :]).astype(jnp.bfloat16)
     nfilters = coeffs.shape[0]
     filter_hit = (
@@ -48,7 +49,7 @@
     coupling = jnp.dot(
         coeffs.T, counts, precision=lax.Precision.HIGHEST, preferred_element_type=jnp.float32
     )
-    return coupling.reshape(BASIS, LAT_DEV, SHIFTS, rows_in)
+    return coupling
 
 
 def gather_rows(x):
@@ -77,15 +78,25 @@
 
 
 WINDOW = 30
-ROW_PAD = 16
+LON_PAD = 32
+TAPS = 128
 
 
-def conv_mix_kernel(toeplitz_ref, rows_ref, weight_ref, mix_ref, out_ref):
-    nwin = out_ref.shape[0] // (2 * WINDOW * LAT_DEV)
-    span = WINDOW * LAT_DEV
+def conv_mix_kernel(coupling_ref, rows_ref, weight_ref, mix_ref, out_ref, toeplitz_ref):
+    lo = SHIFTS - 1
+    cols = (WINDOW + lo + 4) * ROW_PAD
+    for k in range(BASIS):
+        for q in range(LAT_DEV):
+            taps = coupling_ref[k : k + 1, q * TAPS : (q + 1) * TAPS]
+            wide = jnp.concatenate([taps, jnp.zeros((1, cols - TAPS), jnp.float32)], axis=1)
+            block = jnp.broadcast_to(wide, (LON_PAD, cols))
+            block = pltpu.roll(block, 0, 1, stride=ROW_PAD, stride_axis=0)
+            toeplitz_ref[pl.ds((k * LAT_DEV + q) * LON_PAD, LON_PAD), :] = block.astype(jnp.bfloat16)
+    nwin = out_ref.shape[0] // (2 * LAT_DEV * LON_PAD)
+    span = LAT_DEV * LON_PAD
     pieces = [[[] for _ in range(2)] for _ in range(BASIS)]
     for j in range(nwin):
-        window = rows_ref[pl.ds(j * WINDOW * ROW_PAD, (WINDOW + SHIFTS - 1) * ROW_PAD), :]
+        window = rows_ref[pl.ds(j * WINDOW, cols // ROW_PAD), :, :].reshape(cols, 2 * CHANNELS)
         conv = jnp.dot(toeplitz_ref[...], window, preferred_element_type=jnp.float32)
         for k in range(BASIS):
             for m in range(2):
@@ -110,34 +121,31 @@
     grid_rows = LAT_DEV * lax.axis_size("lat")
     nrows, nlon, members, channels = fields.shape
     lo = SHIFTS - 1
-    coupling = band_coupling(entries, band_info, coeffs, band_index, grid_rows).astype(jnp.bfloat16)
+    coupling = band_coupling(entries, band_info, coeffs, band_index, grid_rows)
+    coupling = coupling.astype(jnp.bfloat16).astype(jnp.float32)
     rows = gather_rows(fields)
     rows_in, ext = rows.shape[0], rows.shape[1]
-    rows = jnp.pad(rows, ((0, ROW_PAD - rows_in), (0, 0), (0, 0), (0, 0)))
-    rows = jnp.transpose(rows, (1, 0, 2, 3)).reshape(ext * ROW_PAD, members * channels)
-    pick = (
-        jnp.arange(WINDOW + lo, dtype=jnp.int32)[None, None, :]
-        == jnp.arange(WINDOW, dtype=jnp.int32)[None, :, None]
-        + lo
-        - jnp.arange(SHIFTS, dtype=jnp.int32)[:, None, None]
-    ).astype(jnp.bfloat16)
-    toeplitz = jnp.einsum("kqsr,slt->klqtr", coupling, pick, preferred_element_type=jnp.float32)
-    toeplitz = jnp.pad(toeplitz, ((0, 0),) * 4 + ((0, ROW_PAD - rows_in),)).astype(jnp.bfloat16)
-    toeplitz = toeplitz.reshape(BASIS * WINDOW * LAT_DEV, (WINDOW + lo) * ROW_PAD)
-    out_rows = members * nlon * LAT_DEV
+    nwin = nlon // WINDOW
+    cols = (WINDOW + lo + 4) * ROW_PAD
+    lon_rows = (nwin - 1) * WINDOW + cols // ROW_PAD
+    rows = jnp.pad(rows, ((0, ROW_PAD - rows_in), (0, lon_rows - ext), (0, 0), (0, 0)))
+    rows = jnp.transpose(rows, (1, 0, 2, 3)).reshape(lon_rows, ROW_PAD, members * channels)
+    out_rows = members * nwin * LAT_DEV * LON_PAD
     mixed = pl.pallas_call(
         conv_mix_kernel,
         out_shape=jax.ShapeDtypeStruct((out_rows, CHANNELS), jnp.bfloat16),
         in_specs=[pl.BlockSpec(memory_space=pltpu.VMEM)] * 4,
         out_specs=pl.BlockSpec(memory_space=pltpu.VMEM),
+        scratch_shapes=[pltpu.VMEM((BASIS * LAT_DEV * LON_PAD, cols), jnp.bfloat16)],
         cost_estimate=pl.CostEstimate(
-            flops=2 * toeplitz.shape[0] * toeplitz.shape[1] * 1024 * (nlon // WINDOW)
+            flops=2 * BASIS * LAT_DEV * LON_PAD * cols * 1024 * nwin
             + 2 * out_rows * CHANNELS * CHANNELS * (BASIS + 1),
             transcendentals=out_rows * CHANNELS,
-            bytes_accessed=rows.size * 2 + toeplitz.size * 2 + (BASIS + 2) * CHANNELS * CHANNELS * 2,
+            bytes_accessed=rows.size * 2 + (BASIS + 2) * CHANNELS * CHANNELS * 2,
         ),
-    )(toeplitz, rows, conv_weight, mix_weight)
-    return jnp.transpose(mixed.reshape(members, nlon, LAT_DEV, CHANNELS), (2, 1, 0, 3))
+    )(coupling, rows, conv_weight, mix_weight)
+    mixed = mixed.reshape(members, nwin, LAT_DEV, LON_PAD, CHANNELS)[:, :, :, :WINDOW]
+    return jnp.transpose(mixed, (2, 1, 3, 0, 4)).reshape(LAT_DEV, nlon, members, CHANNELS)
 
 
 def solution(mesh):

time: 69.1 us -> 60.9 us (0.88)
  local copies, waits for them, and re-layouts: 30.7 us -> 19.1 us
  other arithmetic: 5.74 us -> 8.73 us
    unnamed x9 -> x11, local copies, waits for them, and re-layouts: 7.63 us -> 2.16 us
    pad x1 -> x0, local copies, waits for them, and re-layouts: 4.62 us -> none  [shards(): jnp.pad(toeplitz, ((0, 0),) * 4 + ((0, ROW_PAD - rows_in),))]
    transpose x1, other arithmetic: 5.09 us -> 8.15 us  [shards(): jnp.transpose(rows, (1, 0, 2, 3))]
    dot_general x1, matrix products: 0.9 us -> 1.8 us  [band_coupling(): jnp.dot(coeffs.T, counts, precision=lax.Precision.HIGHEST, preferred_elem...]
    slice x1, local copies, waits for them, and re-layouts: 2.82 us -> 2.02 us  [gather_rows(): below = move(x[LAT_DEV - OVERHANG:], 1, 0)]
    reshape x3 -> x2, local copies, waits for them, and re-layouts: 8.09 us -> 8.82 us  [shards(): jnp.transpose(rows, (1, 0, 2, 3))]
    transpose x1 -> x2, local copies, waits for them, and re-layouts: 3.49 us -> 2.81 us  [shards(): jnp.transpose(mixed, (2, 1, 3, 0, 4))]
  transfers between devices with their start and end apart: 5 -> 5, of which waited for: 0 -> 0; matrix products, arithmetic and copies ran while one was open for 34% -> 15% of each run, Pallas kernels for 0% -> 0%
where the time goes in v3:
time: 60.9 us; the launch traced here: 60.4 us
  starting transfers between devices  20.9 us (34%)
  local copies, waits for them, and re-layouts  19.1 us (31%)
  other arithmetic  8.73 us (14%)
  Pallas kernels  7.29 us (12%)
  matrix products  4.21 us (7%)
    ppermute x5, starting transfers between devices, move(): return lax.ppermute(value, ('lat', 'lon'), pairs)  20.9 us
    reshape x2, local copies, waits for them, and re-layouts, shards(): jnp.transpose(rows, (1, 0, 2, 3))  8.82 us
    transpose x1, other arithmetic, shards(): jnp.transpose(rows, (1, 0, 2, 3))  8.15 us
    pallas_call x1, Pallas kernels, shards(): pl.pallas_call(conv_mix_kernel, out_shape=jax.ShapeDtypeStruct((out_rows,...  7.29 us
    transpose x2, local copies, waits for them, and re-layouts, shards(): jnp.transpose(mixed, (2, 1, 3, 0, 4))  2.81 us
    dot_general x1, matrix products, band_coupling(): lax.dot_general(filter_hit, slot_hit, (((0,), (0,)), ((), ())), preferred...  2.42 us
    unnamed x11, local copies, waits for them, and re-layouts  2.16 us
    slice x1, local copies, waits for them, and re-layouts, gather_rows(): below = move(x[LAT_DEV - OVERHANG:], 1, 0)  2.02 us
  transfers between devices with their start and end apart: 5, of which 0 were waited for; matrix products, arithmetic and copies ran while one was open for 15% of the time, Pallas kernels for 0%

profile of v3, /device:TPU:129, one launch (start us, length us, event | category | flops | bytes accessed | tf_op | source)
XLA Modules:
  0.0 60.4 jit_solution(1402290312297265491)
XLA Ops:
  0.0 2.0 %fusion.30 = (bf16[3,90,2,512]{3,2,1,0:T(2,128)(2,1)S(1)}, bf16[3,90,2,512]{3,2,1,0:T(2,128)(2,1)S(1)}) fusion(bf16[4,90,2,512]{3,2,1,0:T(2,128)(2,1)} %param.6), kind=kLoop, calls=%fused_computation.56 | loop fusion | bytes 2211840 | tf_op jit(solution)/shard_map/slice | solution.py:69
  2.0 3.1 %collective-permute-start.1 = (bf16[3,90,2,512]{3,2,1,0:T(2,128)(2,1)S(1)}, bf16[3,90,2,512]{3,2,1,0:T(2,128)(2,1)S(1)}, u32[]{:S(2)}, u32[]{:S(2)}) collective-permute-start(bf16[3,90,2,512]{3,2,1,0:T(2,128)(2,1)S(1)} %get-tuple-element.14), channel_id=1, source_target_pairs={{0,8},{1,9},{2,10},{3,11},{4,12},{5,13},{6,14},{7,15},{8,16},{9,17... | collective-permute-start | bytes 1658888 | tf_op jit(solution)/shard_map/ppermute | solution.py:67
  5.2 5.5 %collective-permute-start.4 = (bf16[3,90,2,512]{3,2,1,0:T(2,128)(2,1)S(1)}, bf16[3,90,2,512]{3,2,1,0:T(2,128)(2,1)}, u32[]{:S(2)}, u32[]{:S(2)}) collective-permute-start(bf16[3,90,2,512]{3,2,1,0:T(2,128)(2,1)S(1)} %get-tuple-element.15), channel_id=1, source_target_pairs={{8,0},{9,1},{10,2},{11,3},{12,4},{13,5},{14,6},{15,7},{16,8},{17,9... | collective-permute-start | bytes 1658888 | tf_op jit(solution)/shard_map/ppermute | solution.py:67
  10.6 0.9 %fusion.29 = (bf16[3,6,2,512]{3,2,1,0:T(2,128)(2,1)S(1)}, bf16[3,6,2,512]{3,2,1,0:T(2,128)(2,1)S(1)}) fusion(bf16[4,90,2,512]{3,2,1,0:T(2,128)(2,1)} %param.6), kind=kLoop, calls=%fused_computation.55 | loop fusion | bytes 147456 | tf_op jit(solution)/shard_map/slice | solution.py:72
  11.6 1.9 %collective-permute-start = (bf16[3,6,2,512]{3,2,1,0:T(2,128)(2,1)S(1)}, bf16[3,6,2,512]{3,2,1,0:T(2,128)(2,1)}, u32[]{:S(2)}, u32[]{:S(2)}) collective-permute-start(bf16[3,6,2,512]{3,2,1,0:T(2,128)(2,1)S(1)} %get-tuple-element.12), channel_id=1, source_target_pairs={{0,9},{1,10},{2,11},{3,12},{4,13},{5,14},{6,15},{7,8},{8,17},{9,18... | collective-permute-start | bytes 110600 | tf_op jit(solution)/shard_map/ppermute | solution.py:67
  13.5 8.0 %collective-permute-start.3 = (bf16[3,6,2,512]{3,2,1,0:T(2,128)(2,1)S(1)}, bf16[3,6,2,512]{3,2,1,0:T(2,128)(2,1)S(1)}, u32[]{:S(2)}, u32[]{:S(2)}) collective-permute-start(bf16[3,6,2,512]{3,2,1,0:T(2,128)(2,1)S(1)} %get-tuple-element.13), channel_id=1, source_target_pairs={{8,1},{9,2},{10,3},{11,4},{12,5},{13,6},{14,7},{15,0},{16,9},{17,1... | collective-permute-start | bytes 110600 | tf_op jit(solution)/shard_map/ppermute | solution.py:67
  21.5 0.8 %slice.53 = bf16[4,6,2,512]{3,2,1,0:T(2,128)(2,1)S(1)} slice(bf16[4,90,2,512]{3,2,1,0:T(2,128)(2,1)} %param.6), slice={[0:4], [84:90], [0:2], [0:512]} | slice | bytes 98304 | tf_op jit(solution)/shard_map/slice | solution.py:59
  22.3 2.4 %collective-permute-start.2 = (bf16[4,6,2,512]{3,2,1,0:T(2,128)(2,1)S(1)}, bf16[4,6,2,512]{3,2,1,0:T(2,128)(2,1)}, u32[]{:S(2)}, u32[]{:S(2)}) collective-permute-start(bf16[4,6,2,512]{3,2,1,0:T(2,128)(2,1)S(1)} %slice.53), channel_id=1, source_target_pairs={{0,1},{1,2},{2,3},{3,4},{4,5},{5,6},{6,7},{7,0},{8,9},{9,10},{10,1... | collective-permute-start | bytes 147464 | tf_op jit(solution)/shard_map/ppermute | solution.py:67
  24.8 0.6 gather_fusion
  25.4 0.1 broadcast_select_fusion
  25.5 0.1 slice_reduce_fusion
  25.6 0.8 %copy.10 = s32[32,3]{1,0:T(8,128)S(1)} copy(s32[32,3]{0,1:T(4,128)} %param.9) | data formatting | bytes 768 | tf_op args[3]
  26.3 0.6 gather_fusion.1
  26.9 0.1 broadcast_select_fusion.1
  27.0 0.2 negate_reduce_fusion
  27.2 0.1 fusion.26
  27.3 0.1 and.97
  27.4 0.1 ge.53
  27.4 0.1 lt.89
  27.5 0.1 sub.51
  27.7 0.0 copy-start.4
  27.7 0.0 copy-start.1
  27.7 2.4 %fusion.6 = f32[1024,512]{1,0:T(8,128)S(1)} fusion(s32[1536]{0:T(1024)S(1)} %eq.28, s32[1536]{0:T(1024)S(1)} %add_select_fusion), kind=kOutput, calls=%fused_computation.11 | convolution fusion | flops 1612972032 | bytes 2109440 | tf_op jit(solution)/shard_map/dot_general | solution.py:46
  30.1 1.8 %fusion.22.coupling_ref = f32[3,512]{1,0:T(4,128)} fusion(f32[1024,512]{1,0:T(8,128)S(1)} %fusion.6, f32[1024,3]{0,1:T(4,128)S(1)} %copy-done.4), kind=kOutput, calls=%fused_computation.29 | convolution fusion | flops 18877440 | bytes 2115584 | tf_op jit(solution)/shard_map/dot_general | solution.py:49
  31.9 0.6 copy-done.3
  32.5 0.8 %copy-done.2 = bf16[3,90,2,512]{3,2,1,0:T(2,128)(2,1)} copy-done((bf16[3,90,2,512]{3,2,1,0:T(2,128)(2,1)}, bf16[3,90,2,512]{3,2,1,0:T(2,128)(2,1)S(1)}, u32[]{:S(2)}) %copy-start.2) | copy-done | bytes 552984
  33.3 8.1 %fusion.18 = bf16[100,16,2,512]{3,2,0,1:T(2,128)(2,1)S(1)} fusion(bf16[3,90,2,512]{3,2,1,0:T(2,128)(2,1)} %collective-permute-done.4, bf16[3,6,2,512]{3,2,1,0:T(2,128)(2,1)} %copy-done.3, bf16[4,90,2,512]{3,2,1,0:T(2,128)(2,1)S(1)} %copy-done.1, bf16[4,6,2,512]{3,2,1,0:T(2,128)(2,1)} %collective-permute-done.2, bf16[3,90,2,512]{3,2,1,0:T(2,128)(2,1)} %copy-done.2, ...), kind=kLoop, calls=%fused_computation.23 | loop fusion | flops 44236800 | bytes 5242880 | tf_op jit(solution)/shard_map/transpose | solution.py:132
  41.5 3.3 %reshape.207 = bf16[100,16,1024]{2,0,1:T(8,128)(2,1)} reshape(bf16[100,16,2,512]{3,2,0,1:T(2,128)(2,1)S(1)} %fusion.18) | data formatting | bytes 6553600 | tf_op jit(solution)/shard_map/reshape | solution.py:132
  44.8 5.5 %copy.13.rows_ref = bf16[100,16,1024]{2,1,0:T(8,128)(2,1)} copy(bf16[100,16,1024]{2,0,1:T(8,128)(2,1)} %reshape.207) | data formatting | bytes 6553600 | tf_op jit(solution)/shard_map/reshape | solution.py:132
  50.3 7.3 %shard_map.64 = bf16[768,512]{1,0:T(8,128)(2,1)} custom-call(f32[3,512]{1,0:T(4,128)} %fusion.22.coupling_ref, bf16[100,16,1024]{2,1,0:T(8,128)(2,1)} %copy.13.rows_ref, bf16[1536,512]{1,0:T(8,128)(2,1)} %weight_ref.1, bf16[512,512]{1,0:T(8,128)(2,1)} %mix_ref.1), custom_call_target="tpu_custom_call" | custom-call | flops 3120562176 | bytes 5898240 | tf_op jit(solution)/shard_map/pallas_call | solution.py:134
  57.6 1.2 %slice_bitcast_fusion = bf16[4,3,30,2,512]{4,2,0,1,3:T(8,128)(2,1)S(1)} fusion(bf16[2,3,4,32,512]{4,3,2,1,0:T(8,128)(2,1)} %bitcast.28), kind=kLoop, calls=%fused_computation.30 | loop fusion | bytes 1474560 | tf_op jit(solution)/shard_map/transpose | solution.py:148
  58.8 1.6 %copy.12 = bf16[4,3,30,2,512]{4,3,2,1,0:T(2,128)(2,1)} copy(bf16[4,3,30,2,512]{4,2,0,1,3:T(8,128)(2,1)S(1)} %slice_bitcast_fusion) | data formatting | bytes 1474560 | tf_op jit(solution)/shard_map/transpose | solution.py:148
  (24 shorter events, 0.2 us)
Async XLA Ops:
  0.0 24.8 %copy-start = (s32[32,4,4,128]{3,2,1,0:T(4,128)S(1)}, s32[32,4,4,128]{3,2,1,0:T(4,128)}, u32[]{:S(2)}) copy-start(s32[32,4,4,128]{3,2,1,0:T(4,128)} %param.8) | copy-start | bytes 786436
  2.0 29.9 %collective-permute-start.1 = (bf16[3,90,2,512]{3,2,1,0:T(2,128)(2,1)S(1)}, bf16[3,90,2,512]{3,2,1,0:T(2,128)(2,1)S(1)}, u32[]{:S(2)}, u32[]{:S(2)}) collective-permute-start(bf16[3,90,2,512]{3,2,1,0:T(2,128)(2,1)S(1)} %get-tuple-element.14), channel_id=1, source_target_pairs={{0,8},{1,9},{2,10},{3,11},{4,12},{5,13},{6,14},{7,15},{8,16},{9,17... | collective-permute-start | bytes 1658888 | tf_op jit(solution)/shard_map/ppermute | solution.py:67
  5.2 28.2 %collective-permute-start.4 = (bf16[3,90,2,512]{3,2,1,0:T(2,128)(2,1)S(1)}, bf16[3,90,2,512]{3,2,1,0:T(2,128)(2,1)}, u32[]{:S(2)}, u32[]{:S(2)}) collective-permute-start(bf16[3,90,2,512]{3,2,1,0:T(2,128)(2,1)S(1)} %get-tuple-element.15), channel_id=1, source_target_pairs={{8,0},{9,1},{10,2},{11,3},{12,4},{13,5},{14,6},{15,7},{16,8},{17,9... | collective-permute-start | bytes 1658888 | tf_op jit(solution)/shard_map/ppermute | solution.py:67
  11.6 20.4 %collective-permute-start = (bf16[3,6,2,512]{3,2,1,0:T(2,128)(2,1)S(1)}, bf16[3,6,2,512]{3,2,1,0:T(2,128)(2,1)}, u32[]{:S(2)}, u32[]{:S(2)}) collective-permute-start(bf16[3,6,2,512]{3,2,1,0:T(2,128)(2,1)S(1)} %get-tuple-element.12), channel_id=1, source_target_pairs={{0,9},{1,10},{2,11},{3,12},{4,13},{5,14},{6,15},{7,8},{8,17},{9,18... | collective-permute-start | bytes 110600 | tf_op jit(solution)/shard_map/ppermute | solution.py:67
  13.5 18.4 %collective-permute-start.3 = (bf16[3,6,2,512]{3,2,1,0:T(2,128)(2,1)S(1)}, bf16[3,6,2,512]{3,2,1,0:T(2,128)(2,1)S(1)}, u32[]{:S(2)}, u32[]{:S(2)}) collective-permute-start(bf16[3,6,2,512]{3,2,1,0:T(2,128)(2,1)S(1)} %get-tuple-element.13), channel_id=1, source_target_pairs={{8,1},{9,2},{10,3},{11,4},{12,5},{13,6},{14,7},{15,0},{16,9},{17,1... | collective-permute-start | bytes 110600 | tf_op jit(solution)/shard_map/ppermute | solution.py:67
  22.3 9.6 %collective-permute-start.2 = (bf16[4,6,2,512]{3,2,1,0:T(2,128)(2,1)S(1)}, bf16[4,6,2,512]{3,2,1,0:T(2,128)(2,1)}, u32[]{:S(2)}, u32[]{:S(2)}) collective-permute-start(bf16[4,6,2,512]{3,2,1,0:T(2,128)(2,1)S(1)} %slice.53), channel_id=1, source_target_pairs={{0,1},{1,2},{2,3},{3,4},{4,5},{5,6},{6,7},{7,0},{8,9},{9,10},{10,1... | collective-permute-start | bytes 147464 | tf_op jit(solution)/shard_map/ppermute | solution.py:67
  27.7 2.4 %copy-start.4 = (f32[1024,3]{0,1:T(4,128)S(1)}, f32[1024,3]{0,1:T(4,128)}, u32[]{:S(2)}) copy-start(f32[1024,3]{0,1:T(4,128)} %param.7) | copy-start | bytes 36868
  27.7 5.7 %copy-start.1 = (bf16[4,90,2,512]{3,2,1,0:T(2,128)(2,1)S(1)}, bf16[4,90,2,512]{3,2,1,0:T(2,128)(2,1)}, u32[]{:S(2)}) copy-start(bf16[4,90,2,512]{3,2,1,0:T(2,128)(2,1)} %param.6) | copy-start | bytes 2211844
  31.9 0.6 copy-start.3
  32.5 0.8 %copy-start.2 = (bf16[3,90,2,512]{3,2,1,0:T(2,128)(2,1)}, bf16[3,90,2,512]{3,2,1,0:T(2,128)(2,1)S(1)}, u32[]{:S(2)}) copy-start(bf16[3,90,2,512]{3,2,1,0:T(2,128)(2,1)S(1)} %collective-permute-done.1) | copy-start | bytes 1658884

commit v4 on v3

--- a/solution.py
+++ b/solution.py
@@ -10,7 +10,7 @@
 SHIFTS = 7
 OVERHANG = 3
 LAT_DEV = 4
-ROW_PAD = 16
+ROW_PAD = 10
 
 
 def band_coupling(entries, band_meta, coeffs, band_index, grid_rows):
@@ -77,26 +77,30 @@
     return jnp.concatenate([rows_below, rows_mid, rows_above], axis=0)
 
 
-WINDOW = 30
+WINDOW = 32
 LON_PAD = 32
 TAPS = 128
+DEPTH = 384
 
 
 def conv_mix_kernel(coupling_ref, rows_ref, weight_ref, mix_ref, out_ref, toeplitz_ref):
-    lo = SHIFTS - 1
-    cols = (WINDOW + lo + 4) * ROW_PAD
     for k in range(BASIS):
         for q in range(LAT_DEV):
             taps = coupling_ref[k : k + 1, q * TAPS : (q + 1) * TAPS]
-            wide = jnp.concatenate([taps, jnp.zeros((1, cols - TAPS), jnp.float32)], axis=1)
-            block = jnp.broadcast_to(wide, (LON_PAD, cols))
-            block = pltpu.roll(block, 0, 1, stride=ROW_PAD, stride_axis=0)
-            toeplitz_ref[pl.ds((k * LAT_DEV + q) * LON_PAD, LON_PAD), :] = block.astype(jnp.bfloat16)
+            wide = jnp.concatenate([taps, jnp.zeros((1, DEPTH - TAPS), jnp.float32)], axis=1)
+            for g in range(LON_PAD // 8):
+                block = jnp.broadcast_to(wide, (8, DEPTH))
+                if g:
+                    block = pltpu.roll(block, 8 * g * ROW_PAD, 1)
+                block = pltpu.roll(block, 0, 1, stride=ROW_PAD, stride_axis=0)
+                toeplitz_ref[pl.ds((k * LAT_DEV + q) * LON_PAD + 8 * g, 8), :] = block.astype(
+                    jnp.bfloat16
+                )
     nwin = out_ref.shape[0] // (2 * LAT_DEV * LON_PAD)
     span = LAT_DEV * LON_PAD
     pieces = [[[] for _ in range(2)] for _ in range(BASIS)]
     for j in range(nwin):
-        window = rows_ref[pl.ds(j * WINDOW, cols // ROW_PAD), :, :].reshape(cols, 2 * CHANNELS)
+        window = rows_ref[pl.ds(j * WINDOW * ROW_PAD, DEPTH), :]
         conv = jnp.dot(toeplitz_ref[...], window, preferred_element_type=jnp.float32)
         for k in range(BASIS):
             for m in range(2):
@@ -120,32 +124,31 @@
     band_index = lax.axis_index("lat")
     grid_rows = LAT_DEV * lax.axis_size("lat")
     nrows, nlon, members, channels = fields.shape
-    lo = SHIFTS - 1
     coupling = band_coupling(entries, band_info, coeffs, band_index, grid_rows)
     coupling = coupling.astype(jnp.bfloat16).astype(jnp.float32)
     rows = gather_rows(fields)
     rows_in, ext = rows.shape[0], rows.shape[1]
-    nwin = nlon // WINDOW
-    cols = (WINDOW + lo + 4) * ROW_PAD
-    lon_rows = (nwin - 1) * WINDOW + cols // ROW_PAD
-    rows = jnp.pad(rows, ((0, ROW_PAD - rows_in), (0, lon_rows - ext), (0, 0), (0, 0)))
-    rows = jnp.transpose(rows, (1, 0, 2, 3)).reshape(lon_rows, ROW_PAD, members * channels)
+    nwin = -(-nlon // WINDOW)
+    depth_rows = (nwin - 1) * WINDOW * ROW_PAD + DEPTH
+    rows = jnp.transpose(rows, (1, 0, 2, 3)).reshape(ext * rows_in, members * channels)
+    rows = jnp.pad(rows, ((0, depth_rows - ext * rows_in), (0, 0)))
     out_rows = members * nwin * LAT_DEV * LON_PAD
     mixed = pl.pallas_call(
         conv_mix_kernel,
         out_shape=jax.ShapeDtypeStruct((out_rows, CHANNELS), jnp.bfloat16),
         in_specs=[pl.BlockSpec(memory_space=pltpu.VMEM)] * 4,
         out_specs=pl.BlockSpec(memory_space=pltpu.VMEM),
-        scratch_shapes=[pltpu.VMEM((BASIS * LAT_DEV * LON_PAD, cols), jnp.bfloat16)],
+        scratch_shapes=[pltpu.VMEM((BASIS * LAT_DEV * LON_PAD, DEPTH), jnp.bfloat16)],
         cost_estimate=pl.CostEstimate(
-            flops=2 * BASIS * LAT_DEV * LON_PAD * cols * 1024 * nwin
+            flops=2 * BASIS * LAT_DEV * LON_PAD * DEPTH * 1024 * nwin
             + 2 * out_rows * CHANNELS * CHANNELS * (BASIS + 1),
             transcendentals=out_rows * CHANNELS,
             bytes_accessed=rows.size * 2 + (BASIS + 2) * CHANNELS * CHANNELS * 2,
         ),
     )(coupling, rows, conv_weight, mix_weight)
-    mixed = mixed.reshape(members, nwin, LAT_DEV, LON_PAD, CHANNELS)[:, :, :, :WINDOW]
-    return jnp.transpose(mixed, (2, 1, 3, 0, 4)).reshape(LAT_DEV, nlon, members, CHANNELS)
+    mixed = mixed.reshape(members, nwin, LAT_DEV, LON_PAD, CHANNELS)
+    mixed = jnp.transpose(mixed, (2, 1, 3, 0, 4)).reshape(LAT_DEV, nwin * LON_PAD, members, CHANNELS)
+    return mixed[:, :nlon]
 
 
 def solution(mesh):

time: 60.9 us -> 46.3 us (0.76)
  local copies, waits for them, and re-layouts: 19.1 us -> 10.5 us
  other arithmetic: 8.73 us -> 3.63 us
  Pallas kernels: 7.29 us -> 6.53 us
    reshape x2 -> x0, local copies, waits for them, and re-layouts: 8.82 us -> none  [shards(): jnp.transpose(rows, (1, 0, 2, 3))]
    transpose x1, other arithmetic: 8.15 us -> 3.05 us  [shards(): jnp.transpose(rows, (1, 0, 2, 3)).reshape(ext * rows_in, members * channels)]
    unnamed x11 -> x10, local copies, waits for them, and re-layouts: 2.16 us -> 0.63 us
    pad x0 -> x1, local copies, waits for them, and re-layouts: none -> 1.52 us  [shards(): rows = jnp.pad(rows, ((0, depth_rows - ext * rows_in), (0, 0)))]
    slice x0 -> x1, local copies, waits for them, and re-layouts: none -> 1.37 us  [shards(): return mixed[:, :nlon]]
    transpose x0 -> x1, local copies, waits for them, and re-layouts: none -> 1.35 us  [shards(): jnp.transpose(rows, (1, 0, 2, 3)).reshape(ext * rows_in, members * channels)]
    transpose x2 -> x1, local copies, waits for them, and re-layouts: 2.81 us -> 1.94 us  [shards(): jnp.transpose(mixed, (2, 1, 3, 0, 4))]
    slice x1, local copies, waits for them, and re-layouts: 0.9 us -> 0.05 us  [gather_rows(): below_left = move(tail[LAT_DEV - OVERHANG:], 1, 1)]
  transfers between devices with their start and end apart: 5 -> 5, of which waited for: 0 -> 0; matrix products, arithmetic and copies ran while one was open for 15% -> 14% of each run, Pallas kernels for 0% -> 0%
where the time goes in v4:
time: 46.3 us; the launch traced here: 46.1 us
  starting transfers between devices  20.9 us (45%)
  local copies, waits for them, and re-layouts  10.5 us (23%)
  Pallas kernels  6.53 us (14%)
  matrix products  4.22 us (9%)
  other arithmetic  3.63 us (8%)
    ppermute x5, starting transfers between devices, move(): return lax.ppermute(value, ('lat', 'lon'), pairs)  20.9 us
    pallas_call x1, Pallas kernels, shards(): pl.pallas_call(conv_mix_kernel, out_shape=jax.ShapeDtypeStruct((out_rows,...  6.53 us
    transpose x1, other arithmetic, shards(): jnp.transpose(rows, (1, 0, 2, 3)).reshape(ext * rows_in, members * channels)  3.05 us
    dot_general x1, matrix products, band_coupling(): lax.dot_general(filter_hit, slot_hit, (((0,), (0,)), ((), ())), preferred...  2.42 us
    slice x1, local copies, waits for them, and re-layouts, gather_rows(): below = move(x[LAT_DEV - OVERHANG:], 1, 0)  2.12 us
    transpose x1, local copies, waits for them, and re-layouts, shards(): jnp.transpose(mixed, (2, 1, 3, 0, 4))  1.94 us
    dot_general x1, matrix products, band_coupling(): jnp.dot(coeffs.T, counts, precision=lax.Precision.HIGHEST, preferred_elem...  1.8 us
    pad x1, local copies, waits for them, and re-layouts, shards(): rows = jnp.pad(rows, ((0, depth_rows - ext * rows_in), (0, 0)))  1.52 us
  transfers between devices with their start and end apart: 5, of which 0 were waited for; matrix products, arithmetic and copies ran while one was open for 14% of the time, Pallas kernels for 0%

profile of v4, /device:TPU:129, one launch (start us, length us, event | category | flops | bytes accessed | tf_op | source)
XLA Modules:
  0.0 46.1 jit_solution(13188263518654580207)
XLA Ops:
  0.0 2.1 %fusion.12 = (bf16[3,90,2,512]{3,2,1,0:T(2,128)(2,1)S(1)}, bf16[3,90,2,512]{3,2,1,0:T(2,128)(2,1)S(1)}) fusion(bf16[4,90,2,512]{3,2,1,0:T(2,128)(2,1)} %param.6), kind=kLoop, calls=%fused_computation.36 | loop fusion | bytes 2211840 | tf_op jit(solution)/shard_map/slice | solution.py:69
  2.1 3.1 %collective-permute-start.1 = (bf16[3,90,2,512]{3,2,1,0:T(2,128)(2,1)S(1)}, bf16[3,90,2,512]{3,2,1,0:T(2,128)(2,1)S(1)}, u32[]{:S(2)}, u32[]{:S(2)}) collective-permute-start(bf16[3,90,2,512]{3,2,1,0:T(2,128)(2,1)S(1)} %get-tuple-element.14), channel_id=1, source_target_pairs={{0,8},{1,9},{2,10},{3,11},{4,12},{5,13},{6,14},{7,15},{8,16},{9,17... | collective-permute-start | bytes 1658888 | tf_op jit(solution)/shard_map/ppermute | solution.py:67
  5.3 5.5 %collective-permute-start.4 = (bf16[3,90,2,512]{3,2,1,0:T(2,128)(2,1)S(1)}, bf16[3,90,2,512]{3,2,1,0:T(2,128)(2,1)S(1)}, u32[]{:S(2)}, u32[]{:S(2)}) collective-permute-start(bf16[3,90,2,512]{3,2,1,0:T(2,128)(2,1)S(1)} %get-tuple-element.15), channel_id=1, source_target_pairs={{8,0},{9,1},{10,2},{11,3},{12,4},{13,5},{14,6},{15,7},{16,8},{17,9... | collective-permute-start | bytes 1658888 | tf_op jit(solution)/shard_map/ppermute | solution.py:67
  10.8 1.9 %collective-permute-start = (bf16[3,6,2,512]{3,2,1,0:T(2,128)(2,1)S(1)}, bf16[3,6,2,512]{3,2,1,0:T(2,128)(2,1)S(1)}, u32[]{:S(2)}, u32[]{:S(2)}) collective-permute-start(bf16[3,6,2,512]{3,2,1,0:T(2,128)(2,1)S(1)} %get-tuple-element.12), channel_id=1, source_target_pairs={{0,9},{1,10},{2,11},{3,12},{4,13},{5,14},{6,15},{7,8},{8,17},{9,18... | collective-permute-start | bytes 110600 | tf_op jit(solution)/shard_map/ppermute | solution.py:67
  12.8 8.0 %collective-permute-start.3 = (bf16[3,6,2,512]{3,2,1,0:T(2,128)(2,1)S(1)}, bf16[3,6,2,512]{3,2,1,0:T(2,128)(2,1)S(1)}, u32[]{:S(2)}, u32[]{:S(2)}) collective-permute-start(bf16[3,6,2,512]{3,2,1,0:T(2,128)(2,1)S(1)} %get-tuple-element.13), channel_id=1, source_target_pairs={{8,1},{9,2},{10,3},{11,4},{12,5},{13,6},{14,7},{15,0},{16,9},{17,1... | collective-permute-start | bytes 110600 | tf_op jit(solution)/shard_map/ppermute | solution.py:67
  20.8 2.4 %collective-permute-start.2 = (bf16[4,6,2,512]{3,2,1,0:T(2,128)(2,1)S(1)}, bf16[4,6,2,512]{3,2,1,0:T(2,128)(2,1)S(1)}, u32[]{:S(2)}, u32[]{:S(2)}) collective-permute-start(bf16[4,6,2,512]{3,2,1,0:T(2,128)(2,1)S(1)} %slice.53), channel_id=1, source_target_pairs={{0,1},{1,2},{2,3},{3,4},{4,5},{5,6},{6,7},{7,0},{8,9},{9,10},{10,1... | collective-permute-start | bytes 147464 | tf_op jit(solution)/shard_map/ppermute | solution.py:67
  23.3 0.6 %gather_fusion = s32[3,4,4,128]{3,2,1,0:T(4,128)S(1)} fusion(s32[32,4,4,128]{3,2,1,0:T(4,128)S(1)} %copy-done, s32[1024]{0:T(1024)S(1)} %pad_clamp_fusion), kind=kCustom, calls=%fused_computation | custom fusion | bytes 49164 | tf_op jit(solution)/shard_map/jit(_take)/gather | solution.py:22
  23.8 0.1 broadcast_select_fusion
  23.9 0.1 slice_reduce_fusion
  24.1 0.1 copy.10
  24.1 0.6 %gather_fusion.1 = s32[3,3]{1,0:T(4,128)S(1)} fusion(s32[32,3]{1,0:T(8,128)S(1)} %copy.10, s32[1024]{0:T(1024)S(1)} %pad_clamp_fusion), kind=kCustom, calls=%fused_computation.1 | custom fusion | bytes 84 | tf_op jit(solution)/shard_map/jit(_take)/gather | solution.py:23
  24.7 0.1 broadcast_select_fusion.1
  24.8 0.2 negate_reduce_fusion
  25.0 0.1 fusion.8
  25.1 0.1 and.97
  25.2 0.1 ge.53
  25.2 0.1 lt.86
  25.3 0.1 sub.51
  25.5 0.0 copy-start.2
  25.5 2.4 %fusion = f32[1024,512]{1,0:T(8,128)S(1)} fusion(s32[1536]{0:T(1024)S(1)} %eq.28, s32[1536]{0:T(1024)S(1)} %add_select_fusion), kind=kOutput, calls=%fused_computation.3 | convolution fusion | flops 1612972032 | bytes 2109440 | tf_op jit(solution)/shard_map/dot_general | solution.py:46
  27.9 1.8 %fusion.4.coupling_ref = f32[3,512]{1,0:T(4,128)} fusion(f32[1024,512]{1,0:T(8,128)S(1)} %fusion, f32[1024,3]{0,1:T(4,128)S(1)} %copy-done.2), kind=kOutput, calls=%fused_computation.10 | convolution fusion | flops 18877440 | bytes 2115584 | tf_op jit(solution)/shard_map/dot_general | solution.py:49
  29.7 0.0 collective-permute-done
  29.7 0.0 collective-permute-done.2
  29.7 0.0 collective-permute-done.1
  29.7 0.0 collective-permute-done.4
  29.7 3.1 %maximum_bitcast_fusion = bf16[96,10,2,512]{3,2,0,1:T(2,128)(2,1)S(1)} fusion(bf16[3,90,2,512]{3,2,1,0:T(2,128)(2,1)S(1)} %collective-permute-done.4, bf16[3,6,2,512]{3,2,1,0:T(2,128)(2,1)S(1)} %collective-permute-done.3, bf16[4,90,2,512]{3,2,1,0:T(2,128)(2,1)S(1)} %copy-done.1, bf16[4,6,2,512]{3,2,1,0:T(2,128)(2,1)S(1)} %collective-permute-done.2, ...), kind=kLoop, calls=%fused_computation.6 | loop fusion | flops 4915200 | bytes 3932160 | tf_op jit(solution)/shard_map/transpose | solution.py:133
  32.8 1.4 %copy.11 = bf16[96,10,2,512]{3,2,1,0:T(2,128)(2,1)S(1)} copy(bf16[96,10,2,512]{3,2,0,1:T(2,128)(2,1)S(1)} %maximum_bitcast_fusion) | data formatting | bytes 3932160 | tf_op jit(solution)/shard_map/transpose | solution.py:133
  34.2 0.5 %copy.20 = bf16[120,8,2,512]{3,1,2,0:T(8,128)(2,1)S(1)} copy(bf16[120,8,2,512]{3,2,1,0:T(2,128)(2,1)S(1)} %bitcast.30) | data formatting | bytes 3932160
  34.7 1.5 %pad.4.rows_ref = bf16[1024,1024]{1,0:T(8,128)(2,1)} pad(bf16[960,1024]{1,0:T(8,128)(2,1)S(1)} %bitcast.29, bf16[]{:T(256)} %constant.56.clone.1), padding=0_64x0_0 | pad | bytes 4063234 | tf_op jit(solution)/shard_map/jit(_pad)/pad | solution.py:134
  36.2 6.5 %shard_map.64 = bf16[768,512]{1,0:T(8,128)(2,1)} custom-call(f32[3,512]{1,0:T(4,128)} %fusion.4.coupling_ref, bf16[1024,1024]{1,0:T(8,128)(2,1)} %pad.4.rows_ref, bf16[1536,512]{1,0:T(8,128)(2,1)} %weight_ref.1, bf16[512,512]{1,0:T(8,128)(2,1)} %mix_ref.1), custom_call_target="tpu_custom_call" | custom-call | flops 2516582400 | bytes 4718592 | tf_op jit(solution)/shard_map/pallas_call | solution.py:136
  42.7 1.9 %copy.12 = bf16[4,3,32,2,512]{4,3,2,1,0:T(2,128)(2,1)S(1)} copy(bf16[4,3,32,2,512]{4,2,0,1,3:T(8,128)(2,1)} %bitcast.32) | data formatting | bytes 1572864 | tf_op jit(solution)/shard_map/transpose | solution.py:150
  44.7 1.4 %slice.65 = bf16[4,90,2,512]{3,2,1,0:T(2,128)(2,1)} slice(bf16[4,96,2,512]{3,2,1,0:T(2,128)(2,1)S(1)} %bitcast.31), slice={[0:4], [0:90], [0:2], [0:512]} | slice | bytes 1474560 | tf_op jit(solution)/shard_map/slice | solution.py:151
  (23 shorter events, 0.2 us)
Async XLA Ops:
  0.0 23.3 %copy-start = (s32[32,4,4,128]{3,2,1,0:T(4,128)S(1)}, s32[32,4,4,128]{3,2,1,0:T(4,128)}, u32[]{:S(2)}) copy-start(s32[32,4,4,128]{3,2,1,0:T(4,128)} %param.8) | copy-start | bytes 786436
  0.0 10.8 %copy-start.1 = (bf16[4,90,2,512]{3,2,1,0:T(2,128)(2,1)S(1)}, bf16[4,90,2,512]{3,2,1,0:T(2,128)(2,1)}, u32[]{:S(2)}) copy-start(bf16[4,90,2,512]{3,2,1,0:T(2,128)(2,1)} %param.6) | copy-start | bytes 2211844
  0.0 24.0 %copy-start.3 = (s32[32,3]{0,1:T(4,128)S(1)}, s32[32,3]{0,1:T(4,128)}, u32[]{:S(2)}) copy-start(s32[32,3]{0,1:T(4,128)} %param.9) | copy-start | bytes 1156
  2.1 27.6 %collective-permute-start.1 = (bf16[3,90,2,512]{3,2,1,0:T(2,128)(2,1)S(1)}, bf16[3,90,2,512]{3,2,1,0:T(2,128)(2,1)S(1)}, u32[]{:S(2)}, u32[]{:S(2)}) collective-permute-start(bf16[3,90,2,512]{3,2,1,0:T(2,128)(2,1)S(1)} %get-tuple-element.14), channel_id=1, source_target_pairs={{0,8},{1,9},{2,10},{3,11},{4,12},{5,13},{6,14},{7,15},{8,16},{9,17... | collective-permute-start | bytes 1658888 | tf_op jit(solution)/shard_map/ppermute | solution.py:67
  5.3 24.5 %collective-permute-start.4 = (bf16[3,90,2,512]{3,2,1,0:T(2,128)(2,1)S(1)}, bf16[3,90,2,512]{3,2,1,0:T(2,128)(2,1)S(1)}, u32[]{:S(2)}, u32[]{:S(2)}) collective-permute-start(bf16[3,90,2,512]{3,2,1,0:T(2,128)(2,1)S(1)} %get-tuple-element.15), channel_id=1, source_target_pairs={{8,0},{9,1},{10,2},{11,3},{12,4},{13,5},{14,6},{15,7},{16,8},{17,9... | collective-permute-start | bytes 1658888 | tf_op jit(solution)/shard_map/ppermute | solution.py:67
  10.8 18.9 %collective-permute-start = (bf16[3,6,2,512]{3,2,1,0:T(2,128)(2,1)S(1)}, bf16[3,6,2,512]{3,2,1,0:T(2,128)(2,1)S(1)}, u32[]{:S(2)}, u32[]{:S(2)}) collective-permute-start(bf16[3,6,2,512]{3,2,1,0:T(2,128)(2,1)S(1)} %get-tuple-element.12), channel_id=1, source_target_pairs={{0,9},{1,10},{2,11},{3,12},{4,13},{5,14},{6,15},{7,8},{8,17},{9,18... | collective-permute-start | bytes 110600 | tf_op jit(solution)/shard_map/ppermute | solution.py:67
  12.8 16.9 %collective-permute-start.3 = (bf16[3,6,2,512]{3,2,1,0:T(2,128)(2,1)S(1)}, bf16[3,6,2,512]{3,2,1,0:T(2,128)(2,1)S(1)}, u32[]{:S(2)}, u32[]{:S(2)}) collective-permute-start(bf16[3,6,2,512]{3,2,1,0:T(2,128)(2,1)S(1)} %get-tuple-element.13), channel_id=1, source_target_pairs={{8,1},{9,2},{10,3},{11,4},{12,5},{13,6},{14,7},{15,0},{16,9},{17,1... | collective-permute-start | bytes 110600 | tf_op jit(solution)/shard_map/ppermute | solution.py:67
  20.8 8.9 %collective-permute-start.2 = (bf16[4,6,2,512]{3,2,1,0:T(2,128)(2,1)S(1)}, bf16[4,6,2,512]{3,2,1,0:T(2,128)(2,1)S(1)}, u32[]{:S(2)}, u32[]{:S(2)}) collective-permute-start(bf16[4,6,2,512]{3,2,1,0:T(2,128)(2,1)S(1)} %slice.53), channel_id=1, source_target_pairs={{0,1},{1,2},{2,3},{3,4},{4,5},{5,6},{6,7},{7,0},{8,9},{9,10},{10,1... | collective-permute-start | bytes 147464 | tf_op jit(solution)/shard_map/ppermute | solution.py:67
  25.5 2.4 %copy-start.2 = (f32[1024,3]{0,1:T(4,128)S(1)}, f32[1024,3]{0,1:T(4,128)}, u32[]{:S(2)}) copy-start(f32[1024,3]{0,1:T(4,128)} %param.7) | copy-start | bytes 36868

commit v5 on v4

--- a/solution.py
+++ b/solution.py
@@ -56,25 +56,12 @@
     nlat = lax.axis_size("lat")
     nlon = lax.axis_size("lon")
     lo = SHIFTS - 1
-    tail = x[:, x.shape[1] - lo :]
-
-    def move(value, dlat, dlon):
-        pairs = []
-        for b in range(nlat):
-            if 0 <= b + dlat < nlat:
-                for j in range(nlon):
-                    pairs.append((b * nlon + j, (b + dlat) * nlon + (j + dlon) % nlon))
-        return lax.ppermute(value, ("lat", "lon"), pairs)
-
-    below = move(x[LAT_DEV - OVERHANG :], 1, 0)
-    above = move(x[:OVERHANG], -1, 0)
-    left = move(tail, 0, 1)
-    below_left = move(tail[LAT_DEV - OVERHANG :], 1, 1)
-    above_left = move(tail[:OVERHANG], -1, 1)
-    rows_below = jnp.concatenate([below_left, below], axis=1)
-    rows_mid = jnp.concatenate([left, x], axis=1)
-    rows_above = jnp.concatenate([above_left, above], axis=1)
-    return jnp.concatenate([rows_below, rows_mid, rows_above], axis=0)
+    down = [(b, b + 1) for b in range(nlat - 1)]
+    below = lax.ppermute(x[LAT_DEV - OVERHANG :], "lat", down)
+    above = lax.ppermute(x[:OVERHANG], "lat", [(t, s) for s, t in down])
+    rows = jnp.concatenate([below, x, above], axis=0)
+    tail = lax.ppermute(rows[:, x.shape[1] - lo :], "lon", [(j, (j + 1) % nlon) for j in range(nlon)])
+    return jnp.concatenate([tail, rows], axis=1)
 
 
 WINDOW = 32

time: 46.3 us -> 48.3 us (1.043)
  the two profiles are of different devices: /device:TPU:129 before, /device:TPU:102 now
where the time goes in v5:
time: 48.3 us; the launch traced here: 48.1 us
  waiting for transfers between devices  15.3 us (32%)
  local copies, waits for them, and re-layouts  11.9 us (25%)
  starting transfers between devices  6.89 us (14%)
  Pallas kernels  6.52 us (13%)
  matrix products  4.22 us (9%)
  other arithmetic  3.11 us (6%)
    pallas_call x1, Pallas kernels, shards(): pl.pallas_call(conv_mix_kernel, out_shape=jax.ShapeDtypeStruct((out_rows,...  6.52 us
    ppermute x1, waiting for transfers between devices, gather_rows(): above = lax.ppermute(x[:OVERHANG], 'lat', [(t, s) for s, t in down])  6.46 us
    ppermute x1, waiting for transfers between devices, gather_rows(): below = lax.ppermute(x[LAT_DEV - OVERHANG:], 'lat', down)  5.14 us
    ppermute x1, starting transfers between devices, gather_rows(): below = lax.ppermute(x[LAT_DEV - OVERHANG:], 'lat', down)  4.95 us
    ppermute x1, waiting for transfers between devices, gather_rows(): lax.ppermute(rows[:, x.shape[1] - lo:], 'lon', [(j, (j + 1) % nlon) for j...  3.69 us
    transpose x1, other arithmetic, shards(): jnp.transpose(rows, (1, 0, 2, 3)).reshape(ext * rows_in, members * channels)  2.53 us
    dot_general x1, matrix products, band_coupling(): lax.dot_general(filter_hit, slot_hit, (((0,), (0,)), ((), ())), preferred...  2.42 us
    slice x1, local copies, waits for them, and re-layouts, gather_rows(): above = lax.ppermute(x[:OVERHANG], 'lat', [(t, s) for s, t in down])  2.11 us
  transfers between devices with their start and end apart: 3, of which 3 were waited for; matrix products, arithmetic and copies ran while one was open for 15% of the time, Pallas kernels for 0%

profile of v5, /device:TPU:102, one launch (start us, length us, event | category | flops | bytes accessed | tf_op | source)
XLA Modules:
  0.0 48.1 jit_solution(7748850555043963761)
XLA Ops:
  0.0 2.1 %fusion.11 = (bf16[3,90,2,512]{3,2,1,0:T(2,128)(2,1)S(1)}, bf16[3,90,2,512]{3,2,1,0:T(2,128)(2,1)S(1)}) fusion(bf16[4,90,2,512]{3,2,1,0:T(2,128)(2,1)} %param.6), kind=kLoop, calls=%fused_computation.38 | loop fusion | bytes 2211840 | tf_op jit(solution)/shard_map/slice | solution.py:61
  2.1 5.0 %collective-permute-start = (bf16[3,90,2,512]{3,2,1,0:T(2,128)(2,1)S(1)}, bf16[3,90,2,512]{3,2,1,0:T(2,128)(2,1)S(1)}, u32[]{:S(2)}, u32[]{:S(2)}) collective-permute-start(bf16[3,90,2,512]{3,2,1,0:T(2,128)(2,1)S(1)} %get-tuple-element.13), channel_id=1, source_target_pairs={{0,8},{8,16},{16,24},{24,32},{32,40},{40,48},{48,56},{56,64},{64,7... | collective-permute-start | bytes 1658888 | tf_op jit(solution)/shard_map/ppermute | solution.py:60
  7.1 1.9 %collective-permute-start.1 = (bf16[3,90,2,512]{3,2,1,0:T(2,128)(2,1)S(1)}, bf16[3,90,2,512]{3,2,1,0:T(2,128)(2,1)S(1)}, u32[]{:S(2)}, u32[]{:S(2)}) collective-permute-start(bf16[3,90,2,512]{3,2,1,0:T(2,128)(2,1)S(1)} %get-tuple-element.12), channel_id=1, source_target_pairs={{8,0},{16,8},{24,16},{32,24},{40,32},{48,40},{56,48},{64,56},{72,6... | collective-permute-start | bytes 1658888 | tf_op jit(solution)/shard_map/ppermute | solution.py:61
  9.1 0.6 %gather_fusion = s32[3,4,4,128]{3,2,1,0:T(4,128)S(1)} fusion(s32[32,4,4,128]{3,2,1,0:T(4,128)S(1)} %copy-done, s32[1024]{0:T(1024)S(1)} %pad_clamp_fusion), kind=kCustom, calls=%fused_computation | custom fusion | bytes 49164 | tf_op jit(solution)/shard_map/jit(_take)/gather | solution.py:22
  9.7 0.1 broadcast_select_fusion
  9.7 0.1 slice_reduce_fusion
  9.9 0.1 copy.10
  9.9 0.6 %gather_fusion.1 = s32[3,3]{1,0:T(4,128)S(1)} fusion(s32[32,3]{1,0:T(8,128)S(1)} %copy.10, s32[1024]{0:T(1024)S(1)} %pad_clamp_fusion), kind=kCustom, calls=%fused_computation.1 | custom fusion | bytes 84 | tf_op jit(solution)/shard_map/jit(_take)/gather | solution.py:23
  10.5 0.1 broadcast_select_fusion.1
  10.6 0.2 negate_reduce_fusion
  10.8 0.1 fusion.8
  10.9 0.1 and.97
  11.0 0.1 ge.53
  11.1 0.1 lt.86
  11.1 0.1 sub.51
  11.3 2.4 %fusion = f32[1024,512]{1,0:T(8,128)S(1)} fusion(s32[1536]{0:T(1024)S(1)} %eq.28, s32[1536]{0:T(1024)S(1)} %add_select_fusion), kind=kOutput, calls=%fused_computation.3 | convolution fusion | flops 1612972032 | bytes 2109440 | tf_op jit(solution)/shard_map/dot_general | solution.py:46
  13.7 5.1 %collective-permute-done = bf16[3,90,2,512]{3,2,1,0:T(2,128)(2,1)S(1)} collective-permute-done((bf16[3,90,2,512]{3,2,1,0:T(2,128)(2,1)S(1)}, bf16[3,90,2,512]{3,2,1,0:T(2,128)(2,1)S(1)}, u32[]{:S(2)}, u32[]{:S(2)}) %collective-permute-start) | collective-permute-done | bytes 552992 | tf_op jit(solution)/shard_map/ppermute | solution.py:60
  18.8 0.4 constant_dynamic-update-slice_fusion.2
  19.2 0.6 %constant_dynamic-update-slice_fusion.1 = bf16[10,90,2,512]{3,2,1,0:T(2,128)(2,1)S(1)} fusion(bf16[10,90,2,512]{3,2,1,0:T(2,128)(2,1)S(1)} %constant_dynamic-update-slice_fusion.2, bf16[4,90,2,512]{3,2,1,0:T(2,128)(2,1)S(1)} %copy-done.1), kind=kLoop, calls=%fused_computation.21 | loop fusion | bytes 1474560
  19.8 6.5 %collective-permute-done.1 = bf16[3,90,2,512]{3,2,1,0:T(2,128)(2,1)S(1)} collective-permute-done((bf16[3,90,2,512]{3,2,1,0:T(2,128)(2,1)S(1)}, bf16[3,90,2,512]{3,2,1,0:T(2,128)(2,1)S(1)}, u32[]{:S(2)}, u32[]{:S(2)}) %collective-permute-start.1) | collective-permute-done | bytes 552992 | tf_op jit(solution)/shard_map/ppermute | solution.py:61
  26.3 0.4 constant_dynamic-update-slice_fusion
  26.7 0.1 slice.55
  26.8 0.0 collective-permute-start.2
  26.9 1.8 %fusion.4.coupling_ref = f32[3,512]{1,0:T(4,128)} fusion(f32[1024,512]{1,0:T(8,128)S(1)} %fusion, f32[1024,3]{0,1:T(4,128)S(1)} %copy-done.2), kind=kOutput, calls=%fused_computation.10 | convolution fusion | flops 18877440 | bytes 2115584 | tf_op jit(solution)/shard_map/dot_general | solution.py:49
  28.7 3.7 %collective-permute-done.2 = bf16[10,6,2,512]{3,2,1,0:T(2,128)(2,1)S(1)} collective-permute-done((bf16[10,6,2,512]{3,2,1,0:T(2,128)(2,1)S(1)}, bf16[10,6,2,512]{3,2,1,0:T(2,128)(2,1)S(1)}, u32[]{:S(2)}, u32[]{:S(2)}) %collective-permute-start.2) | collective-permute-done | bytes 122912 | tf_op jit(solution)/shard_map/ppermute | solution.py:63
  32.3 2.5 %maximum_bitcast_fusion = bf16[96,10,2,512]{3,2,0,1:T(2,128)(2,1)S(1)} fusion(bf16[10,90,2,512]{3,2,1,0:T(2,128)(2,1)S(1)} %constant_dynamic-update-slice_fusion, bf16[10,6,2,512]{3,2,1,0:T(2,128)(2,1)S(1)} %collective-permute-done.2), kind=kLoop, calls=%fused_computation.6 | loop fusion | flops 983040 | bytes 3932160 | tf_op jit(solution)/shard_map/transpose | solution.py:120
  34.9 1.4 %copy.11 = bf16[96,10,2,512]{3,2,1,0:T(2,128)(2,1)S(1)} copy(bf16[96,10,2,512]{3,2,0,1:T(2,128)(2,1)S(1)} %maximum_bitcast_fusion) | data formatting | bytes 3932160 | tf_op jit(solution)/shard_map/transpose | solution.py:120
  36.2 0.5 %copy.20 = bf16[120,8,2,512]{3,1,2,0:T(8,128)(2,1)S(1)} copy(bf16[120,8,2,512]{3,2,1,0:T(2,128)(2,1)S(1)} %bitcast.30) | data formatting | bytes 3932160
  36.8 1.5 %pad.4.rows_ref = bf16[1024,1024]{1,0:T(8,128)(2,1)} pad(bf16[960,1024]{1,0:T(8,128)(2,1)S(1)} %bitcast.29, bf16[]{:T(256)} %constant.56.clone.1), padding=0_64x0_0 | pad | bytes 4063234 | tf_op jit(solution)/shard_map/jit(_pad)/pad | solution.py:121
  38.3 6.5 %shard_map.64 = bf16[768,512]{1,0:T(8,128)(2,1)} custom-call(f32[3,512]{1,0:T(4,128)} %fusion.4.coupling_ref, bf16[1024,1024]{1,0:T(8,128)(2,1)} %pad.4.rows_ref, bf16[1536,512]{1,0:T(8,128)(2,1)} %weight_ref.1, bf16[512,512]{1,0:T(8,128)(2,1)} %mix_ref.1), custom_call_target="tpu_custom_call" | custom-call | flops 2516582400 | bytes 4718592 | tf_op jit(solution)/shard_map/pallas_call | solution.py:123
  44.8 1.9 %copy.12 = bf16[4,3,32,2,512]{4,3,2,1,0:T(2,128)(2,1)S(1)} copy(bf16[4,3,32,2,512]{4,2,0,1,3:T(8,128)(2,1)} %bitcast.32) | data formatting | bytes 1572864 | tf_op jit(solution)/shard_map/transpose | solution.py:137
  46.8 1.4 %slice.56 = bf16[4,90,2,512]{3,2,1,0:T(2,128)(2,1)} slice(bf16[4,96,2,512]{3,2,1,0:T(2,128)(2,1)S(1)} %bitcast.31), slice={[0:4], [0:90], [0:2], [0:512]} | slice | bytes 1474560 | tf_op jit(solution)/shard_map/slice | solution.py:138
  (21 shorter events, 0.2 us)
Async XLA Ops:
  0.0 9.1 %copy-start = (s32[32,4,4,128]{3,2,1,0:T(4,128)S(1)}, s32[32,4,4,128]{3,2,1,0:T(4,128)}, u32[]{:S(2)}) copy-start(s32[32,4,4,128]{3,2,1,0:T(4,128)} %param.8) | copy-start | bytes 786436
  0.0 9.8 %copy-start.3 = (s32[32,3]{0,1:T(4,128)S(1)}, s32[32,3]{0,1:T(4,128)}, u32[]{:S(2)}) copy-start(s32[32,3]{0,1:T(4,128)} %param.9) | copy-start | bytes 1156
  2.1 16.7 %collective-permute-start = (bf16[3,90,2,512]{3,2,1,0:T(2,128)(2,1)S(1)}, bf16[3,90,2,512]{3,2,1,0:T(2,128)(2,1)S(1)}, u32[]{:S(2)}, u32[]{:S(2)}) collective-permute-start(bf16[3,90,2,512]{3,2,1,0:T(2,128)(2,1)S(1)} %get-tuple-element.13), channel_id=1, source_target_pairs={{0,8},{8,16},{16,24},{24,32},{32,40},{40,48},{48,56},{56,64},{64,7... | collective-permute-start | bytes 1658888 | tf_op jit(solution)/shard_map/ppermute | solution.py:60
  7.1 19.2 %collective-permute-start.1 = (bf16[3,90,2,512]{3,2,1,0:T(2,128)(2,1)S(1)}, bf16[3,90,2,512]{3,2,1,0:T(2,128)(2,1)S(1)}, u32[]{:S(2)}, u32[]{:S(2)}) collective-permute-start(bf16[3,90,2,512]{3,2,1,0:T(2,128)(2,1)S(1)} %get-tuple-element.12), channel_id=1, source_target_pairs={{8,0},{16,8},{24,16},{32,24},{40,32},{48,40},{56,48},{64,56},{72,6... | collective-permute-start | bytes 1658888 | tf_op jit(solution)/shard_map/ppermute | solution.py:61
  11.3 8.0 %copy-start.1 = (bf16[4,90,2,512]{3,2,1,0:T(2,128)(2,1)S(1)}, bf16[4,90,2,512]{3,2,1,0:T(2,128)(2,1)}, u32[]{:S(2)}) copy-start(bf16[4,90,2,512]{3,2,1,0:T(2,128)(2,1)} %param.6) | copy-start | bytes 2211844
  13.7 13.2 %copy-start.2 = (f32[1024,3]{0,1:T(4,128)S(1)}, f32[1024,3]{0,1:T(4,128)}, u32[]{:S(2)}) copy-start(f32[1024,3]{0,1:T(4,128)} %param.7) | copy-start | bytes 36868
  26.8 5.5 %collective-permute-start.2 = (bf16[10,6,2,512]{3,2,1,0:T(2,128)(2,1)S(1)}, bf16[10,6,2,512]{3,2,1,0:T(2,128)(2,1)S(1)}, u32[]{:S(2)}, u32[]{:S(2)}) collective-permute-start(bf16[10,6,2,512]{3,2,1,0:T(2,128)(2,1)S(1)} %slice.55), channel_id=1, source_target_pairs={{0,1},{1,2},{2,3},{3,4},{4,5},{5,6},{6,7},{7,0},{8,9},{9,10},{10,1... | collective-permute-start | bytes 368648 | tf_op jit(solution)/shard_map/ppermute | solution.py:63

commit v6 on v4

--- a/solution.py
+++ b/solution.py
@@ -10,7 +10,7 @@
 SHIFTS = 7
 OVERHANG = 3
 LAT_DEV = 4
-ROW_PAD = 10
+PIECE_LANES = 32
 
 
 def band_coupling(entries, band_meta, coeffs, band_index, grid_rows):
@@ -36,7 +36,11 @@
     q = out_rows - band_start
     r = in_rows - (band_start - OVERHANG)
     usable = usable & (q >= 0) & (q < LAT_DEV) & (r >= 0) & (r < rows_in)
-    slot = jnp.where(usable, q * 128 + (SHIFTS - 1 - shifts) * ROW_PAD + r, -1).reshape(-1)
+    piece = (r >= OVERHANG).astype(jnp.int32) + (r >= OVERHANG + LAT_DEV).astype(jnp.int32)
+    width = jnp.where(piece == 1, LAT_DEV, OVERHANG)
+    local = r - jnp.where(piece == 0, 0, jnp.where(piece == 1, OVERHANG, OVERHANG + LAT_DEV))
+    lane = q * 128 + piece * PIECE_LANES + (SHIFTS - 1 - shifts) * width + local
+    slot = jnp.where(usable, lane, -1).reshape(-1)
     nslots = LAT_DEV * 128
     slot_hit = (slot[:, None] == jnp.arange(nslots, dtype=jnp.int32)[None, :]).astype(jnp.bfloat16)
     nfilters = coeffs.shape[0]
@@ -52,11 +56,15 @@
     return coupling
 
 
-def gather_rows(x):
+def lon_major(rows):
+    count, nlon, members, channels = rows.shape
+    return jnp.transpose(rows, (1, 0, 2, 3)).reshape(nlon * count, members * channels)
+
+
+def gather_pieces(x):
     nlat = lax.axis_size("lat")
     nlon = lax.axis_size("lon")
     lo = SHIFTS - 1
-    tail = x[:, x.shape[1] - lo :]
 
     def move(value, dlat, dlon):
         pairs = []
@@ -66,42 +74,59 @@
                     pairs.append((b * nlon + j, (b + dlat) * nlon + (j + dlon) % nlon))
         return lax.ppermute(value, ("lat", "lon"), pairs)
 
-    below = move(x[LAT_DEV - OVERHANG :], 1, 0)
-    above = move(x[:OVERHANG], -1, 0)
-    left = move(tail, 0, 1)
-    below_left = move(tail[LAT_DEV - OVERHANG :], 1, 1)
-    above_left = move(tail[:OVERHANG], -1, 1)
-    rows_below = jnp.concatenate([below_left, below], axis=1)
-    rows_mid = jnp.concatenate([left, x], axis=1)
-    rows_above = jnp.concatenate([above_left, above], axis=1)
-    return jnp.concatenate([rows_below, rows_mid, rows_above], axis=0)
+    own = lon_major(x)
+    send_up = lon_major(x[LAT_DEV - OVERHANG :])
+    send_down = lon_major(x[:OVERHANG])
+    ntail = lo * OVERHANG
+    below = move(send_up, 1, 0)
+    above = move(send_down, -1, 0)
+    left = move(own[own.shape[0] - lo * LAT_DEV :], 0, 1)
+    below_left = move(send_up[send_up.shape[0] - ntail :], 1, 1)
+    above_left = move(send_down[send_down.shape[0] - ntail :], -1, 1)
+    return (
+        jnp.concatenate([below_left, below], axis=0),
+        jnp.concatenate([left, own], axis=0),
+        jnp.concatenate([above_left, above], axis=0),
+    )
 
 
 WINDOW = 32
 LON_PAD = 32
 TAPS = 128
-DEPTH = 384
+WIDTHS = (OVERHANG, LAT_DEV, OVERHANG)
+DEPTHS = (128, 256, 128)
 
 
-def conv_mix_kernel(coupling_ref, rows_ref, weight_ref, mix_ref, out_ref, toeplitz_ref):
-    for k in range(BASIS):
-        for q in range(LAT_DEV):
-            taps = coupling_ref[k : k + 1, q * TAPS : (q + 1) * TAPS]
-            wide = jnp.concatenate([taps, jnp.zeros((1, DEPTH - TAPS), jnp.float32)], axis=1)
-            for g in range(LON_PAD // 8):
-                block = jnp.broadcast_to(wide, (8, DEPTH))
-                if g:
-                    block = pltpu.roll(block, 8 * g * ROW_PAD, 1)
-                block = pltpu.roll(block, 0, 1, stride=ROW_PAD, stride_axis=0)
-                toeplitz_ref[pl.ds((k * LAT_DEV + q) * LON_PAD + 8 * g, 8), :] = block.astype(
-                    jnp.bfloat16
-                )
+def conv_mix_kernel(coupling_ref, below_ref, own_ref, above_ref, weight_ref, mix_ref, out_ref, *toeplitz_refs):
+    for p in range(3):
+        width, depth = WIDTHS[p], DEPTHS[p]
+        lane = lax.broadcasted_iota(jnp.int32, (1, TAPS), 1)
+        for k in range(BASIS):
+            for q in range(LAT_DEV):
+                taps = coupling_ref[k : k + 1, q * TAPS : (q + 1) * TAPS]
+                if p:
+                    taps = pltpu.roll(taps, TAPS - p * PIECE_LANES, 1)
+                taps = jnp.where(lane < SHIFTS * width, taps, 0.0)
+                if depth > TAPS:
+                    taps = jnp.concatenate([taps, jnp.zeros((1, depth - TAPS), jnp.float32)], axis=1)
+                for g in range(LON_PAD // 8):
+                    block = jnp.broadcast_to(taps, (8, depth))
+                    if g:
+                        block = pltpu.roll(block, 8 * g * width, 1)
+                    block = pltpu.roll(block, 0, 1, stride=width, stride_axis=0)
+                    toeplitz_refs[p][pl.ds((k * LAT_DEV + q) * LON_PAD + 8 * g, 8), :] = block.astype(
+                        jnp.bfloat16
+                    )
     nwin = out_ref.shape[0] // (2 * LAT_DEV * LON_PAD)
     span = LAT_DEV * LON_PAD
     pieces = [[[] for _ in range(2)] for _ in range(BASIS)]
+    row_refs = (below_ref, own_ref, above_ref)
     for j in range(nwin):
-        window = rows_ref[pl.ds(j * WINDOW * ROW_PAD, DEPTH), :]
-        conv = jnp.dot(toeplitz_ref[...], window, preferred_element_type=jnp.float32)
+        conv = None
+        for p in range(3):
+            window = row_refs[p][pl.ds(j * WINDOW * WIDTHS[p], DEPTHS[p]), :]
+            term = jnp.dot(toeplitz_refs[p][...], window, preferred_element_type=jnp.float32)
+            conv = term if conv is None else conv + term
         for k in range(BASIS):
             for m in range(2):
                 pieces[k][m].append(conv[k * span : (k + 1) * span, m * CHANNELS : (m + 1) * CHANNELS])
@@ -126,26 +151,26 @@
     nrows, nlon, members, channels = fields.shape
     coupling = band_coupling(entries, band_info, coeffs, band_index, grid_rows)
     coupling = coupling.astype(jnp.bfloat16).astype(jnp.float32)
-    rows = gather_rows(fields)
-    rows_in, ext = rows.shape[0], rows.shape[1]
     nwin = -(-nlon // WINDOW)
-    depth_rows = (nwin - 1) * WINDOW * ROW_PAD + DEPTH
-    rows = jnp.transpose(rows, (1, 0, 2, 3)).reshape(ext * rows_in, members * channels)
-    rows = jnp.pad(rows, ((0, depth_rows - ext * rows_in), (0, 0)))
+    pieces = []
+    for piece, width, depth in zip(gather_pieces(fields), WIDTHS, DEPTHS):
+        need = (nwin - 1) * WINDOW * width + depth
+        pieces.append(jnp.pad(piece, ((0, need - piece.shape[0]), (0, 0))))
     out_rows = members * nwin * LAT_DEV * LON_PAD
+    toeplitz_rows = BASIS * LAT_DEV * LON_PAD
     mixed = pl.pallas_call(
         conv_mix_kernel,
         out_shape=jax.ShapeDtypeStruct((out_rows, CHANNELS), jnp.bfloat16),
-        in_specs=[pl.BlockSpec(memory_space=pltpu.VMEM)] * 4,
+        in_specs=[pl.BlockSpec(memory_space=pltpu.VMEM)] * 6,
         out_specs=pl.BlockSpec(memory_space=pltpu.VMEM),
-        scratch_shapes=[pltpu.VMEM((BASIS * LAT_DEV * LON_PAD, DEPTH), jnp.bfloat16)],
+        scratch_shapes=[pltpu.VMEM((toeplitz_rows, depth), jnp.bfloat16) for depth in DEPTHS],
         cost_estimate=pl.CostEstimate(
-            flops=2 * BASIS * LAT_DEV * LON_PAD * DEPTH * 1024 * nwin
+            flops=2 * toeplitz_rows * sum(DEPTHS) * 1024 * nwin
             + 2 * out_rows * CHANNELS * CHANNELS * (BASIS + 1),
             transcendentals=out_rows * CHANNELS,
-            bytes_accessed=rows.size * 2 + (BASIS + 2) * CHANNELS * CHANNELS * 2,
+            bytes_accessed=sum(p.size for p in pieces) * 2 + (BASIS + 2) * CHANNELS * CHANNELS * 2,
         ),
-    )(coupling, rows, conv_weight, mix_weight)
+    )(coupling, *pieces, conv_weight, mix_weight)
     mixed = mixed.reshape(members, nwin, LAT_DEV, LON_PAD, CHANNELS)
     mixed = jnp.transpose(mixed, (2, 1, 3, 0, 4)).reshape(LAT_DEV, nwin * LON_PAD, members, CHANNELS)
     return mixed[:, :nlon]

time: 46.3 us -> 47.4 us (1.024)
  the two profiles are of different devices: /device:TPU:129 before, /device:TPU:102 now
where the time goes in v6:
time: 47.4 us; the launch traced here: 47.1 us
  starting transfers between devices  13.9 us (29%)
  local copies, waits for them, and re-layouts  9.71 us (20%)
  Pallas kernels  7.46 us (16%)
  waiting for transfers between devices  7.06 us (15%)
  other arithmetic  4.48 us (9%)
  matrix products  4.22 us (9%)
    ppermute x5, starting transfers between devices, move(): return lax.ppermute(value, ('lat', 'lon'), pairs)  13.9 us
    pallas_call x1, Pallas kernels, shards(): pl.pallas_call(conv_mix_kernel, out_shape=jax.ShapeDtypeStruct((out_rows,...  7.46 us
    ppermute x5, waiting for transfers between devices, move(): return lax.ppermute(value, ('lat', 'lon'), pairs)  7.06 us
    transpose x4, local copies, waits for them, and re-layouts, lon_major(): jnp.transpose(rows, (1, 0, 2, 3)).reshape(nlon * count, members * channels)  3.38 us
    dot_general x1, matrix products, band_coupling(): lax.dot_general(filter_hit, slot_hit, (((0,), (0,)), ((), ())), preferred...  2.42 us
    transpose x1, local copies, waits for them, and re-layouts, shards(): jnp.transpose(mixed, (2, 1, 3, 0, 4))  1.94 us
    concatenate x1, other arithmetic, gather_pieces(): jnp.concatenate([left, own], axis=0)  1.92 us
    dot_general x1, matrix products, band_coupling(): jnp.dot(coeffs.T, counts, precision=lax.Precision.HIGHEST, preferred_elem...  1.8 us
  transfers between devices with their start and end apart: 5, of which 1 were waited for; matrix products, arithmetic and copies ran while one was open for 24% of the time, Pallas kernels for 0%

profile of v6, /device:TPU:102, one launch (start us, length us, event | category | flops | bytes accessed | tf_op | source)
XLA Modules:
  0.0 47.1 jit_solution(17118579351842848218)
XLA Ops:
  0.0 2.1 %slice_bitcast_fusion = (bf16[90,3,2,512]{3,2,0,1:T(2,128)(2,1)S(1)}, bf16[90,3,2,512]{3,2,0,1:T(2,128)(2,1)S(1)}) fusion(bf16[4,90,2,512]{3,2,1,0:T(2,128)(2,1)} %param.6), kind=kLoop, calls=%fused_computation.21 | loop fusion | bytes 2211840 | tf_op jit(solution)/shard_map/transpose | solution.py:61
  2.1 0.4 copy.17
  2.5 0.4 pad.31
  2.9 0.1 copy.28
  3.0 5.1 %collective-permute-start.1 = (bf16[270,1024]{1,0:T(8,128)(2,1)S(1)}, bf16[270,1024]{1,0:T(8,128)(2,1)S(1)}, u32[]{:S(2)}, u32[]{:S(2)}) collective-permute-start(bf16[270,1024]{1,0:T(8,128)(2,1)S(1)} %bitcast.61), channel_id=1, source_target_pairs={{0,8},{1,9},{2,10},{3,11},{4,12},{5,13},{6,14},{7,15},{8,16},{9,17... | collective-permute-start | bytes 1658888 | tf_op jit(solution)/shard_map/ppermute | solution.py:75
  8.3 2.6 %collective-permute-start = (bf16[18,1024]{1,0:T(8,128)(2,1)S(1)}, bf16[18,1024]{1,0:T(8,128)(2,1)S(1)}, u32[]{:S(2)}, u32[]{:S(2)}) collective-permute-start(bf16[18,1024]{1,0:T(8,128)(2,1)S(1)} %bitcast.68), channel_id=1, source_target_pairs={{0,9},{1,10},{2,11},{3,12},{4,13},{5,14},{6,15},{7,8},{8,17},{9,18... | collective-permute-start | bytes 110600 | tf_op jit(solution)/shard_map/ppermute | solution.py:75
  10.8 0.4 copy.21
  11.2 0.4 pad.29
  11.7 0.1 copy.24
  11.7 2.4 %collective-permute-start.4 = (bf16[270,1024]{1,0:T(8,128)(2,1)S(1)}, bf16[270,1024]{1,0:T(8,128)(2,1)S(1)}, u32[]{:S(2)}, u32[]{:S(2)}) collective-permute-start(bf16[270,1024]{1,0:T(8,128)(2,1)S(1)} %bitcast.62), channel_id=1, source_target_pairs={{8,0},{9,1},{10,2},{11,3},{12,4},{13,5},{14,6},{15,7},{16,8},{17,9... | collective-permute-start | bytes 1658888 | tf_op jit(solution)/shard_map/ppermute | solution.py:75
  14.3 3.7 %collective-permute-start.3 = (bf16[18,1024]{1,0:T(8,128)(2,1)S(1)}, bf16[18,1024]{1,0:T(8,128)(2,1)S(1)}, u32[]{:S(2)}, u32[]{:S(2)}) collective-permute-start(bf16[18,1024]{1,0:T(8,128)(2,1)S(1)} %bitcast.69), channel_id=1, source_target_pairs={{8,1},{9,2},{10,3},{11,4},{12,5},{13,6},{14,7},{15,0},{16,9},{17,1... | collective-permute-start | bytes 110600 | tf_op jit(solution)/shard_map/ppermute | solution.py:75
  18.1 0.1 collective-permute-start.2
  18.3 0.6 %gather_fusion = s32[3,4,4,128]{3,2,1,0:T(4,128)S(1)} fusion(s32[32,4,4,128]{3,2,1,0:T(4,128)S(1)} %copy-done, s32[1024]{0:T(1024)S(1)} %pad_clamp_fusion), kind=kCustom, calls=%fused_computation | custom fusion | bytes 49164 | tf_op jit(solution)/shard_map/jit(_take)/gather | solution.py:22
  18.9 0.1 broadcast_select_fusion
  19.0 0.1 slice_reduce_fusion
  19.1 0.1 copy.15
  19.2 0.6 %gather_fusion.1 = s32[3,3]{1,0:T(4,128)S(1)} fusion(s32[32,3]{1,0:T(8,128)S(1)} %copy.15, s32[1024]{0:T(1024)S(1)} %pad_clamp_fusion), kind=kCustom, calls=%fused_computation.1 | custom fusion | bytes 84 | tf_op jit(solution)/shard_map/jit(_take)/gather | solution.py:23
  19.7 0.1 broadcast_select_fusion.1
  19.8 0.2 negate_reduce_fusion
  20.0 0.1 fusion.18
  20.1 0.1 and.97
  20.5 2.4 %fusion = f32[1024,512]{1,0:T(8,128)S(1)} fusion(s32[1536]{0:T(1024)S(1)} %eq.43, s32[1536]{0:T(1024)S(1)} %add_select_fusion), kind=kOutput, calls=%fused_computation.3 | convolution fusion | flops 1612972032 | bytes 2109440 | tf_op jit(solution)/shard_map/dot_general | solution.py:50
  22.9 1.8 %fusion.10.coupling_ref = f32[3,512]{1,0:T(4,128)} fusion(f32[1024,512]{1,0:T(8,128)S(1)} %fusion, f32[1024,3]{0,1:T(4,128)S(1)} %copy-done.2), kind=kOutput, calls=%fused_computation.17 | convolution fusion | flops 18877440 | bytes 2115584 | tf_op jit(solution)/shard_map/dot_general | solution.py:53
  24.8 0.5 %copy.19 = bf16[90,4,2,512]{3,2,1,0:T(2,128)(2,1)S(1)} copy(bf16[90,4,2,512]{3,2,0,1:T(2,128)(2,1)S(1)} %bitcast.52) | data formatting | bytes 1474560 | tf_op jit(solution)/shard_map/transpose | solution.py:61
  25.3 0.1 copy.26
  25.4 1.9 %fusion.11.own_ref = bf16[512,1024]{1,0:T(8,128)(2,1)} fusion(bf16[360,1024]{1,0:T(8,128)(2,1)S(1)} %bitcast.54, bf16[24,1024]{1,0:T(8,128)(2,1)} %collective-permute-done.2), kind=kLoop, calls=%fused_computation.18 | loop fusion | flops 3670016 | bytes 1835008 | tf_op jit(solution)/shard_map/concatenate | solution.py:88
  27.3 1.0 %fusion.12.below_ref = bf16[320,1024]{1,0:T(8,128)(2,1)} fusion(bf16[270,1024]{1,0:T(8,128)(2,1)S(1)} %collective-permute-done.1, bf16[18,1024]{1,0:T(8,128)(2,1)S(1)} %collective-permute-done), kind=kLoop, calls=%fused_computation.19 | loop fusion | flops 2293760 | bytes 1245184 | tf_op jit(solution)/shard_map/concatenate | solution.py:87
  28.3 7.1 %collective-permute-done.3 = bf16[18,1024]{1,0:T(8,128)(2,1)S(1)} collective-permute-done((bf16[18,1024]{1,0:T(8,128)(2,1)S(1)}, bf16[18,1024]{1,0:T(8,128)(2,1)S(1)}, u32[]{:S(2)}, u32[]{:S(2)}) %collective-permute-start.3) | collective-permute-done | bytes 36896 | tf_op jit(solution)/shard_map/ppermute | solution.py:75
  35.4 1.0 %fusion.13.above_ref = bf16[320,1024]{1,0:T(8,128)(2,1)} fusion(bf16[270,1024]{1,0:T(8,128)(2,1)S(1)} %collective-permute-done.4, bf16[18,1024]{1,0:T(8,128)(2,1)S(1)} %collective-permute-done.3), kind=kLoop, calls=%fused_computation.20 | loop fusion | flops 2293760 | bytes 1245184 | tf_op jit(solution)/shard_map/concatenate | solution.py:89
  36.3 7.5 %shard_map.64 = bf16[768,512]{1,0:T(8,128)(2,1)} custom-call(f32[3,512]{1,0:T(4,128)} %fusion.10.coupling_ref, bf16[320,1024]{1,0:T(8,128)(2,1)} %fusion.12.below_ref, bf16[512,1024]{1,0:T(8,128)(2,1)} %fusion.11.own_ref, bf16[320,1024]{1,0:T(8,128)(2,1)} %fusion.13.above_ref, bf16[1536,512]{1,0:T(8,128)(2,1)} %weight_ref.1, bf16[512,512]{1,0:T(8,128)(2,1)} %mix_ref.1), custom_call_target="tpu_custom_call" | custom-call | flops 2818572288 | bytes 4980736 | tf_op jit(solution)/shard_map/pallas_call | solution.py:161
  43.8 1.9 %copy.22 = bf16[4,3,32,2,512]{4,3,2,1,0:T(2,128)(2,1)S(1)} copy(bf16[4,3,32,2,512]{4,2,0,1,3:T(8,128)(2,1)} %bitcast.60) | data formatting | bytes 1572864 | tf_op jit(solution)/shard_map/transpose | solution.py:175
  45.8 1.4 %slice.78 = bf16[4,90,2,512]{3,2,1,0:T(2,128)(2,1)} slice(bf16[4,96,2,512]{3,2,1,0:T(2,128)(2,1)S(1)} %bitcast.53), slice={[0:4], [0:90], [0:2], [0:512]} | slice | bytes 1474560 | tf_op jit(solution)/shard_map/slice | solution.py:176
  (39 shorter events, 0.7 us)
Async XLA Ops:
  0.0 18.3 %copy-start = (s32[32,4,4,128]{3,2,1,0:T(4,128)S(1)}, s32[32,4,4,128]{3,2,1,0:T(4,128)}, u32[]{:S(2)}) copy-start(s32[32,4,4,128]{3,2,1,0:T(4,128)} %param.8) | copy-start | bytes 786436
  3.0 15.0 %copy-start.1 = (bf16[4,90,2,512]{3,2,1,0:T(2,128)(2,1)S(1)}, bf16[4,90,2,512]{3,2,1,0:T(2,128)(2,1)}, u32[]{:S(2)}) copy-start(bf16[4,90,2,512]{3,2,1,0:T(2,128)(2,1)} %param.6) | copy-start | bytes 2211844
  3.0 24.3 %collective-permute-start.1 = (bf16[270,1024]{1,0:T(8,128)(2,1)S(1)}, bf16[270,1024]{1,0:T(8,128)(2,1)S(1)}, u32[]{:S(2)}, u32[]{:S(2)}) collective-permute-start(bf16[270,1024]{1,0:T(8,128)(2,1)S(1)} %bitcast.61), channel_id=1, source_target_pairs={{0,8},{1,9},{2,10},{3,11},{4,12},{5,13},{6,14},{7,15},{8,16},{9,17... | collective-permute-start | bytes 1658888 | tf_op jit(solution)/shard_map/ppermute | solution.py:75
  8.3 19.1 %collective-permute-start = (bf16[18,1024]{1,0:T(8,128)(2,1)S(1)}, bf16[18,1024]{1,0:T(8,128)(2,1)S(1)}, u32[]{:S(2)}, u32[]{:S(2)}) collective-permute-start(bf16[18,1024]{1,0:T(8,128)(2,1)S(1)} %bitcast.68), channel_id=1, source_target_pairs={{0,9},{1,10},{2,11},{3,12},{4,13},{5,14},{6,15},{7,8},{8,17},{9,18... | collective-permute-start | bytes 110600 | tf_op jit(solution)/shard_map/ppermute | solution.py:75
  10.8 8.3 %copy-start.3 = (s32[32,3]{0,1:T(4,128)S(1)}, s32[32,3]{0,1:T(4,128)}, u32[]{:S(2)}) copy-start(s32[32,3]{0,1:T(4,128)} %param.9) | copy-start | bytes 1156
  11.7 23.6 %collective-permute-start.4 = (bf16[270,1024]{1,0:T(8,128)(2,1)S(1)}, bf16[270,1024]{1,0:T(8,128)(2,1)S(1)}, u32[]{:S(2)}, u32[]{:S(2)}) collective-permute-start(bf16[270,1024]{1,0:T(8,128)(2,1)S(1)} %bitcast.62), channel_id=1, source_target_pairs={{8,0},{9,1},{10,2},{11,3},{12,4},{13,5},{14,6},{15,7},{16,8},{17,9... | collective-permute-start | bytes 1658888 | tf_op jit(solution)/shard_map/ppermute | solution.py:75
  14.3 21.0 %collective-permute-start.3 = (bf16[18,1024]{1,0:T(8,128)(2,1)S(1)}, bf16[18,1024]{1,0:T(8,128)(2,1)S(1)}, u32[]{:S(2)}, u32[]{:S(2)}) collective-permute-start(bf16[18,1024]{1,0:T(8,128)(2,1)S(1)} %bitcast.69), channel_id=1, source_target_pairs={{8,1},{9,2},{10,3},{11,4},{12,5},{13,6},{14,7},{15,0},{16,9},{17,1... | collective-permute-start | bytes 110600 | tf_op jit(solution)/shard_map/ppermute | solution.py:75
  18.1 7.3 %collective-permute-start.2 = (bf16[24,1024]{1,0:T(8,128)(2,1)S(1)}, bf16[24,1024]{1,0:T(8,128)(2,1)}, u32[]{:S(2)}, u32[]{:S(2)}) collective-permute-start(bf16[24,1024]{1,0:T(8,128)(2,1)S(1)} %bitcast.70), channel_id=1, source_target_pairs={{0,1},{1,2},{2,3},{3,4},{4,5},{5,6},{6,7},{7,0},{8,9},{9,10},{10,1... | collective-permute-start | bytes 147464 | tf_op jit(solution)/shard_map/ppermute | solution.py:75
  20.5 2.4 %copy-start.2 = (f32[1024,3]{0,1:T(4,128)S(1)}, f32[1024,3]{0,1:T(4,128)}, u32[]{:S(2)}) copy-start(f32[1024,3]{0,1:T(4,128)} %param.7) | copy-start | bytes 36868

commit v7 on v6

--- a/solution.py
+++ b/solution.py
@@ -65,29 +65,12 @@
     nlat = lax.axis_size("lat")
     nlon = lax.axis_size("lon")
     lo = SHIFTS - 1
-
-    def move(value, dlat, dlon):
-        pairs = []
-        for b in range(nlat):
-            if 0 <= b + dlat < nlat:
-                for j in range(nlon):
-                    pairs.append((b * nlon + j, (b + dlat) * nlon + (j + dlon) % nlon))
-        return lax.ppermute(value, ("lat", "lon"), pairs)
-
-    own = lon_major(x)
-    send_up = lon_major(x[LAT_DEV - OVERHANG :])
-    send_down = lon_major(x[:OVERHANG])
-    ntail = lo * OVERHANG
-    below = move(send_up, 1, 0)
-    above = move(send_down, -1, 0)
-    left = move(own[own.shape[0] - lo * LAT_DEV :], 0, 1)
-    below_left = move(send_up[send_up.shape[0] - ntail :], 1, 1)
-    above_left = move(send_down[send_down.shape[0] - ntail :], -1, 1)
-    return (
-        jnp.concatenate([below_left, below], axis=0),
-        jnp.concatenate([left, own], axis=0),
-        jnp.concatenate([above_left, above], axis=0),
-    )
+    left = lax.ppermute(x[:, x.shape[1] - lo :], "lon", [(j, (j + 1) % nlon) for j in range(nlon)])
+    ext = jnp.concatenate([left, x], axis=1)
+    down = [(b, b + 1) for b in range(nlat - 1)]
+    below = lax.ppermute(ext[LAT_DEV - OVERHANG :], "lat", down)
+    above = lax.ppermute(ext[:OVERHANG], "lat", [(t, s) for s, t in down])
+    return lon_major(below), lon_major(ext), lon_major(above)
 
 
 WINDOW = 32

time: 47.4 us -> 45.7 us (0.964)
  starting transfers between devices: 13.9 us -> 6.89 us
  waiting for transfers between devices: 7.06 us -> 12.5 us
  other arithmetic: 4.48 us -> 0.59 us
  local copies, waits for them, and re-layouts: 9.71 us -> 13.5 us
    ppermute x5 -> x3, starting transfers between devices: 13.9 us -> 6.89 us  [the longest x1 4.95 us: gather_pieces(): below = lax.ppermute(ext[LAT_DEV - OVERHANG:], 'lat', down)]
    ppermute x5 -> x3, waiting for transfers between devices: 7.06 us -> 12.5 us  [the longest x1 6.05 us: gather_pieces(): above = lax.ppermute(ext[:OVERHANG], 'lat', [(t, s) for s, t in down])]
    concatenate x3 -> x0, other arithmetic: 3.9 us -> none  [the longest x1 1.92 us: gather_pieces(): jnp.concatenate([left, own], axis=0)]
    pad x0 -> x3, local copies, waits for them, and re-layouts: none -> 2.94 us  [shards(): pieces.append(jnp.pad(piece, ((0, need - piece.shape[0]), (0, 0))))]
    transpose x4 -> x3, local copies, waits for them, and re-layouts: 3.38 us -> 1.35 us  [lon_major(): jnp.transpose(rows, (1, 0, 2, 3)).reshape(nlon * count, members * channels)]
    concatenate x0 -> x1, local copies, waits for them, and re-layouts: none -> 1.69 us  [gather_pieces(): ext = jnp.concatenate([left, x], axis=1)]
    slice x6 -> x2, local copies, waits for them, and re-layouts: 0.18 us -> 1.55 us  [the longest x1 0.88 us: gather_pieces(): x[:, x.shape[1] - lo:]]
    unnamed x19 -> x9, local copies, waits for them, and re-layouts: 1.33 us -> 1.1 us
  transfers between devices with their start and end apart: 5 -> 3, of which waited for: 1 -> 3; matrix products, arithmetic and copies ran while one was open for 24% -> 23% of each run, Pallas kernels for 0% -> 0%
where the time goes in v7:
time: 45.7 us; the launch traced here: 45.3 us
  local copies, waits for them, and re-layouts  13.5 us (30%)
  waiting for transfers between devices  12.5 us (27%)
  Pallas kernels  7.46 us (16%)
  starting transfers between devices  6.89 us (15%)
  matrix products  4.22 us (9%)
  other arithmetic  0.59 us (1%)
    pallas_call x1, Pallas kernels, shards(): pl.pallas_call(conv_mix_kernel, out_shape=jax.ShapeDtypeStruct((out_rows,...  7.46 us
    ppermute x1, waiting for transfers between devices, gather_pieces(): above = lax.ppermute(ext[:OVERHANG], 'lat', [(t, s) for s, t in down])  6.05 us
    ppermute x1, starting transfers between devices, gather_pieces(): below = lax.ppermute(ext[LAT_DEV - OVERHANG:], 'lat', down)  4.95 us
    ppermute x1, waiting for transfers between devices, gather_pieces(): below = lax.ppermute(ext[LAT_DEV - OVERHANG:], 'lat', down)  4.65 us
    pad x3, local copies, waits for them, and re-layouts, shards(): pieces.append(jnp.pad(piece, ((0, need - piece.shape[0]), (0, 0))))  2.94 us
    dot_general x1, matrix products, band_coupling(): lax.dot_general(filter_hit, slot_hit, (((0,), (0,)), ((), ())), preferred...  2.42 us
    transpose x1, local copies, waits for them, and re-layouts, shards(): jnp.transpose(mixed, (2, 1, 3, 0, 4))  1.94 us
    ppermute x1, starting transfers between devices, gather_pieces(): above = lax.ppermute(ext[:OVERHANG], 'lat', [(t, s) for s, t in down])  1.92 us
  transfers between devices with their start and end apart: 3, of which 3 were waited for; matrix products, arithmetic and copies ran while one was open for 23% of the time, Pallas kernels for 0%

profile of v7, /device:TPU:102, one launch (start us, length us, event | category | flops | bytes accessed | tf_op | source)
XLA Modules:
  0.0 45.3 jit_solution(4202767105504781455)
XLA Ops:
  0.0 0.9 %slice.43 = bf16[4,6,2,512]{3,2,1,0:T(2,128)(2,1)S(1)} slice(bf16[4,90,2,512]{3,2,1,0:T(2,128)(2,1)} %param.6), slice={[0:4], [84:90], [0:2], [0:512]} | slice | bytes 98304 | tf_op jit(solution)/shard_map/slice | solution.py:68
  1.0 0.6 %gather_fusion = s32[3,4,4,128]{3,2,1,0:T(4,128)S(1)} fusion(s32[32,4,4,128]{3,2,1,0:T(4,128)S(1)} %copy-done, s32[1024]{0:T(1024)S(1)} %pad_clamp_fusion), kind=kCustom, calls=%fused_computation | custom fusion | bytes 49164 | tf_op jit(solution)/shard_map/jit(_take)/gather | solution.py:22
  1.6 0.1 broadcast_select_fusion
  1.6 0.1 slice_reduce_fusion
  1.8 0.8 %copy.12 = s32[32,3]{1,0:T(8,128)S(1)} copy(s32[32,3]{0,1:T(4,128)} %param.9) | data formatting | bytes 768 | tf_op args[3]
  2.5 0.6 %gather_fusion.1 = s32[3,3]{1,0:T(4,128)S(1)} fusion(s32[32,3]{1,0:T(8,128)S(1)} %copy.12, s32[1024]{0:T(1024)S(1)} %pad_clamp_fusion), kind=kCustom, calls=%fused_computation.1 | custom fusion | bytes 84 | tf_op jit(solution)/shard_map/jit(_take)/gather | solution.py:23
  3.1 0.1 broadcast_select_fusion.1
  3.2 0.2 negate_reduce_fusion
  3.4 0.1 fusion.9
  3.4 0.1 and.97
  3.5 0.1 ge.73
  3.8 1.8 %collective-permute-done = bf16[4,6,2,512]{3,2,1,0:T(2,128)(2,1)S(1)} collective-permute-done((bf16[4,6,2,512]{3,2,1,0:T(2,128)(2,1)S(1)}, bf16[4,6,2,512]{3,2,1,0:T(2,128)(2,1)S(1)}, u32[]{:S(2)}, u32[]{:S(2)}) %collective-permute-start) | collective-permute-done | bytes 49184 | tf_op jit(solution)/shard_map/ppermute | solution.py:68
  5.7 1.7 %constant_dynamic-update-slice_fusion = bf16[4,96,2,512]{3,2,1,0:T(2,128)(2,1)S(1)} fusion(bf16[4,96,2,512]{3,2,1,0:T(2,128)(2,1)S(1)} %constant_dynamic-update-slice_fusion.1, bf16[4,90,2,512]{3,2,1,0:T(2,128)(2,1)} %param.6), kind=kLoop, calls=%fused_computation.22 | loop fusion | bytes 1474560 | tf_op jit(solution)/shard_map/concatenate | solution.py:69
  7.3 0.7 %fusion.12 = (bf16[3,96,2,512]{3,2,1,0:T(2,128)(2,1)S(1)}, bf16[3,96,2,512]{3,2,1,0:T(2,128)(2,1)S(1)}) fusion(bf16[4,96,2,512]{3,2,1,0:T(2,128)(2,1)S(1)} %constant_dynamic-update-slice_fusion), kind=kLoop, calls=%fused_computation.38 | loop fusion | bytes 2359296 | tf_op jit(solution)/shard_map/slice | solution.py:72
  8.0 5.0 %collective-permute-start.1 = (bf16[3,96,2,512]{3,2,1,0:T(2,128)(2,1)S(1)}, bf16[3,96,2,512]{3,2,1,0:T(2,128)(2,1)S(1)}, u32[]{:S(2)}, u32[]{:S(2)}) collective-permute-start(bf16[3,96,2,512]{3,2,1,0:T(2,128)(2,1)S(1)} %get-tuple-element.13), channel_id=1, source_target_pairs={{0,8},{8,16},{16,24},{24,32},{32,40},{40,48},{48,56},{56,64},{64,7... | collective-permute-start | bytes 1769480 | tf_op jit(solution)/shard_map/ppermute | solution.py:71
  13.0 1.9 %collective-permute-start.2 = (bf16[3,96,2,512]{3,2,1,0:T(2,128)(2,1)S(1)}, bf16[3,96,2,512]{3,2,1,0:T(2,128)(2,1)S(1)}, u32[]{:S(2)}, u32[]{:S(2)}) collective-permute-start(bf16[3,96,2,512]{3,2,1,0:T(2,128)(2,1)S(1)} %get-tuple-element.12), channel_id=1, source_target_pairs={{8,0},{16,8},{24,16},{32,24},{40,32},{48,40},{56,48},{64,56},{72,6... | collective-permute-start | bytes 1769480 | tf_op jit(solution)/shard_map/ppermute | solution.py:72
  14.9 2.4 %fusion = f32[1024,512]{1,0:T(8,128)S(1)} fusion(s32[1536]{0:T(1024)S(1)} %eq.43, s32[1536]{0:T(1024)S(1)} %add_select_fusion), kind=kOutput, calls=%fused_computation.3 | convolution fusion | flops 1612972032 | bytes 2109440 | tf_op jit(solution)/shard_map/dot_general | solution.py:50
  17.4 1.8 %fusion.4.coupling_ref = f32[3,512]{1,0:T(4,128)} fusion(f32[1024,512]{1,0:T(8,128)S(1)} %fusion, f32[1024,3]{0,1:T(4,128)S(1)} %copy-done.1), kind=kOutput, calls=%fused_computation.9 | convolution fusion | flops 18877440 | bytes 2115584 | tf_op jit(solution)/shard_map/dot_general | solution.py:53
  19.2 0.5 %copy.14 = bf16[96,4,2,512]{3,2,1,0:T(2,128)(2,1)S(1)} copy(bf16[96,4,2,512]{3,2,0,1:T(2,128)(2,1)S(1)} %bitcast.36) | data formatting | bytes 1572864 | tf_op jit(solution)/shard_map/transpose | solution.py:61
  19.7 0.1 copy.25
  19.8 1.1 %pad.12.own_ref = bf16[512,1024]{1,0:T(8,128)(2,1)} pad(bf16[384,1024]{1,0:T(8,128)(2,1)S(1)} %bitcast.38, bf16[]{:T(256)} %constant.37.clone.1), padding=0_128x0_0 | pad | bytes 1835010 | tf_op jit(solution)/shard_map/jit(_pad)/pad | solution.py:141
  21.0 4.7 %collective-permute-done.1 = bf16[3,96,2,512]{3,2,1,0:T(2,128)(2,1)S(1)} collective-permute-done((bf16[3,96,2,512]{3,2,1,0:T(2,128)(2,1)S(1)}, bf16[3,96,2,512]{3,2,1,0:T(2,128)(2,1)S(1)}, u32[]{:S(2)}, u32[]{:S(2)}) %collective-permute-start.1) | collective-permute-done | bytes 589856 | tf_op jit(solution)/shard_map/ppermute | solution.py:71
  25.6 0.4 copy.13
  26.0 0.1 copy.24
  26.1 0.9 %pad.11.below_ref = bf16[320,1024]{1,0:T(8,128)(2,1)} pad(bf16[288,1024]{1,0:T(8,128)(2,1)S(1)} %bitcast.42, bf16[]{:T(256)} %constant.37.clone.1), padding=0_32x0_0 | pad | bytes 1245186 | tf_op jit(solution)/shard_map/jit(_pad)/pad | solution.py:141
  27.0 6.0 %collective-permute-done.2 = bf16[3,96,2,512]{3,2,1,0:T(2,128)(2,1)S(1)} collective-permute-done((bf16[3,96,2,512]{3,2,1,0:T(2,128)(2,1)S(1)}, bf16[3,96,2,512]{3,2,1,0:T(2,128)(2,1)S(1)}, u32[]{:S(2)}, u32[]{:S(2)}) %collective-permute-start.2) | collective-permute-done | bytes 589856 | tf_op jit(solution)/shard_map/ppermute | solution.py:72
  33.1 0.4 copy.15
  33.5 0.1 copy.26
  33.6 0.9 %pad.13.above_ref = bf16[320,1024]{1,0:T(8,128)(2,1)} pad(bf16[288,1024]{1,0:T(8,128)(2,1)S(1)} %bitcast.40, bf16[]{:T(256)} %constant.37.clone.1), padding=0_32x0_0 | pad | bytes 1245186 | tf_op jit(solution)/shard_map/jit(_pad)/pad | solution.py:141
  34.5 7.5 %shard_map.64 = bf16[768,512]{1,0:T(8,128)(2,1)} custom-call(f32[3,512]{1,0:T(4,128)} %fusion.4.coupling_ref, bf16[320,1024]{1,0:T(8,128)(2,1)} %pad.11.below_ref, bf16[512,1024]{1,0:T(8,128)(2,1)} %pad.12.own_ref, bf16[320,1024]{1,0:T(8,128)(2,1)} %pad.13.above_ref, bf16[1536,512]{1,0:T(8,128)(2,1)} %weight_ref.1, bf16[512,512]{1,0:T(8,128)(2,1)} %mix_ref.1), custom_call_target="tpu_custom_call" | custom-call | flops 2818572288 | bytes 4980736 | tf_op jit(solution)/shard_map/pallas_call | solution.py:144
  42.0 1.9 %copy.16 = bf16[4,3,32,2,512]{4,3,2,1,0:T(2,128)(2,1)S(1)} copy(bf16[4,3,32,2,512]{4,2,0,1,3:T(8,128)(2,1)} %bitcast.44) | data formatting | bytes 1572864 | tf_op jit(solution)/shard_map/transpose | solution.py:158
  43.9 1.4 %slice.57 = bf16[4,90,2,512]{3,2,1,0:T(2,128)(2,1)} slice(bf16[4,96,2,512]{3,2,1,0:T(2,128)(2,1)S(1)} %bitcast.39), slice={[0:4], [0:90], [0:2], [0:512]} | slice | bytes 1474560 | tf_op jit(solution)/shard_map/slice | solution.py:159
  (21 shorter events, 0.4 us)
Async XLA Ops:
  0.0 1.0 %copy-start = (s32[32,4,4,128]{3,2,1,0:T(4,128)S(1)}, s32[32,4,4,128]{3,2,1,0:T(4,128)}, u32[]{:S(2)}) copy-start(s32[32,4,4,128]{3,2,1,0:T(4,128)} %param.8) | copy-start | bytes 786436
  0.9 4.7 %collective-permute-start = (bf16[4,6,2,512]{3,2,1,0:T(2,128)(2,1)S(1)}, bf16[4,6,2,512]{3,2,1,0:T(2,128)(2,1)S(1)}, u32[]{:S(2)}, u32[]{:S(2)}) collective-permute-start(bf16[4,6,2,512]{3,2,1,0:T(2,128)(2,1)S(1)} %slice.43), channel_id=1, source_target_pairs={{0,1},{1,2},{2,3},{3,4},{4,5},{5,6},{6,7},{7,0},{8,9},{9,10},{10,1... | collective-permute-start | bytes 147464 | tf_op jit(solution)/shard_map/ppermute | solution.py:68
  8.0 17.6 %collective-permute-start.1 = (bf16[3,96,2,512]{3,2,1,0:T(2,128)(2,1)S(1)}, bf16[3,96,2,512]{3,2,1,0:T(2,128)(2,1)S(1)}, u32[]{:S(2)}, u32[]{:S(2)}) collective-permute-start(bf16[3,96,2,512]{3,2,1,0:T(2,128)(2,1)S(1)} %get-tuple-element.13), channel_id=1, source_target_pairs={{0,8},{8,16},{16,24},{24,32},{32,40},{40,48},{48,56},{56,64},{64,7... | collective-permute-start | bytes 1769480 | tf_op jit(solution)/shard_map/ppermute | solution.py:71
  13.0 4.4 %copy-start.1 = (f32[1024,3]{0,1:T(4,128)S(1)}, f32[1024,3]{0,1:T(4,128)}, u32[]{:S(2)}) copy-start(f32[1024,3]{0,1:T(4,128)} %param.7) | copy-start | bytes 36868
  13.0 20.1 %collective-permute-start.2 = (bf16[3,96,2,512]{3,2,1,0:T(2,128)(2,1)S(1)}, bf16[3,96,2,512]{3,2,1,0:T(2,128)(2,1)S(1)}, u32[]{:S(2)}, u32[]{:S(2)}) collective-permute-start(bf16[3,96,2,512]{3,2,1,0:T(2,128)(2,1)S(1)} %get-tuple-element.12), channel_id=1, source_target_pairs={{8,0},{16,8},{24,16},{32,24},{40,32},{48,40},{56,48},{64,56},{72,6... | collective-permute-start | bytes 1769480 | tf_op jit(solution)/shard_map/ppermute | solution.py:72

commit v8 on v6

--- a/solution.py
+++ b/solution.py
@@ -65,6 +65,7 @@
     nlat = lax.axis_size("lat")
     nlon = lax.axis_size("lon")
     lo = SHIFTS - 1
+    tail = x[:, x.shape[1] - lo :]
 
     def move(value, dlat, dlon):
         pairs = []
@@ -74,19 +75,15 @@
                     pairs.append((b * nlon + j, (b + dlat) * nlon + (j + dlon) % nlon))
         return lax.ppermute(value, ("lat", "lon"), pairs)
 
-    own = lon_major(x)
-    send_up = lon_major(x[LAT_DEV - OVERHANG :])
-    send_down = lon_major(x[:OVERHANG])
-    ntail = lo * OVERHANG
-    below = move(send_up, 1, 0)
-    above = move(send_down, -1, 0)
-    left = move(own[own.shape[0] - lo * LAT_DEV :], 0, 1)
-    below_left = move(send_up[send_up.shape[0] - ntail :], 1, 1)
-    above_left = move(send_down[send_down.shape[0] - ntail :], -1, 1)
+    below = move(x[LAT_DEV - OVERHANG :], 1, 0)
+    above = move(x[:OVERHANG], -1, 0)
+    below_left = move(tail[LAT_DEV - OVERHANG :], 1, 1)
+    above_left = move(tail[:OVERHANG], -1, 1)
+    left = move(tail, 0, 1)
     return (
-        jnp.concatenate([below_left, below], axis=0),
-        jnp.concatenate([left, own], axis=0),
-        jnp.concatenate([above_left, above], axis=0),
+        lon_major(jnp.concatenate([below_left, below], axis=1)),
+        lon_major(jnp.concatenate([left, x], axis=1)),
+        lon_major(jnp.concatenate([above_left, above], axis=1)),
     )
 
 

time: 47.4 us -> 46.2 us (0.975)
  local copies, waits for them, and re-layouts: 9.71 us -> 11.7 us
  waiting for transfers between devices: 7.06 us -> 5.63 us
  other arithmetic: 4.48 us -> 3.12 us
    concatenate x3 -> x0, other arithmetic: 3.9 us -> none  [the longest x1 1.92 us: gather_pieces(): jnp.concatenate([left, own], axis=0)]
    pad x0 -> x3, local copies, waits for them, and re-layouts: none -> 2.94 us  [shards(): pieces.append(jnp.pad(piece, ((0, need - piece.shape[0]), (0, 0))))]
    transpose x0 -> x3, other arithmetic: none -> 2.54 us  [lon_major(): jnp.transpose(rows, (1, 0, 2, 3)).reshape(nlon * count, members * channels)]
    slice x6 -> x3, local copies, waits for them, and re-layouts: 0.18 us -> 2.21 us  [the longest x1 2.12 us: gather_pieces(): above = move(x[:OVERHANG], -1, 0)]
    transpose x4 -> x3, local copies, waits for them, and re-layouts: 3.38 us -> 1.36 us  [lon_major(): jnp.transpose(rows, (1, 0, 2, 3)).reshape(nlon * count, members * channels)]
    ppermute x5, waiting for transfers between devices: 7.06 us -> 5.63 us  [move(): return lax.ppermute(value, ('lat', 'lon'), pairs)]
    unnamed x19 -> x12, local copies, waits for them, and re-layouts: 1.33 us -> 0.4 us
  transfers between devices with their start and end apart: 5 -> 5, of which waited for: 1 -> 1; matrix products, arithmetic and copies ran while one was open for 24% -> 25% of each run, Pallas kernels for 0% -> 0%
where the time goes in v8:
time: 46.2 us; the launch traced here: 46 us
  starting transfers between devices  13.6 us (29%)
  local copies, waits for them, and re-layouts  11.7 us (25%)
  Pallas kernels  7.47 us (16%)
  waiting for transfers between devices  5.63 us (12%)
  matrix products  4.22 us (9%)
  other arithmetic  3.12 us (7%)
    ppermute x5, starting transfers between devices, move(): return lax.ppermute(value, ('lat', 'lon'), pairs)  13.6 us
    pallas_call x1, Pallas kernels, shards(): pl.pallas_call(conv_mix_kernel, out_shape=jax.ShapeDtypeStruct((out_rows,...  7.47 us
    ppermute x5, waiting for transfers between devices, move(): return lax.ppermute(value, ('lat', 'lon'), pairs)  5.63 us
    pad x3, local copies, waits for them, and re-layouts, shards(): pieces.append(jnp.pad(piece, ((0, need - piece.shape[0]), (0, 0))))  2.94 us
    transpose x3, other arithmetic, lon_major(): jnp.transpose(rows, (1, 0, 2, 3)).reshape(nlon * count, members * channels)  2.54 us
    dot_general x1, matrix products, band_coupling(): lax.dot_general(filter_hit, slot_hit, (((0,), (0,)), ((), ())), preferred...  2.42 us
    slice x1, local copies, waits for them, and re-layouts, gather_pieces(): above = move(x[:OVERHANG], -1, 0)  2.12 us
    transpose x1, local copies, waits for them, and re-layouts, shards(): jnp.transpose(mixed, (2, 1, 3, 0, 4))  1.94 us
  transfers between devices with their start and end apart: 5, of which 1 were waited for; matrix products, arithmetic and copies ran while one was open for 25% of the time, Pallas kernels for 0%

profile of v8, /device:TPU:102, one launch (start us, length us, event | category | flops | bytes accessed | tf_op | source)
XLA Modules:
  0.0 46.0 jit_solution(8221959419131214654)
XLA Ops:
  0.0 2.1 %fusion.13 = (bf16[3,90,2,512]{3,2,1,0:T(2,128)(2,1)S(1)}, bf16[3,90,2,512]{3,2,1,0:T(2,128)(2,1)S(1)}) fusion(bf16[4,90,2,512]{3,2,1,0:T(2,128)(2,1)} %param.6), kind=kLoop, calls=%fused_computation.40 | loop fusion | bytes 2211840 | tf_op jit(solution)/shard_map/slice | solution.py:79
  2.1 5.0 %collective-permute-start.1 = (bf16[3,90,2,512]{3,2,1,0:T(2,128)(2,1)S(1)}, bf16[3,90,2,512]{3,2,1,0:T(2,128)(2,1)S(1)}, u32[]{:S(2)}, u32[]{:S(2)}) collective-permute-start(bf16[3,90,2,512]{3,2,1,0:T(2,128)(2,1)S(1)} %get-tuple-element.15), channel_id=1, source_target_pairs={{0,8},{1,9},{2,10},{3,11},{4,12},{5,13},{6,14},{7,15},{8,16},{9,17... | collective-permute-start | bytes 1658888 | tf_op jit(solution)/shard_map/ppermute | solution.py:76
  7.2 2.6 %collective-permute-start = (bf16[3,6,2,512]{3,2,1,0:T(2,128)(2,1)S(1)}, bf16[3,6,2,512]{3,2,1,0:T(2,128)(2,1)S(1)}, u32[]{:S(2)}, u32[]{:S(2)}) collective-permute-start(bf16[3,6,2,512]{3,2,1,0:T(2,128)(2,1)S(1)} %get-tuple-element.13), channel_id=1, source_target_pairs={{0,9},{1,10},{2,11},{3,12},{4,13},{5,14},{6,15},{7,8},{8,17},{9,18... | collective-permute-start | bytes 110600 | tf_op jit(solution)/shard_map/ppermute | solution.py:76
  9.7 2.4 %collective-permute-start.4 = (bf16[3,90,2,512]{3,2,1,0:T(2,128)(2,1)S(1)}, bf16[3,90,2,512]{3,2,1,0:T(2,128)(2,1)S(1)}, u32[]{:S(2)}, u32[]{:S(2)}) collective-permute-start(bf16[3,90,2,512]{3,2,1,0:T(2,128)(2,1)S(1)} %get-tuple-element.14), channel_id=1, source_target_pairs={{8,0},{9,1},{10,2},{11,3},{12,4},{13,5},{14,6},{15,7},{16,8},{17,9... | collective-permute-start | bytes 1658888 | tf_op jit(solution)/shard_map/ppermute | solution.py:76
  12.2 3.5 %collective-permute-start.3 = (bf16[3,6,2,512]{3,2,1,0:T(2,128)(2,1)S(1)}, bf16[3,6,2,512]{3,2,1,0:T(2,128)(2,1)S(1)}, u32[]{:S(2)}, u32[]{:S(2)}) collective-permute-start(bf16[3,6,2,512]{3,2,1,0:T(2,128)(2,1)S(1)} %get-tuple-element.12), channel_id=1, source_target_pairs={{8,1},{9,2},{10,3},{11,4},{12,5},{13,6},{14,7},{15,0},{16,9},{17,1... | collective-permute-start | bytes 110600 | tf_op jit(solution)/shard_map/ppermute | solution.py:76
  15.7 0.1 collective-permute-start.2
  15.9 0.6 %gather_fusion = s32[3,4,4,128]{3,2,1,0:T(4,128)S(1)} fusion(s32[32,4,4,128]{3,2,1,0:T(4,128)S(1)} %copy-done, s32[1024]{0:T(1024)S(1)} %pad_clamp_fusion), kind=kCustom, calls=%fused_computation | custom fusion | bytes 49164 | tf_op jit(solution)/shard_map/jit(_take)/gather | solution.py:22
  16.5 0.1 broadcast_select_fusion
  16.6 0.1 slice_reduce_fusion
  16.7 0.1 copy.12
  16.8 0.6 %gather_fusion.1 = s32[3,3]{1,0:T(4,128)S(1)} fusion(s32[32,3]{1,0:T(8,128)S(1)} %copy.12, s32[1024]{0:T(1024)S(1)} %pad_clamp_fusion), kind=kCustom, calls=%fused_computation.1 | custom fusion | bytes 84 | tf_op jit(solution)/shard_map/jit(_take)/gather | solution.py:23
  17.4 0.2 negate_reduce_fusion
  17.6 0.1 fusion.9
  17.7 0.1 and.97
  18.1 2.4 %fusion = f32[1024,512]{1,0:T(8,128)S(1)} fusion(s32[1536]{0:T(1024)S(1)} %eq.43, s32[1536]{0:T(1024)S(1)} %add_select_fusion), kind=kOutput, calls=%fused_computation.3 | convolution fusion | flops 1612972032 | bytes 2109440 | tf_op jit(solution)/shard_map/dot_general | solution.py:50
  20.5 1.8 %fusion.4.coupling_ref = f32[3,512]{1,0:T(4,128)} fusion(f32[1024,512]{1,0:T(8,128)S(1)} %fusion, f32[1024,3]{0,1:T(4,128)S(1)} %copy-done.2), kind=kOutput, calls=%fused_computation.9 | convolution fusion | flops 18877440 | bytes 2115584 | tf_op jit(solution)/shard_map/dot_general | solution.py:53
  22.3 1.0 %maximum_bitcast_fusion = bf16[96,4,2,512]{3,2,0,1:T(2,128)(2,1)S(1)} fusion(bf16[4,90,2,512]{3,2,1,0:T(2,128)(2,1)S(1)} %copy-done.1, bf16[4,6,2,512]{3,2,1,0:T(2,128)(2,1)S(1)} %collective-permute-done.2), kind=kLoop, calls=%fused_computation.10 | loop fusion | flops 393216 | bytes 1572864 | tf_op jit(solution)/shard_map/transpose | solution.py:61
  23.4 0.5 %copy.14 = bf16[96,4,2,512]{3,2,1,0:T(2,128)(2,1)S(1)} copy(bf16[96,4,2,512]{3,2,0,1:T(2,128)(2,1)S(1)} %maximum_bitcast_fusion) | data formatting | bytes 1572864 | tf_op jit(solution)/shard_map/transpose | solution.py:61
  23.9 0.1 copy.25
  24.1 1.1 %pad.12.own_ref = bf16[512,1024]{1,0:T(8,128)(2,1)} pad(bf16[384,1024]{1,0:T(8,128)(2,1)S(1)} %bitcast.40, bf16[]{:T(256)} %constant.37.clone.1), padding=0_128x0_0 | pad | bytes 1835010 | tf_op jit(solution)/shard_map/jit(_pad)/pad | solution.py:155
  25.2 0.8 %maximum_bitcast_fusion.1 = bf16[96,3,2,512]{3,2,0,1:T(2,128)(2,1)S(1)} fusion(bf16[3,90,2,512]{3,2,1,0:T(2,128)(2,1)S(1)} %collective-permute-done.1, bf16[3,6,2,512]{3,2,1,0:T(2,128)(2,1)S(1)} %collective-permute-done), kind=kLoop, calls=%fused_computation.11 | loop fusion | flops 294912 | bytes 1179648 | tf_op jit(solution)/shard_map/transpose | solution.py:61
  25.9 0.4 copy.13
  26.4 0.1 copy.24
  26.5 0.9 %pad.11.below_ref = bf16[320,1024]{1,0:T(8,128)(2,1)} pad(bf16[288,1024]{1,0:T(8,128)(2,1)S(1)} %bitcast.44, bf16[]{:T(256)} %constant.37.clone.1), padding=0_32x0_0 | pad | bytes 1245186 | tf_op jit(solution)/shard_map/jit(_pad)/pad | solution.py:155
  27.4 5.6 %collective-permute-done.3 = bf16[3,6,2,512]{3,2,1,0:T(2,128)(2,1)S(1)} collective-permute-done((bf16[3,6,2,512]{3,2,1,0:T(2,128)(2,1)S(1)}, bf16[3,6,2,512]{3,2,1,0:T(2,128)(2,1)S(1)}, u32[]{:S(2)}, u32[]{:S(2)}) %collective-permute-start.3) | collective-permute-done | bytes 36896 | tf_op jit(solution)/shard_map/ppermute | solution.py:76
  33.0 0.8 %maximum_bitcast_fusion.2 = bf16[96,3,2,512]{3,2,0,1:T(2,128)(2,1)S(1)} fusion(bf16[3,90,2,512]{3,2,1,0:T(2,128)(2,1)S(1)} %collective-permute-done.4, bf16[3,6,2,512]{3,2,1,0:T(2,128)(2,1)S(1)} %collective-permute-done.3), kind=kLoop, calls=%fused_computation.12 | loop fusion | flops 294912 | bytes 1179648 | tf_op jit(solution)/shard_map/transpose | solution.py:61
  33.7 0.4 copy.15
  34.2 0.1 copy.26
  34.3 0.9 %pad.13.above_ref = bf16[320,1024]{1,0:T(8,128)(2,1)} pad(bf16[288,1024]{1,0:T(8,128)(2,1)S(1)} %bitcast.42, bf16[]{:T(256)} %constant.37.clone.1), padding=0_32x0_0 | pad | bytes 1245186 | tf_op jit(solution)/shard_map/jit(_pad)/pad | solution.py:155
  35.2 7.5 %shard_map.64 = bf16[768,512]{1,0:T(8,128)(2,1)} custom-call(f32[3,512]{1,0:T(4,128)} %fusion.4.coupling_ref, bf16[320,1024]{1,0:T(8,128)(2,1)} %pad.11.below_ref, bf16[512,1024]{1,0:T(8,128)(2,1)} %pad.12.own_ref, bf16[320,1024]{1,0:T(8,128)(2,1)} %pad.13.above_ref, bf16[1536,512]{1,0:T(8,128)(2,1)} %weight_ref.1, bf16[512,512]{1,0:T(8,128)(2,1)} %mix_ref.1), custom_call_target="tpu_custom_call" | custom-call | flops 2818572288 | bytes 4980736 | tf_op jit(solution)/shard_map/pallas_call | solution.py:158
  42.6 1.9 %copy.16 = bf16[4,3,32,2,512]{4,3,2,1,0:T(2,128)(2,1)S(1)} copy(bf16[4,3,32,2,512]{4,2,0,1,3:T(8,128)(2,1)} %bitcast.46) | data formatting | bytes 1572864 | tf_op jit(solution)/shard_map/transpose | solution.py:172
  44.6 1.4 %slice.65 = bf16[4,90,2,512]{3,2,1,0:T(2,128)(2,1)} slice(bf16[4,96,2,512]{3,2,1,0:T(2,128)(2,1)S(1)} %bitcast.41), slice={[0:4], [0:90], [0:2], [0:512]} | slice | bytes 1474560 | tf_op jit(solution)/shard_map/slice | solution.py:173
  (31 shorter events, 0.5 us)
Async XLA Ops:
  0.0 15.9 %copy-start = (s32[32,4,4,128]{3,2,1,0:T(4,128)S(1)}, s32[32,4,4,128]{3,2,1,0:T(4,128)}, u32[]{:S(2)}) copy-start(s32[32,4,4,128]{3,2,1,0:T(4,128)} %param.8) | copy-start | bytes 786436
  0.0 7.1 %copy-start.1 = (bf16[4,90,2,512]{3,2,1,0:T(2,128)(2,1)S(1)}, bf16[4,90,2,512]{3,2,1,0:T(2,128)(2,1)}, u32[]{:S(2)}) copy-start(bf16[4,90,2,512]{3,2,1,0:T(2,128)(2,1)} %param.6) | copy-start | bytes 2211844
  0.0 16.7 %copy-start.3 = (s32[32,3]{0,1:T(4,128)S(1)}, s32[32,3]{0,1:T(4,128)}, u32[]{:S(2)}) copy-start(s32[32,3]{0,1:T(4,128)} %param.9) | copy-start | bytes 1156
  2.1 23.0 %collective-permute-start.1 = (bf16[3,90,2,512]{3,2,1,0:T(2,128)(2,1)S(1)}, bf16[3,90,2,512]{3,2,1,0:T(2,128)(2,1)S(1)}, u32[]{:S(2)}, u32[]{:S(2)}) collective-permute-start(bf16[3,90,2,512]{3,2,1,0:T(2,128)(2,1)S(1)} %get-tuple-element.15), channel_id=1, source_target_pairs={{0,8},{1,9},{2,10},{3,11},{4,12},{5,13},{6,14},{7,15},{8,16},{9,17... | collective-permute-start | bytes 1658888 | tf_op jit(solution)/shard_map/ppermute | solution.py:76
  7.2 18.0 %collective-permute-start = (bf16[3,6,2,512]{3,2,1,0:T(2,128)(2,1)S(1)}, bf16[3,6,2,512]{3,2,1,0:T(2,128)(2,1)S(1)}, u32[]{:S(2)}, u32[]{:S(2)}) collective-permute-start(bf16[3,6,2,512]{3,2,1,0:T(2,128)(2,1)S(1)} %get-tuple-element.13), channel_id=1, source_target_pairs={{0,9},{1,10},{2,11},{3,12},{4,13},{5,14},{6,15},{7,8},{8,17},{9,18... | collective-permute-start | bytes 110600 | tf_op jit(solution)/shard_map/ppermute | solution.py:76
  9.7 23.3 %collective-permute-start.4 = (bf16[3,90,2,512]{3,2,1,0:T(2,128)(2,1)S(1)}, bf16[3,90,2,512]{3,2,1,0:T(2,128)(2,1)S(1)}, u32[]{:S(2)}, u32[]{:S(2)}) collective-permute-start(bf16[3,90,2,512]{3,2,1,0:T(2,128)(2,1)S(1)} %get-tuple-element.14), channel_id=1, source_target_pairs={{8,0},{9,1},{10,2},{11,3},{12,4},{13,5},{14,6},{15,7},{16,8},{17,9... | collective-permute-start | bytes 1658888 | tf_op jit(solution)/shard_map/ppermute | solution.py:76
  12.2 20.8 %collective-permute-start.3 = (bf16[3,6,2,512]{3,2,1,0:T(2,128)(2,1)S(1)}, bf16[3,6,2,512]{3,2,1,0:T(2,128)(2,1)S(1)}, u32[]{:S(2)}, u32[]{:S(2)}) collective-permute-start(bf16[3,6,2,512]{3,2,1,0:T(2,128)(2,1)S(1)} %get-tuple-element.12), channel_id=1, source_target_pairs={{8,1},{9,2},{10,3},{11,4},{12,5},{13,6},{14,7},{15,0},{16,9},{17,1... | collective-permute-start | bytes 110600 | tf_op jit(solution)/shard_map/ppermute | solution.py:76
  15.7 6.6 %collective-permute-start.2 = (bf16[4,6,2,512]{3,2,1,0:T(2,128)(2,1)S(1)}, bf16[4,6,2,512]{3,2,1,0:T(2,128)(2,1)S(1)}, u32[]{:S(2)}, u32[]{:S(2)}) collective-permute-start(bf16[4,6,2,512]{3,2,1,0:T(2,128)(2,1)S(1)} %slice.53), channel_id=1, source_target_pairs={{0,1},{1,2},{2,3},{3,4},{4,5},{5,6},{6,7},{7,0},{8,9},{9,10},{10,1... | collective-permute-start | bytes 147464 | tf_op jit(solution)/shard_map/ppermute | solution.py:76
  18.1 2.4 %copy-start.2 = (f32[1024,3]{0,1:T(4,128)S(1)}, f32[1024,3]{0,1:T(4,128)}, u32[]{:S(2)}) copy-start(f32[1024,3]{0,1:T(4,128)} %param.7) | copy-start | bytes 36868

commit v9 on v8

--- a/solution.py
+++ b/solution.py
@@ -94,7 +94,9 @@
 DEPTHS = (128, 256, 128)
 
 
-def conv_mix_kernel(coupling_ref, below_ref, own_ref, above_ref, weight_ref, mix_ref, out_ref, *toeplitz_refs):
+def conv_mix_kernel(
+    coupling_ref, below_ref, own_ref, above_ref, weight_ref, mix_ref, out_ref, feature_ref, *toeplitz_refs
+):
     for p in range(3):
         width, depth = WIDTHS[p], DEPTHS[p]
         lane = lax.broadcasted_iota(jnp.int32, (1, TAPS), 1)
@@ -115,8 +117,6 @@
                         jnp.bfloat16
                     )
     nwin = out_ref.shape[0] // (2 * LAT_DEV * LON_PAD)
-    span = LAT_DEV * LON_PAD
-    pieces = [[[] for _ in range(2)] for _ in range(BASIS)]
     row_refs = (below_ref, own_ref, above_ref)
     for j in range(nwin):
         conv = None
@@ -125,11 +125,20 @@
             term = jnp.dot(toeplitz_refs[p][...], window, preferred_element_type=jnp.float32)
             conv = term if conv is None else conv + term
         for k in range(BASIS):
-            for m in range(2):
-                pieces[k][m].append(conv[k * span : (k + 1) * span, m * CHANNELS : (m + 1) * CHANNELS])
+            for q in range(LAT_DEV):
+                block = conv[(k * LAT_DEV + q) * LON_PAD : (k * LAT_DEV + q + 1) * LON_PAD]
+                base = (q * nwin + j) * LON_PAD * 2
+                for m in range(2):
+                    for c in range(CHANNELS // 128):
+                        lanes = m * CHANNELS + c * 128
+                        feature_ref[k * (CHANNELS // 128) + c, pl.ds(base + m, LON_PAD, stride=2), :] = (
+                            block[:, lanes : lanes + 128]
+                        )
     combined = None
     for k in range(BASIS):
-        features = jnp.concatenate(pieces[k][0] + pieces[k][1], axis=0).astype(jnp.bfloat16)
+        features = jnp.concatenate(
+            [feature_ref[k * (CHANNELS // 128) + c] for c in range(CHANNELS // 128)], axis=1
+        ).astype(jnp.bfloat16)
         term = jnp.dot(
             features,
             weight_ref[k * CHANNELS : (k + 1) * CHANNELS, :],
@@ -160,7 +169,8 @@
         out_shape=jax.ShapeDtypeStruct((out_rows, CHANNELS), jnp.bfloat16),
         in_specs=[pl.BlockSpec(memory_space=pltpu.VMEM)] * 6,
         out_specs=pl.BlockSpec(memory_space=pltpu.VMEM),
-        scratch_shapes=[pltpu.VMEM((toeplitz_rows, depth), jnp.bfloat16) for depth in DEPTHS],
+        scratch_shapes=[pltpu.VMEM((BASIS * CHANNELS // 128, out_rows, 128), jnp.float32)]
+        + [pltpu.VMEM((toeplitz_rows, depth), jnp.bfloat16) for depth in DEPTHS],
         cost_estimate=pl.CostEstimate(
             flops=2 * toeplitz_rows * sum(DEPTHS) * 1024 * nwin
             + 2 * out_rows * CHANNELS * CHANNELS * (BASIS + 1),
@@ -168,8 +178,7 @@
             bytes_accessed=sum(p.size for p in pieces) * 2 + (BASIS + 2) * CHANNELS * CHANNELS * 2,
         ),
     )(coupling, *pieces, conv_weight, mix_weight)
-    mixed = mixed.reshape(members, nwin, LAT_DEV, LON_PAD, CHANNELS)
-    mixed = jnp.transpose(mixed, (2, 1, 3, 0, 4)).reshape(LAT_DEV, nwin * LON_PAD, members, CHANNELS)
+    mixed = mixed.reshape(LAT_DEV, nwin * LON_PAD, members, CHANNELS)
     return mixed[:, :nlon]
 
 

time: 46.2 us -> 46.4 us (level)
    reshape x0 -> x1, local copies, waits for them, and re-layouts: none -> 2.15 us  [shards(): mixed = mixed.reshape(LAT_DEV, nwin * LON_PAD, members, CHANNELS)]
    transpose x1 -> x0, local copies, waits for them, and re-layouts: 1.94 us -> none  [shards(): jnp.transpose(mixed, (2, 1, 3, 0, 4))]
where the time goes in v9:
time: 46.4 us; the launch traced here: 46.2 us
  starting transfers between devices  13.6 us (29%)
  local copies, waits for them, and re-layouts  11.9 us (26%)
  Pallas kernels  7.52 us (16%)
  waiting for transfers between devices  5.63 us (12%)
  matrix products  4.22 us (9%)
  other arithmetic  3.12 us (7%)
    ppermute x5, starting transfers between devices, move(): return lax.ppermute(value, ('lat', 'lon'), pairs)  13.6 us
    pallas_call x1, Pallas kernels, shards(): pl.pallas_call(conv_mix_kernel, out_shape=jax.ShapeDtypeStruct((out_rows,...  7.52 us
    ppermute x5, waiting for transfers between devices, move(): return lax.ppermute(value, ('lat', 'lon'), pairs)  5.63 us
    pad x3, local copies, waits for them, and re-layouts, shards(): pieces.append(jnp.pad(piece, ((0, need - piece.shape[0]), (0, 0))))  2.93 us
    transpose x3, other arithmetic, lon_major(): jnp.transpose(rows, (1, 0, 2, 3)).reshape(nlon * count, members * channels)  2.54 us
    dot_general x1, matrix products, band_coupling(): lax.dot_general(filter_hit, slot_hit, (((0,), (0,)), ((), ())), preferred...  2.42 us
    reshape x1, local copies, waits for them, and re-layouts, shards(): mixed = mixed.reshape(LAT_DEV, nwin * LON_PAD, members, CHANNELS)  2.15 us
    slice x1, local copies, waits for them, and re-layouts, gather_pieces(): above = move(x[:OVERHANG], -1, 0)  2.12 us
  transfers between devices with their start and end apart: 5, of which 1 were waited for; matrix products, arithmetic and copies ran while one was open for 25% of the time, Pallas kernels for 0%

profile of v9, /device:TPU:102, one launch (start us, length us, event | category | flops | bytes accessed | tf_op | source)
XLA Modules:
  0.0 46.2 jit_solution(17058587544350390022)
XLA Ops:
  0.0 2.1 %fusion.13 = (bf16[3,90,2,512]{3,2,1,0:T(2,128)(2,1)S(1)}, bf16[3,90,2,512]{3,2,1,0:T(2,128)(2,1)S(1)}) fusion(bf16[4,90,2,512]{3,2,1,0:T(2,128)(2,1)} %param.6), kind=kLoop, calls=%fused_computation.40 | loop fusion | bytes 2211840 | tf_op jit(solution)/shard_map/slice | solution.py:79
  2.1 5.0 %collective-permute-start.1 = (bf16[3,90,2,512]{3,2,1,0:T(2,128)(2,1)S(1)}, bf16[3,90,2,512]{3,2,1,0:T(2,128)(2,1)S(1)}, u32[]{:S(2)}, u32[]{:S(2)}) collective-permute-start(bf16[3,90,2,512]{3,2,1,0:T(2,128)(2,1)S(1)} %get-tuple-element.15), channel_id=1, source_target_pairs={{0,8},{1,9},{2,10},{3,11},{4,12},{5,13},{6,14},{7,15},{8,16},{9,17... | collective-permute-start | bytes 1658888 | tf_op jit(solution)/shard_map/ppermute | solution.py:76
  7.2 2.6 %collective-permute-start = (bf16[3,6,2,512]{3,2,1,0:T(2,128)(2,1)S(1)}, bf16[3,6,2,512]{3,2,1,0:T(2,128)(2,1)S(1)}, u32[]{:S(2)}, u32[]{:S(2)}) collective-permute-start(bf16[3,6,2,512]{3,2,1,0:T(2,128)(2,1)S(1)} %get-tuple-element.13), channel_id=1, source_target_pairs={{0,9},{1,10},{2,11},{3,12},{4,13},{5,14},{6,15},{7,8},{8,17},{9,18... | collective-permute-start | bytes 110600 | tf_op jit(solution)/shard_map/ppermute | solution.py:76
  9.7 2.4 %collective-permute-start.4 = (bf16[3,90,2,512]{3,2,1,0:T(2,128)(2,1)S(1)}, bf16[3,90,2,512]{3,2,1,0:T(2,128)(2,1)S(1)}, u32[]{:S(2)}, u32[]{:S(2)}) collective-permute-start(bf16[3,90,2,512]{3,2,1,0:T(2,128)(2,1)S(1)} %get-tuple-element.14), channel_id=1, source_target_pairs={{8,0},{9,1},{10,2},{11,3},{12,4},{13,5},{14,6},{15,7},{16,8},{17,9... | collective-permute-start | bytes 1658888 | tf_op jit(solution)/shard_map/ppermute | solution.py:76
  12.2 3.5 %collective-permute-start.3 = (bf16[3,6,2,512]{3,2,1,0:T(2,128)(2,1)S(1)}, bf16[3,6,2,512]{3,2,1,0:T(2,128)(2,1)S(1)}, u32[]{:S(2)}, u32[]{:S(2)}) collective-permute-start(bf16[3,6,2,512]{3,2,1,0:T(2,128)(2,1)S(1)} %get-tuple-element.12), channel_id=1, source_target_pairs={{8,1},{9,2},{10,3},{11,4},{12,5},{13,6},{14,7},{15,0},{16,9},{17,1... | collective-permute-start | bytes 110600 | tf_op jit(solution)/shard_map/ppermute | solution.py:76
  15.7 0.1 collective-permute-start.2
  15.9 0.6 %gather_fusion = s32[3,4,4,128]{3,2,1,0:T(4,128)S(1)} fusion(s32[32,4,4,128]{3,2,1,0:T(4,128)S(1)} %copy-done, s32[1024]{0:T(1024)S(1)} %pad_clamp_fusion), kind=kCustom, calls=%fused_computation | custom fusion | bytes 49164 | tf_op jit(solution)/shard_map/jit(_take)/gather | solution.py:22
  16.5 0.1 broadcast_select_fusion
  16.6 0.1 slice_reduce_fusion
  16.7 0.1 copy.11
  16.8 0.6 %gather_fusion.1 = s32[3,3]{1,0:T(4,128)S(1)} fusion(s32[32,3]{1,0:T(8,128)S(1)} %copy.11, s32[1024]{0:T(1024)S(1)} %pad_clamp_fusion), kind=kCustom, calls=%fused_computation.1 | custom fusion | bytes 84 | tf_op jit(solution)/shard_map/jit(_take)/gather | solution.py:23
  17.4 0.2 negate_reduce_fusion
  17.6 0.1 fusion.9
  17.7 0.1 and.97
  18.1 2.4 %fusion = f32[1024,512]{1,0:T(8,128)S(1)} fusion(s32[1536]{0:T(1024)S(1)} %eq.43, s32[1536]{0:T(1024)S(1)} %add_select_fusion), kind=kOutput, calls=%fused_computation.3 | convolution fusion | flops 1612972032 | bytes 2109440 | tf_op jit(solution)/shard_map/dot_general | solution.py:50
  20.5 1.8 %fusion.4.coupling_ref = f32[3,512]{1,0:T(4,128)} fusion(f32[1024,512]{1,0:T(8,128)S(1)} %fusion, f32[1024,3]{0,1:T(4,128)S(1)} %copy-done.2), kind=kOutput, calls=%fused_computation.9 | convolution fusion | flops 18877440 | bytes 2115584 | tf_op jit(solution)/shard_map/dot_general | solution.py:53
  22.3 1.0 %maximum_bitcast_fusion = bf16[96,4,2,512]{3,2,0,1:T(2,128)(2,1)S(1)} fusion(bf16[4,90,2,512]{3,2,1,0:T(2,128)(2,1)S(1)} %copy-done.1, bf16[4,6,2,512]{3,2,1,0:T(2,128)(2,1)S(1)} %collective-permute-done.2), kind=kLoop, calls=%fused_computation.10 | loop fusion | flops 393216 | bytes 1572864 | tf_op jit(solution)/shard_map/transpose | solution.py:61
  23.4 0.5 %copy.13 = bf16[96,4,2,512]{3,2,1,0:T(2,128)(2,1)S(1)} copy(bf16[96,4,2,512]{3,2,0,1:T(2,128)(2,1)S(1)} %maximum_bitcast_fusion) | data formatting | bytes 1572864 | tf_op jit(solution)/shard_map/transpose | solution.py:61
  23.9 0.1 copy.23
  24.1 1.1 %pad.12.own_ref = bf16[512,1024]{1,0:T(8,128)(2,1)} pad(bf16[384,1024]{1,0:T(8,128)(2,1)S(1)} %bitcast.36, bf16[]{:T(256)} %constant.37.clone.1), padding=0_128x0_0 | pad | bytes 1835010 | tf_op jit(solution)/shard_map/jit(_pad)/pad | solution.py:164
  25.2 0.8 %maximum_bitcast_fusion.1 = bf16[96,3,2,512]{3,2,0,1:T(2,128)(2,1)S(1)} fusion(bf16[3,90,2,512]{3,2,1,0:T(2,128)(2,1)S(1)} %collective-permute-done.1, bf16[3,6,2,512]{3,2,1,0:T(2,128)(2,1)S(1)} %collective-permute-done), kind=kLoop, calls=%fused_computation.11 | loop fusion | flops 294912 | bytes 1179648 | tf_op jit(solution)/shard_map/transpose | solution.py:61
  25.9 0.4 copy.12
  26.4 0.1 copy.22
  26.5 0.9 %pad.11.below_ref = bf16[320,1024]{1,0:T(8,128)(2,1)} pad(bf16[288,1024]{1,0:T(8,128)(2,1)S(1)} %bitcast.39, bf16[]{:T(256)} %constant.37.clone.1), padding=0_32x0_0 | pad | bytes 1245186 | tf_op jit(solution)/shard_map/jit(_pad)/pad | solution.py:164
  27.4 5.6 %collective-permute-done.3 = bf16[3,6,2,512]{3,2,1,0:T(2,128)(2,1)S(1)} collective-permute-done((bf16[3,6,2,512]{3,2,1,0:T(2,128)(2,1)S(1)}, bf16[3,6,2,512]{3,2,1,0:T(2,128)(2,1)S(1)}, u32[]{:S(2)}, u32[]{:S(2)}) %collective-permute-start.3) | collective-permute-done | bytes 36896 | tf_op jit(solution)/shard_map/ppermute | solution.py:76
  33.0 0.8 %maximum_bitcast_fusion.2 = bf16[96,3,2,512]{3,2,0,1:T(2,128)(2,1)S(1)} fusion(bf16[3,90,2,512]{3,2,1,0:T(2,128)(2,1)S(1)} %collective-permute-done.4, bf16[3,6,2,512]{3,2,1,0:T(2,128)(2,1)S(1)} %collective-permute-done.3), kind=kLoop, calls=%fused_computation.12 | loop fusion | flops 294912 | bytes 1179648 | tf_op jit(solution)/shard_map/transpose | solution.py:61
  33.7 0.4 copy.14
  34.2 0.1 copy.24
  34.3 0.9 %pad.13.above_ref = bf16[320,1024]{1,0:T(8,128)(2,1)} pad(bf16[288,1024]{1,0:T(8,128)(2,1)S(1)} %bitcast.37, bf16[]{:T(256)} %constant.37.clone.1), padding=0_32x0_0 | pad | bytes 1245186 | tf_op jit(solution)/shard_map/jit(_pad)/pad | solution.py:164
  35.2 7.5 %shard_map.64 = bf16[768,512]{1,0:T(8,128)(2,1)} custom-call(f32[3,512]{1,0:T(4,128)} %fusion.4.coupling_ref, bf16[320,1024]{1,0:T(8,128)(2,1)} %pad.11.below_ref, bf16[512,1024]{1,0:T(8,128)(2,1)} %pad.12.own_ref, bf16[320,1024]{1,0:T(8,128)(2,1)} %pad.13.above_ref, bf16[1536,512]{1,0:T(8,128)(2,1)} %weight_ref.1, bf16[512,512]{1,0:T(8,128)(2,1)} %mix_ref.1), custom_call_target="tpu_custom_call" | custom-call | flops 2818572288 | bytes 4980736 | tf_op jit(solution)/shard_map/pallas_call | solution.py:167
  42.7 2.1 %reshape.205 = bf16[4,96,2,512]{3,2,1,0:T(2,128)(2,1)S(1)} reshape(bf16[768,512]{1,0:T(8,128)(2,1)} %shard_map.64) | data formatting | bytes 1572864 | tf_op jit(solution)/shard_map/reshape | solution.py:181
  44.8 1.4 %slice.65 = bf16[4,90,2,512]{3,2,1,0:T(2,128)(2,1)} slice(bf16[4,96,2,512]{3,2,1,0:T(2,128)(2,1)S(1)} %reshape.205), slice={[0:4], [0:90], [0:2], [0:512]} | slice | bytes 1474560 | tf_op jit(solution)/shard_map/slice | solution.py:182
  (31 shorter events, 0.5 us)
Async XLA Ops:
  0.0 15.9 %copy-start = (s32[32,4,4,128]{3,2,1,0:T(4,128)S(1)}, s32[32,4,4,128]{3,2,1,0:T(4,128)}, u32[]{:S(2)}) copy-start(s32[32,4,4,128]{3,2,1,0:T(4,128)} %param.8) | copy-start | bytes 786436
  0.0 7.1 %copy-start.1 = (bf16[4,90,2,512]{3,2,1,0:T(2,128)(2,1)S(1)}, bf16[4,90,2,512]{3,2,1,0:T(2,128)(2,1)}, u32[]{:S(2)}) copy-start(bf16[4,90,2,512]{3,2,1,0:T(2,128)(2,1)} %param.6) | copy-start | bytes 2211844
  0.0 16.7 %copy-start.3 = (s32[32,3]{0,1:T(4,128)S(1)}, s32[32,3]{0,1:T(4,128)}, u32[]{:S(2)}) copy-start(s32[32,3]{0,1:T(4,128)} %param.9) | copy-start | bytes 1156
  2.1 23.0 %collective-permute-start.1 = (bf16[3,90,2,512]{3,2,1,0:T(2,128)(2,1)S(1)}, bf16[3,90,2,512]{3,2,1,0:T(2,128)(2,1)S(1)}, u32[]{:S(2)}, u32[]{:S(2)}) collective-permute-start(bf16[3,90,2,512]{3,2,1,0:T(2,128)(2,1)S(1)} %get-tuple-element.15), channel_id=1, source_target_pairs={{0,8},{1,9},{2,10},{3,11},{4,12},{5,13},{6,14},{7,15},{8,16},{9,17... | collective-permute-start | bytes 1658888 | tf_op jit(solution)/shard_map/ppermute | solution.py:76
  7.2 18.0 %collective-permute-start = (bf16[3,6,2,512]{3,2,1,0:T(2,128)(2,1)S(1)}, bf16[3,6,2,512]{3,2,1,0:T(2,128)(2,1)S(1)}, u32[]{:S(2)}, u32[]{:S(2)}) collective-permute-start(bf16[3,6,2,512]{3,2,1,0:T(2,128)(2,1)S(1)} %get-tuple-element.13), channel_id=1, source_target_pairs={{0,9},{1,10},{2,11},{3,12},{4,13},{5,14},{6,15},{7,8},{8,17},{9,18... | collective-permute-start | bytes 110600 | tf_op jit(solution)/shard_map/ppermute | solution.py:76
  9.7 23.3 %collective-permute-start.4 = (bf16[3,90,2,512]{3,2,1,0:T(2,128)(2,1)S(1)}, bf16[3,90,2,512]{3,2,1,0:T(2,128)(2,1)S(1)}, u32[]{:S(2)}, u32[]{:S(2)}) collective-permute-start(bf16[3,90,2,512]{3,2,1,0:T(2,128)(2,1)S(1)} %get-tuple-element.14), channel_id=1, source_target_pairs={{8,0},{9,1},{10,2},{11,3},{12,4},{13,5},{14,6},{15,7},{16,8},{17,9... | collective-permute-start | bytes 1658888 | tf_op jit(solution)/shard_map/ppermute | solution.py:76
  12.2 20.8 %collective-permute-start.3 = (bf16[3,6,2,512]{3,2,1,0:T(2,128)(2,1)S(1)}, bf16[3,6,2,512]{3,2,1,0:T(2,128)(2,1)S(1)}, u32[]{:S(2)}, u32[]{:S(2)}) collective-permute-start(bf16[3,6,2,512]{3,2,1,0:T(2,128)(2,1)S(1)} %get-tuple-element.12), channel_id=1, source_target_pairs={{8,1},{9,2},{10,3},{11,4},{12,5},{13,6},{14,7},{15,0},{16,9},{17,1... | collective-permute-start | bytes 110600 | tf_op jit(solution)/shard_map/ppermute | solution.py:76
  15.7 6.6 %collective-permute-start.2 = (bf16[4,6,2,512]{3,2,1,0:T(2,128)(2,1)S(1)}, bf16[4,6,2,512]{3,2,1,0:T(2,128)(2,1)S(1)}, u32[]{:S(2)}, u32[]{:S(2)}) collective-permute-start(bf16[4,6,2,512]{3,2,1,0:T(2,128)(2,1)S(1)} %slice.53), channel_id=1, source_target_pairs={{0,1},{1,2},{2,3},{3,4},{4,5},{5,6},{6,7},{7,0},{8,9},{9,10},{10,1... | collective-permute-start | bytes 147464 | tf_op jit(solution)/shard_map/ppermute | solution.py:76
  18.1 2.4 %copy-start.2 = (f32[1024,3]{0,1:T(4,128)S(1)}, f32[1024,3]{0,1:T(4,128)}, u32[]{:S(2)}) copy-start(f32[1024,3]{0,1:T(4,128)} %param.7) | copy-start | bytes 36868

commit v10 on v9

--- a/solution.py
+++ b/solution.py
@@ -116,7 +116,8 @@
                     toeplitz_refs[p][pl.ds((k * LAT_DEV + q) * LON_PAD + 8 * g, 8), :] = block.astype(
                         jnp.bfloat16
                     )
-    nwin = out_ref.shape[0] // (2 * LAT_DEV * LON_PAD)
+    nlon = out_ref.shape[0] // (2 * LAT_DEV)
+    nwin = -(-nlon // WINDOW)
     row_refs = (below_ref, own_ref, above_ref)
     for j in range(nwin):
         conv = None
@@ -126,12 +127,14 @@
             conv = term if conv is None else conv + term
         for k in range(BASIS):
             for q in range(LAT_DEV):
-                block = conv[(k * LAT_DEV + q) * LON_PAD : (k * LAT_DEV + q + 1) * LON_PAD]
-                base = (q * nwin + j) * LON_PAD * 2
+                count = min(WINDOW, nlon - j * WINDOW)
+                first = (k * LAT_DEV + q) * LON_PAD
+                block = conv[first : first + count]
+                base = (q * nlon + j * WINDOW) * 2
                 for m in range(2):
                     for c in range(CHANNELS // 128):
                         lanes = m * CHANNELS + c * 128
-                        feature_ref[k * (CHANNELS // 128) + c, pl.ds(base + m, LON_PAD, stride=2), :] = (
+                        feature_ref[k * (CHANNELS // 128) + c, pl.ds(base + m, count, stride=2), :] = (
                             block[:, lanes : lanes + 128]
                         )
     combined = None
@@ -162,7 +165,7 @@
     for piece, width, depth in zip(gather_pieces(fields), WIDTHS, DEPTHS):
         need = (nwin - 1) * WINDOW * width + depth
         pieces.append(jnp.pad(piece, ((0, need - piece.shape[0]), (0, 0))))
-    out_rows = members * nwin * LAT_DEV * LON_PAD
+    out_rows = members * nlon * LAT_DEV
     toeplitz_rows = BASIS * LAT_DEV * LON_PAD
     mixed = pl.pallas_call(
         conv_mix_kernel,
@@ -178,8 +181,7 @@
             bytes_accessed=sum(p.size for p in pieces) * 2 + (BASIS + 2) * CHANNELS * CHANNELS * 2,
         ),
     )(coupling, *pieces, conv_weight, mix_weight)
-    mixed = mixed.reshape(LAT_DEV, nwin * LON_PAD, members, CHANNELS)
-    return mixed[:, :nlon]
+    return mixed.reshape(LAT_DEV, nlon, members, CHANNELS)
 
 
 def solution(mesh):

time: 46.4 us -> 45 us (0.970)
  waiting for transfers between devices: 5.63 us -> 4.74 us
  local copies, waits for them, and re-layouts: 11.9 us -> 11.2 us
    slice x1 -> x0, local copies, waits for them, and re-layouts: 1.37 us -> none  [shards(): return mixed[:, :nlon]]
    ppermute x5, waiting for transfers between devices: 5.63 us -> 4.74 us  [move(): return lax.ppermute(value, ('lat', 'lon'), pairs)]
    reshape x1, local copies, waits for them, and re-layouts: 2.15 us -> 2.76 us  [shards(): return mixed.reshape(LAT_DEV, nlon, members, CHANNELS)]
  transfers between devices with their start and end apart: 5 -> 5, of which waited for: 1 -> 1; matrix products, arithmetic and copies ran while one was open for 25% -> 26% of each run, Pallas kernels for 0% -> 0%
where the time goes in v10:
time: 45 us; the launch traced here: 44.7 us
  starting transfers between devices  13.8 us (31%)
  local copies, waits for them, and re-layouts  11.2 us (25%)
  Pallas kernels  7.36 us (16%)
  waiting for transfers between devices  4.74 us (11%)
  matrix products  4.22 us (9%)
  other arithmetic  3.13 us (7%)
    ppermute x5, starting transfers between devices, move(): return lax.ppermute(value, ('lat', 'lon'), pairs)  13.8 us
    pallas_call x1, Pallas kernels, shards(): pl.pallas_call(conv_mix_kernel, out_shape=jax.ShapeDtypeStruct((out_rows,...  7.36 us
    ppermute x5, waiting for transfers between devices, move(): return lax.ppermute(value, ('lat', 'lon'), pairs)  4.74 us
    pad x3, local copies, waits for them, and re-layouts, shards(): pieces.append(jnp.pad(piece, ((0, need - piece.shape[0]), (0, 0))))  2.95 us
    reshape x1, local copies, waits for them, and re-layouts, shards(): return mixed.reshape(LAT_DEV, nlon, members, CHANNELS)  2.76 us
    transpose x3, other arithmetic, lon_major(): jnp.transpose(rows, (1, 0, 2, 3)).reshape(nlon * count, members * channels)  2.54 us
    dot_general x1, matrix products, band_coupling(): lax.dot_general(filter_hit, slot_hit, (((0,), (0,)), ((), ())), preferred...  2.42 us
    slice x1, local copies, waits for them, and re-layouts, gather_pieces(): above = move(x[:OVERHANG], -1, 0)  2.12 us
  transfers between devices with their start and end apart: 5, of which 1 were waited for; matrix products, arithmetic and copies ran while one was open for 26% of the time, Pallas kernels for 0%

profile of v10, /device:TPU:102, one launch (start us, length us, event | category | flops | bytes accessed | tf_op | source)
XLA Modules:
  0.0 44.7 jit_solution(7277011456322699942)
XLA Ops:
  0.0 2.1 %fusion.13 = (bf16[3,90,2,512]{3,2,1,0:T(2,128)(2,1)S(1)}, bf16[3,90,2,512]{3,2,1,0:T(2,128)(2,1)S(1)}) fusion(bf16[4,90,2,512]{3,2,1,0:T(2,128)(2,1)} %param.6), kind=kLoop, calls=%fused_computation.40 | loop fusion | bytes 2211840 | tf_op jit(solution)/shard_map/slice | solution.py:79
  2.1 5.0 %collective-permute-start.1 = (bf16[3,90,2,512]{3,2,1,0:T(2,128)(2,1)S(1)}, bf16[3,90,2,512]{3,2,1,0:T(2,128)(2,1)S(1)}, u32[]{:S(2)}, u32[]{:S(2)}) collective-permute-start(bf16[3,90,2,512]{3,2,1,0:T(2,128)(2,1)S(1)} %get-tuple-element.15), channel_id=1, source_target_pairs={{0,8},{1,9},{2,10},{3,11},{4,12},{5,13},{6,14},{7,15},{8,16},{9,17... | collective-permute-start | bytes 1658888 | tf_op jit(solution)/shard_map/ppermute | solution.py:76
  7.2 2.6 %collective-permute-start = (bf16[3,6,2,512]{3,2,1,0:T(2,128)(2,1)S(1)}, bf16[3,6,2,512]{3,2,1,0:T(2,128)(2,1)S(1)}, u32[]{:S(2)}, u32[]{:S(2)}) collective-permute-start(bf16[3,6,2,512]{3,2,1,0:T(2,128)(2,1)S(1)} %get-tuple-element.13), channel_id=1, source_target_pairs={{0,9},{1,10},{2,11},{3,12},{4,13},{5,14},{6,15},{7,8},{8,17},{9,18... | collective-permute-start | bytes 110600 | tf_op jit(solution)/shard_map/ppermute | solution.py:76
  9.8 2.0 %collective-permute-start.2 = (bf16[4,6,2,512]{3,2,1,0:T(2,128)(2,1)S(1)}, bf16[4,6,2,512]{3,2,1,0:T(2,128)(2,1)S(1)}, u32[]{:S(2)}, u32[]{:S(2)}) collective-permute-start(bf16[4,6,2,512]{3,2,1,0:T(2,128)(2,1)S(1)} %slice.50), channel_id=1, source_target_pairs={{0,1},{1,2},{2,3},{3,4},{4,5},{5,6},{6,7},{7,0},{8,9},{9,10},{10,1... | collective-permute-start | bytes 147464 | tf_op jit(solution)/shard_map/ppermute | solution.py:76
  11.8 2.4 %collective-permute-start.4 = (bf16[3,90,2,512]{3,2,1,0:T(2,128)(2,1)S(1)}, bf16[3,90,2,512]{3,2,1,0:T(2,128)(2,1)S(1)}, u32[]{:S(2)}, u32[]{:S(2)}) collective-permute-start(bf16[3,90,2,512]{3,2,1,0:T(2,128)(2,1)S(1)} %get-tuple-element.14), channel_id=1, source_target_pairs={{8,0},{9,1},{10,2},{11,3},{12,4},{13,5},{14,6},{15,7},{16,8},{17,9... | collective-permute-start | bytes 1658888 | tf_op jit(solution)/shard_map/ppermute | solution.py:76
  14.2 1.9 %collective-permute-start.3 = (bf16[3,6,2,512]{3,2,1,0:T(2,128)(2,1)S(1)}, bf16[3,6,2,512]{3,2,1,0:T(2,128)(2,1)S(1)}, u32[]{:S(2)}, u32[]{:S(2)}) collective-permute-start(bf16[3,6,2,512]{3,2,1,0:T(2,128)(2,1)S(1)} %get-tuple-element.12), channel_id=1, source_target_pairs={{8,1},{9,2},{10,3},{11,4},{12,5},{13,6},{14,7},{15,0},{16,9},{17,1... | collective-permute-start | bytes 110600 | tf_op jit(solution)/shard_map/ppermute | solution.py:76
  16.2 0.6 %gather_fusion = s32[3,4,4,128]{3,2,1,0:T(4,128)S(1)} fusion(s32[32,4,4,128]{3,2,1,0:T(4,128)S(1)} %copy-done, s32[1024]{0:T(1024)S(1)} %pad_clamp_fusion), kind=kCustom, calls=%fused_computation | custom fusion | bytes 49164 | tf_op jit(solution)/shard_map/jit(_take)/gather | solution.py:22
  16.8 0.1 broadcast_select_fusion
  16.8 0.1 slice_reduce_fusion
  17.0 0.1 copy.11
  17.1 0.6 %gather_fusion.1 = s32[3,3]{1,0:T(4,128)S(1)} fusion(s32[32,3]{1,0:T(8,128)S(1)} %copy.11, s32[1024]{0:T(1024)S(1)} %pad_clamp_fusion), kind=kCustom, calls=%fused_computation.1 | custom fusion | bytes 84 | tf_op jit(solution)/shard_map/jit(_take)/gather | solution.py:23
  17.6 0.1 broadcast_select_fusion.1
  17.7 0.2 negate_reduce_fusion
  18.0 0.1 fusion.9
  18.1 0.1 and.97
  18.4 2.4 %fusion = f32[1024,512]{1,0:T(8,128)S(1)} fusion(s32[1536]{0:T(1024)S(1)} %eq.43, s32[1536]{0:T(1024)S(1)} %add_select_fusion), kind=kOutput, calls=%fused_computation.3 | convolution fusion | flops 1612972032 | bytes 2109440 | tf_op jit(solution)/shard_map/dot_general | solution.py:50
  20.8 1.8 %fusion.4.coupling_ref = f32[3,512]{1,0:T(4,128)} fusion(f32[1024,512]{1,0:T(8,128)S(1)} %fusion, f32[1024,3]{0,1:T(4,128)S(1)} %copy-done.2), kind=kOutput, calls=%fused_computation.9 | convolution fusion | flops 18877440 | bytes 2115584 | tf_op jit(solution)/shard_map/dot_general | solution.py:53
  22.6 1.0 %maximum_bitcast_fusion = bf16[96,4,2,512]{3,2,0,1:T(2,128)(2,1)S(1)} fusion(bf16[4,90,2,512]{3,2,1,0:T(2,128)(2,1)S(1)} %copy-done.1, bf16[4,6,2,512]{3,2,1,0:T(2,128)(2,1)S(1)} %collective-permute-done.2), kind=kLoop, calls=%fused_computation.10 | loop fusion | flops 393216 | bytes 1572864 | tf_op jit(solution)/shard_map/transpose | solution.py:61
  23.7 0.5 %copy.13 = bf16[96,4,2,512]{3,2,1,0:T(2,128)(2,1)S(1)} copy(bf16[96,4,2,512]{3,2,0,1:T(2,128)(2,1)S(1)} %maximum_bitcast_fusion) | data formatting | bytes 1572864 | tf_op jit(solution)/shard_map/transpose | solution.py:61
  24.2 0.1 copy.23
  24.3 1.1 %pad.12.own_ref = bf16[512,1024]{1,0:T(8,128)(2,1)} pad(bf16[384,1024]{1,0:T(8,128)(2,1)S(1)} %bitcast.36, bf16[]{:T(256)} %constant.37.clone.1), padding=0_128x0_0 | pad | bytes 1835010 | tf_op jit(solution)/shard_map/jit(_pad)/pad | solution.py:167
  25.5 0.8 %maximum_bitcast_fusion.1 = bf16[96,3,2,512]{3,2,0,1:T(2,128)(2,1)S(1)} fusion(bf16[3,90,2,512]{3,2,1,0:T(2,128)(2,1)S(1)} %collective-permute-done.1, bf16[3,6,2,512]{3,2,1,0:T(2,128)(2,1)S(1)} %collective-permute-done), kind=kLoop, calls=%fused_computation.11 | loop fusion | flops 294912 | bytes 1179648 | tf_op jit(solution)/shard_map/transpose | solution.py:61
  26.2 0.4 copy.12
  26.7 0.1 copy.22
  26.7 0.9 %pad.11.below_ref = bf16[320,1024]{1,0:T(8,128)(2,1)} pad(bf16[288,1024]{1,0:T(8,128)(2,1)S(1)} %bitcast.39, bf16[]{:T(256)} %constant.37.clone.1), padding=0_32x0_0 | pad | bytes 1245186 | tf_op jit(solution)/shard_map/jit(_pad)/pad | solution.py:167
  27.6 4.7 %collective-permute-done.3 = bf16[3,6,2,512]{3,2,1,0:T(2,128)(2,1)S(1)} collective-permute-done((bf16[3,6,2,512]{3,2,1,0:T(2,128)(2,1)S(1)}, bf16[3,6,2,512]{3,2,1,0:T(2,128)(2,1)S(1)}, u32[]{:S(2)}, u32[]{:S(2)}) %collective-permute-start.3) | collective-permute-done | bytes 36896 | tf_op jit(solution)/shard_map/ppermute | solution.py:76
  32.4 0.8 %maximum_bitcast_fusion.2 = bf16[96,3,2,512]{3,2,0,1:T(2,128)(2,1)S(1)} fusion(bf16[3,90,2,512]{3,2,1,0:T(2,128)(2,1)S(1)} %collective-permute-done.4, bf16[3,6,2,512]{3,2,1,0:T(2,128)(2,1)S(1)} %collective-permute-done.3), kind=kLoop, calls=%fused_computation.12 | loop fusion | flops 294912 | bytes 1179648 | tf_op jit(solution)/shard_map/transpose | solution.py:61
  33.1 0.4 copy.14
  33.6 0.1 copy.24
  33.6 0.9 %pad.13.above_ref = bf16[320,1024]{1,0:T(8,128)(2,1)} pad(bf16[288,1024]{1,0:T(8,128)(2,1)S(1)} %bitcast.37, bf16[]{:T(256)} %constant.37.clone.1), padding=0_32x0_0 | pad | bytes 1245186 | tf_op jit(solution)/shard_map/jit(_pad)/pad | solution.py:167
  34.6 7.4 %shard_map.64 = bf16[720,512]{1,0:T(8,128)(2,1)} custom-call(f32[3,512]{1,0:T(4,128)} %fusion.4.coupling_ref, bf16[320,1024]{1,0:T(8,128)(2,1)} %pad.11.below_ref, bf16[512,1024]{1,0:T(8,128)(2,1)} %pad.12.own_ref, bf16[320,1024]{1,0:T(8,128)(2,1)} %pad.13.above_ref, bf16[1536,512]{1,0:T(8,128)(2,1)} %weight_ref.1, bf16[512,512]{1,0:T(8,128)(2,1)} %mix_ref.1), custom_call_target="tpu_custom_call" | custom-call | flops 2717908992 | bytes 4980736 | tf_op jit(solution)/shard_map/pallas_call | solution.py:170
  41.9 2.8 %reshape.205 = bf16[4,90,2,512]{3,2,1,0:T(2,128)(2,1)} reshape(bf16[720,512]{1,0:T(8,128)(2,1)} %shard_map.64) | data formatting | bytes 1474560 | tf_op jit(solution)/shard_map/reshape | solution.py:184
  (30 shorter events, 0.5 us)
Async XLA Ops:
  0.0 16.2 %copy-start = (s32[32,4,4,128]{3,2,1,0:T(4,128)S(1)}, s32[32,4,4,128]{3,2,1,0:T(4,128)}, u32[]{:S(2)}) copy-start(s32[32,4,4,128]{3,2,1,0:T(4,128)} %param.8) | copy-start | bytes 786436
  0.0 7.1 %copy-start.1 = (bf16[4,90,2,512]{3,2,1,0:T(2,128)(2,1)S(1)}, bf16[4,90,2,512]{3,2,1,0:T(2,128)(2,1)}, u32[]{:S(2)}) copy-start(bf16[4,90,2,512]{3,2,1,0:T(2,128)(2,1)} %param.6) | copy-start | bytes 2211844
  0.0 17.0 %copy-start.3 = (s32[32,3]{0,1:T(4,128)S(1)}, s32[32,3]{0,1:T(4,128)}, u32[]{:S(2)}) copy-start(s32[32,3]{0,1:T(4,128)} %param.9) | copy-start | bytes 1156
  2.1 23.3 %collective-permute-start.1 = (bf16[3,90,2,512]{3,2,1,0:T(2,128)(2,1)S(1)}, bf16[3,90,2,512]{3,2,1,0:T(2,128)(2,1)S(1)}, u32[]{:S(2)}, u32[]{:S(2)}) collective-permute-start(bf16[3,90,2,512]{3,2,1,0:T(2,128)(2,1)S(1)} %get-tuple-element.15), channel_id=1, source_target_pairs={{0,8},{1,9},{2,10},{3,11},{4,12},{5,13},{6,14},{7,15},{8,16},{9,17... | collective-permute-start | bytes 1658888 | tf_op jit(solution)/shard_map/ppermute | solution.py:76
  7.2 18.3 %collective-permute-start = (bf16[3,6,2,512]{3,2,1,0:T(2,128)(2,1)S(1)}, bf16[3,6,2,512]{3,2,1,0:T(2,128)(2,1)S(1)}, u32[]{:S(2)}, u32[]{:S(2)}) collective-permute-start(bf16[3,6,2,512]{3,2,1,0:T(2,128)(2,1)S(1)} %get-tuple-element.13), channel_id=1, source_target_pairs={{0,9},{1,10},{2,11},{3,12},{4,13},{5,14},{6,15},{7,8},{8,17},{9,18... | collective-permute-start | bytes 110600 | tf_op jit(solution)/shard_map/ppermute | solution.py:76
  9.8 12.9 %collective-permute-start.2 = (bf16[4,6,2,512]{3,2,1,0:T(2,128)(2,1)S(1)}, bf16[4,6,2,512]{3,2,1,0:T(2,128)(2,1)S(1)}, u32[]{:S(2)}, u32[]{:S(2)}) collective-permute-start(bf16[4,6,2,512]{3,2,1,0:T(2,128)(2,1)S(1)} %slice.50), channel_id=1, source_target_pairs={{0,1},{1,2},{2,3},{3,4},{4,5},{5,6},{6,7},{7,0},{8,9},{9,10},{10,1... | collective-permute-start | bytes 147464 | tf_op jit(solution)/shard_map/ppermute | solution.py:76
  11.8 20.6 %collective-permute-start.4 = (bf16[3,90,2,512]{3,2,1,0:T(2,128)(2,1)S(1)}, bf16[3,90,2,512]{3,2,1,0:T(2,128)(2,1)S(1)}, u32[]{:S(2)}, u32[]{:S(2)}) collective-permute-start(bf16[3,90,2,512]{3,2,1,0:T(2,128)(2,1)S(1)} %get-tuple-element.14), channel_id=1, source_target_pairs={{8,0},{9,1},{10,2},{11,3},{12,4},{13,5},{14,6},{15,7},{16,8},{17,9... | collective-permute-start | bytes 1658888 | tf_op jit(solution)/shard_map/ppermute | solution.py:76
  14.2 18.2 %collective-permute-start.3 = (bf16[3,6,2,512]{3,2,1,0:T(2,128)(2,1)S(1)}, bf16[3,6,2,512]{3,2,1,0:T(2,128)(2,1)S(1)}, u32[]{:S(2)}, u32[]{:S(2)}) collective-permute-start(bf16[3,6,2,512]{3,2,1,0:T(2,128)(2,1)S(1)} %get-tuple-element.12), channel_id=1, source_target_pairs={{8,1},{9,2},{10,3},{11,4},{12,5},{13,6},{14,7},{15,0},{16,9},{17,1... | collective-permute-start | bytes 110600 | tf_op jit(solution)/shard_map/ppermute | solution.py:76
  18.4 2.4 %copy-start.2 = (f32[1024,3]{0,1:T(4,128)S(1)}, f32[1024,3]{0,1:T(4,128)}, u32[]{:S(2)}) copy-start(f32[1024,3]{0,1:T(4,128)} %param.7) | copy-start | bytes 36868

commit v11 on v10

--- a/solution.py
+++ b/solution.py
@@ -116,7 +116,7 @@
                     toeplitz_refs[p][pl.ds((k * LAT_DEV + q) * LON_PAD + 8 * g, 8), :] = block.astype(
                         jnp.bfloat16
                     )
-    nlon = out_ref.shape[0] // (2 * LAT_DEV)
+    nlon = out_ref.shape[0] // LAT_DEV
     nwin = -(-nlon // WINDOW)
     row_refs = (below_ref, own_ref, above_ref)
     for j in range(nwin):
@@ -149,9 +149,8 @@
         )
         combined = term if combined is None else combined + term
     activated = jax.nn.gelu(combined, approximate=True).astype(jnp.bfloat16)
-    out_ref[...] = jnp.dot(activated, mix_ref[...], preferred_element_type=jnp.float32).astype(
-        out_ref.dtype
-    )
+    mixed = jnp.dot(activated, mix_ref[...], preferred_element_type=jnp.float32).astype(out_ref.dtype)
+    out_ref[...] = mixed.reshape(out_ref.shape)
 
 
 def shards(fields, coeffs, entries, band_info, conv_weight, mix_weight):
@@ -169,7 +168,7 @@
     toeplitz_rows = BASIS * LAT_DEV * LON_PAD
     mixed = pl.pallas_call(
         conv_mix_kernel,
-        out_shape=jax.ShapeDtypeStruct((out_rows, CHANNELS), jnp.bfloat16),
+        out_shape=jax.ShapeDtypeStruct((LAT_DEV * nlon, members, CHANNELS), jnp.bfloat16),
         in_specs=[pl.BlockSpec(memory_space=pltpu.VMEM)] * 6,
         out_specs=pl.BlockSpec(memory_space=pltpu.VMEM),
         scratch_shapes=[pltpu.VMEM((BASIS * CHANNELS // 128, out_rows, 128), jnp.float32)]

time: 45 us -> 42.2 us (0.938)
  local copies, waits for them, and re-layouts: 11.2 us -> 8.37 us
    reshape x1 -> x0, local copies, waits for them, and re-layouts: 2.76 us -> none  [shards(): return mixed.reshape(LAT_DEV, nlon, members, CHANNELS)]
  transfers between devices with their start and end apart: 5 -> 5, of which waited for: 1 -> 1; matrix products, arithmetic and copies ran while one was open for 26% -> 27% of each run, Pallas kernels for 0% -> 0%
where the time goes in v11:
time: 42.2 us; the launch traced here: 41.8 us
  starting transfers between devices  13.8 us (33%)
  local copies, waits for them, and re-layouts  8.37 us (20%)
  Pallas kernels  7.33 us (17%)
  waiting for transfers between devices  4.72 us (11%)
  matrix products  4.22 us (10%)
  other arithmetic  3.13 us (7%)
    ppermute x5, starting transfers between devices, move(): return lax.ppermute(value, ('lat', 'lon'), pairs)  13.8 us
    pallas_call x1, Pallas kernels, shards(): pl.pallas_call(conv_mix_kernel, out_shape=jax.ShapeDtypeStruct((LAT_DEV *...  7.33 us
    ppermute x5, waiting for transfers between devices, move(): return lax.ppermute(value, ('lat', 'lon'), pairs)  4.72 us
    pad x3, local copies, waits for them, and re-layouts, shards(): pieces.append(jnp.pad(piece, ((0, need - piece.shape[0]), (0, 0))))  2.96 us
    transpose x3, other arithmetic, lon_major(): jnp.transpose(rows, (1, 0, 2, 3)).reshape(nlon * count, members * channels)  2.54 us
    dot_general x1, matrix products, band_coupling(): lax.dot_general(filter_hit, slot_hit, (((0,), (0,)), ((), ())), preferred...  2.42 us
    slice x1, local copies, waits for them, and re-layouts, gather_pieces(): above = move(x[:OVERHANG], -1, 0)  2.06 us
    dot_general x1, matrix products, band_coupling(): jnp.dot(coeffs.T, counts, precision=lax.Precision.HIGHEST, preferred_elem...  1.8 us
  transfers between devices with their start and end apart: 5, of which 1 were waited for; matrix products, arithmetic and copies ran while one was open for 27% of the time, Pallas kernels for 0%

profile of v11, /device:TPU:102, one launch (start us, length us, event | category | flops | bytes accessed | tf_op | source)
XLA Modules:
  0.0 41.8 jit_solution(1693852457815490314)
XLA Ops:
  0.0 2.1 %fusion.13 = (bf16[3,90,2,512]{3,2,1,0:T(2,128)(2,1)S(1)}, bf16[3,90,2,512]{3,2,1,0:T(2,128)(2,1)S(1)}) fusion(bf16[4,90,2,512]{3,2,1,0:T(2,128)(2,1)} %param.6), kind=kLoop, calls=%fused_computation.40 | loop fusion | bytes 2211840 | tf_op jit(solution)/shard_map/slice | solution.py:79
  2.1 5.0 %collective-permute-start.1 = (bf16[3,90,2,512]{3,2,1,0:T(2,128)(2,1)S(1)}, bf16[3,90,2,512]{3,2,1,0:T(2,128)(2,1)S(1)}, u32[]{:S(2)}, u32[]{:S(2)}) collective-permute-start(bf16[3,90,2,512]{3,2,1,0:T(2,128)(2,1)S(1)} %get-tuple-element.15), channel_id=1, source_target_pairs={{0,8},{1,9},{2,10},{3,11},{4,12},{5,13},{6,14},{7,15},{8,16},{9,17... | collective-permute-start | bytes 1658888 | tf_op jit(solution)/shard_map/ppermute | solution.py:76
  7.1 2.6 %collective-permute-start = (bf16[3,6,2,512]{3,2,1,0:T(2,128)(2,1)S(1)}, bf16[3,6,2,512]{3,2,1,0:T(2,128)(2,1)S(1)}, u32[]{:S(2)}, u32[]{:S(2)}) collective-permute-start(bf16[3,6,2,512]{3,2,1,0:T(2,128)(2,1)S(1)} %get-tuple-element.13), channel_id=1, source_target_pairs={{0,9},{1,10},{2,11},{3,12},{4,13},{5,14},{6,15},{7,8},{8,17},{9,18... | collective-permute-start | bytes 110600 | tf_op jit(solution)/shard_map/ppermute | solution.py:76
  9.7 2.0 %collective-permute-start.2 = (bf16[4,6,2,512]{3,2,1,0:T(2,128)(2,1)S(1)}, bf16[4,6,2,512]{3,2,1,0:T(2,128)(2,1)S(1)}, u32[]{:S(2)}, u32[]{:S(2)}) collective-permute-start(bf16[4,6,2,512]{3,2,1,0:T(2,128)(2,1)S(1)} %slice.50), channel_id=1, source_target_pairs={{0,1},{1,2},{2,3},{3,4},{4,5},{5,6},{6,7},{7,0},{8,9},{9,10},{10,1... | collective-permute-start | bytes 147464 | tf_op jit(solution)/shard_map/ppermute | solution.py:76
  11.7 2.4 %collective-permute-start.4 = (bf16[3,90,2,512]{3,2,1,0:T(2,128)(2,1)S(1)}, bf16[3,90,2,512]{3,2,1,0:T(2,128)(2,1)S(1)}, u32[]{:S(2)}, u32[]{:S(2)}) collective-permute-start(bf16[3,90,2,512]{3,2,1,0:T(2,128)(2,1)S(1)} %get-tuple-element.14), channel_id=1, source_target_pairs={{8,0},{9,1},{10,2},{11,3},{12,4},{13,5},{14,6},{15,7},{16,8},{17,9... | collective-permute-start | bytes 1658888 | tf_op jit(solution)/shard_map/ppermute | solution.py:76
  14.1 1.9 %collective-permute-start.3 = (bf16[3,6,2,512]{3,2,1,0:T(2,128)(2,1)S(1)}, bf16[3,6,2,512]{3,2,1,0:T(2,128)(2,1)S(1)}, u32[]{:S(2)}, u32[]{:S(2)}) collective-permute-start(bf16[3,6,2,512]{3,2,1,0:T(2,128)(2,1)S(1)} %get-tuple-element.12), channel_id=1, source_target_pairs={{8,1},{9,2},{10,3},{11,4},{12,5},{13,6},{14,7},{15,0},{16,9},{17,1... | collective-permute-start | bytes 110600 | tf_op jit(solution)/shard_map/ppermute | solution.py:76
  16.1 0.6 %gather_fusion = s32[3,4,4,128]{3,2,1,0:T(4,128)S(1)} fusion(s32[32,4,4,128]{3,2,1,0:T(4,128)S(1)} %copy-done, s32[1024]{0:T(1024)S(1)} %pad_clamp_fusion), kind=kCustom, calls=%fused_computation | custom fusion | bytes 49164 | tf_op jit(solution)/shard_map/jit(_take)/gather | solution.py:22
  16.7 0.1 broadcast_select_fusion
  16.8 0.1 slice_reduce_fusion
  16.9 0.1 copy.11
  17.0 0.6 %gather_fusion.1 = s32[3,3]{1,0:T(4,128)S(1)} fusion(s32[32,3]{1,0:T(8,128)S(1)} %copy.11, s32[1024]{0:T(1024)S(1)} %pad_clamp_fusion), kind=kCustom, calls=%fused_computation.1 | custom fusion | bytes 84 | tf_op jit(solution)/shard_map/jit(_take)/gather | solution.py:23
  17.6 0.1 broadcast_select_fusion.1
  17.6 0.2 negate_reduce_fusion
  17.9 0.1 lt.89
  18.0 0.1 fusion.9
  18.0 0.1 and.97
  18.3 2.4 %fusion = f32[1024,512]{1,0:T(8,128)S(1)} fusion(s32[1536]{0:T(1024)S(1)} %eq.43, s32[1536]{0:T(1024)S(1)} %add_select_fusion), kind=kOutput, calls=%fused_computation.3 | convolution fusion | flops 1612972032 | bytes 2109440 | tf_op jit(solution)/shard_map/dot_general | solution.py:50
  20.8 1.8 %fusion.4.coupling_ref = f32[3,512]{1,0:T(4,128)} fusion(f32[1024,512]{1,0:T(8,128)S(1)} %fusion, f32[1024,3]{0,1:T(4,128)S(1)} %copy-done.2), kind=kOutput, calls=%fused_computation.9 | convolution fusion | flops 18877440 | bytes 2115584 | tf_op jit(solution)/shard_map/dot_general | solution.py:53
  22.6 1.0 %maximum_bitcast_fusion = bf16[96,4,2,512]{3,2,0,1:T(2,128)(2,1)S(1)} fusion(bf16[4,90,2,512]{3,2,1,0:T(2,128)(2,1)S(1)} %copy-done.1, bf16[4,6,2,512]{3,2,1,0:T(2,128)(2,1)S(1)} %collective-permute-done.2), kind=kLoop, calls=%fused_computation.10 | loop fusion | flops 393216 | bytes 1572864 | tf_op jit(solution)/shard_map/transpose | solution.py:61
  23.6 0.5 %copy.13 = bf16[96,4,2,512]{3,2,1,0:T(2,128)(2,1)S(1)} copy(bf16[96,4,2,512]{3,2,0,1:T(2,128)(2,1)S(1)} %maximum_bitcast_fusion) | data formatting | bytes 1572864 | tf_op jit(solution)/shard_map/transpose | solution.py:61
  24.1 0.1 copy.23
  24.3 1.1 %pad.12.own_ref = bf16[512,1024]{1,0:T(8,128)(2,1)} pad(bf16[384,1024]{1,0:T(8,128)(2,1)S(1)} %bitcast.37, bf16[]{:T(256)} %constant.37.clone.1), padding=0_128x0_0 | pad | bytes 1835010 | tf_op jit(solution)/shard_map/jit(_pad)/pad | solution.py:166
  25.4 0.8 %maximum_bitcast_fusion.1 = bf16[96,3,2,512]{3,2,0,1:T(2,128)(2,1)S(1)} fusion(bf16[3,90,2,512]{3,2,1,0:T(2,128)(2,1)S(1)} %collective-permute-done.1, bf16[3,6,2,512]{3,2,1,0:T(2,128)(2,1)S(1)} %collective-permute-done), kind=kLoop, calls=%fused_computation.11 | loop fusion | flops 294912 | bytes 1179648 | tf_op jit(solution)/shard_map/transpose | solution.py:61
  26.2 0.4 copy.12
  26.6 0.1 copy.22
  26.7 0.9 %pad.11.below_ref = bf16[320,1024]{1,0:T(8,128)(2,1)} pad(bf16[288,1024]{1,0:T(8,128)(2,1)S(1)} %bitcast.40, bf16[]{:T(256)} %constant.37.clone.1), padding=0_32x0_0 | pad | bytes 1245186 | tf_op jit(solution)/shard_map/jit(_pad)/pad | solution.py:166
  27.6 4.7 %collective-permute-done.3 = bf16[3,6,2,512]{3,2,1,0:T(2,128)(2,1)S(1)} collective-permute-done((bf16[3,6,2,512]{3,2,1,0:T(2,128)(2,1)S(1)}, bf16[3,6,2,512]{3,2,1,0:T(2,128)(2,1)S(1)}, u32[]{:S(2)}, u32[]{:S(2)}) %collective-permute-start.3) | collective-permute-done | bytes 36896 | tf_op jit(solution)/shard_map/ppermute | solution.py:76
  32.3 0.8 %maximum_bitcast_fusion.2 = bf16[96,3,2,512]{3,2,0,1:T(2,128)(2,1)S(1)} fusion(bf16[3,90,2,512]{3,2,1,0:T(2,128)(2,1)S(1)} %collective-permute-done.4, bf16[3,6,2,512]{3,2,1,0:T(2,128)(2,1)S(1)} %collective-permute-done.3), kind=kLoop, calls=%fused_computation.12 | loop fusion | flops 294912 | bytes 1179648 | tf_op jit(solution)/shard_map/transpose | solution.py:61
  33.1 0.4 copy.14
  33.5 0.1 copy.24
  33.6 0.9 %pad.13.above_ref = bf16[320,1024]{1,0:T(8,128)(2,1)} pad(bf16[288,1024]{1,0:T(8,128)(2,1)S(1)} %bitcast.38, bf16[]{:T(256)} %constant.37.clone.1), padding=0_32x0_0 | pad | bytes 1245186 | tf_op jit(solution)/shard_map/jit(_pad)/pad | solution.py:166
  34.5 7.3 %shard_map.64 = bf16[360,2,512]{2,1,0:T(2,128)(2,1)} custom-call(f32[3,512]{1,0:T(4,128)} %fusion.4.coupling_ref, bf16[320,1024]{1,0:T(8,128)(2,1)} %pad.11.below_ref, bf16[512,1024]{1,0:T(8,128)(2,1)} %pad.12.own_ref, bf16[320,1024]{1,0:T(8,128)(2,1)} %pad.13.above_ref, bf16[1536,512]{1,0:T(8,128)(2,1)} %weight_ref.1, bf16[512,512]{1,0:T(8,128)(2,1)} %mix_ref.1), custom_call_target="tpu_custom_call" | custom-call | flops 2717908992 | bytes 4980736 | tf_op jit(solution)/shard_map/pallas_call | solution.py:169
  (29 shorter events, 0.4 us)
Async XLA Ops:
  0.0 16.1 %copy-start = (s32[32,4,4,128]{3,2,1,0:T(4,128)S(1)}, s32[32,4,4,128]{3,2,1,0:T(4,128)}, u32[]{:S(2)}) copy-start(s32[32,4,4,128]{3,2,1,0:T(4,128)} %param.8) | copy-start | bytes 786436
  0.0 7.0 %copy-start.1 = (bf16[4,90,2,512]{3,2,1,0:T(2,128)(2,1)S(1)}, bf16[4,90,2,512]{3,2,1,0:T(2,128)(2,1)}, u32[]{:S(2)}) copy-start(bf16[4,90,2,512]{3,2,1,0:T(2,128)(2,1)} %param.6) | copy-start | bytes 2211844
  0.0 16.9 %copy-start.3 = (s32[32,3]{0,1:T(4,128)S(1)}, s32[32,3]{0,1:T(4,128)}, u32[]{:S(2)}) copy-start(s32[32,3]{0,1:T(4,128)} %param.9) | copy-start | bytes 1156
  2.1 23.3 %collective-permute-start.1 = (bf16[3,90,2,512]{3,2,1,0:T(2,128)(2,1)S(1)}, bf16[3,90,2,512]{3,2,1,0:T(2,128)(2,1)S(1)}, u32[]{:S(2)}, u32[]{:S(2)}) collective-permute-start(bf16[3,90,2,512]{3,2,1,0:T(2,128)(2,1)S(1)} %get-tuple-element.15), channel_id=1, source_target_pairs={{0,8},{1,9},{2,10},{3,11},{4,12},{5,13},{6,14},{7,15},{8,16},{9,17... | collective-permute-start | bytes 1658888 | tf_op jit(solution)/shard_map/ppermute | solution.py:76
  7.1 18.3 %collective-permute-start = (bf16[3,6,2,512]{3,2,1,0:T(2,128)(2,1)S(1)}, bf16[3,6,2,512]{3,2,1,0:T(2,128)(2,1)S(1)}, u32[]{:S(2)}, u32[]{:S(2)}) collective-permute-start(bf16[3,6,2,512]{3,2,1,0:T(2,128)(2,1)S(1)} %get-tuple-element.13), channel_id=1, source_target_pairs={{0,9},{1,10},{2,11},{3,12},{4,13},{5,14},{6,15},{7,8},{8,17},{9,18... | collective-permute-start | bytes 110600 | tf_op jit(solution)/shard_map/ppermute | solution.py:76
  9.7 12.9 %collective-permute-start.2 = (bf16[4,6,2,512]{3,2,1,0:T(2,128)(2,1)S(1)}, bf16[4,6,2,512]{3,2,1,0:T(2,128)(2,1)S(1)}, u32[]{:S(2)}, u32[]{:S(2)}) collective-permute-start(bf16[4,6,2,512]{3,2,1,0:T(2,128)(2,1)S(1)} %slice.50), channel_id=1, source_target_pairs={{0,1},{1,2},{2,3},{3,4},{4,5},{5,6},{6,7},{7,0},{8,9},{9,10},{10,1... | collective-permute-start | bytes 147464 | tf_op jit(solution)/shard_map/ppermute | solution.py:76
  11.7 20.6 %collective-permute-start.4 = (bf16[3,90,2,512]{3,2,1,0:T(2,128)(2,1)S(1)}, bf16[3,90,2,512]{3,2,1,0:T(2,128)(2,1)S(1)}, u32[]{:S(2)}, u32[]{:S(2)}) collective-permute-start(bf16[3,90,2,512]{3,2,1,0:T(2,128)(2,1)S(1)} %get-tuple-element.14), channel_id=1, source_target_pairs={{8,0},{9,1},{10,2},{11,3},{12,4},{13,5},{14,6},{15,7},{16,8},{17,9... | collective-permute-start | bytes 1658888 | tf_op jit(solution)/shard_map/ppermute | solution.py:76
  14.1 18.2 %collective-permute-start.3 = (bf16[3,6,2,512]{3,2,1,0:T(2,128)(2,1)S(1)}, bf16[3,6,2,512]{3,2,1,0:T(2,128)(2,1)S(1)}, u32[]{:S(2)}, u32[]{:S(2)}) collective-permute-start(bf16[3,6,2,512]{3,2,1,0:T(2,128)(2,1)S(1)} %get-tuple-element.12), channel_id=1, source_target_pairs={{8,1},{9,2},{10,3},{11,4},{12,5},{13,6},{14,7},{15,0},{16,9},{17,1... | collective-permute-start | bytes 110600 | tf_op jit(solution)/shard_map/ppermute | solution.py:76
  18.3 2.4 %copy-start.2 = (f32[1024,3]{0,1:T(4,128)S(1)}, f32[1024,3]{0,1:T(4,128)}, u32[]{:S(2)}) copy-start(f32[1024,3]{0,1:T(4,128)} %param.7) | copy-start | bytes 36868

commit v12 on v11

--- a/solution.py
+++ b/solution.py
@@ -77,9 +77,9 @@
 
     below = move(x[LAT_DEV - OVERHANG :], 1, 0)
     above = move(x[:OVERHANG], -1, 0)
-    below_left = move(tail[LAT_DEV - OVERHANG :], 1, 1)
-    above_left = move(tail[:OVERHANG], -1, 1)
     left = move(tail, 0, 1)
+    below_left = move(left[LAT_DEV - OVERHANG :], 1, 0)
+    above_left = move(left[:OVERHANG], -1, 0)
     return (
         lon_major(jnp.concatenate([below_left, below], axis=1)),
         lon_major(jnp.concatenate([left, x], axis=1)),

time: 42.2 us -> 44 us (1.043)
  starting transfers between devices: 13.8 us -> 16.2 us
  waiting for transfers between devices: 4.72 us -> 4.01 us
    ppermute x5, starting transfers between devices: 13.8 us -> 16.2 us  [move(): return lax.ppermute(value, ('lat', 'lon'), pairs)]
    ppermute x5, waiting for transfers between devices: 4.72 us -> 4.01 us  [move(): return lax.ppermute(value, ('lat', 'lon'), pairs)]
  transfers between devices with their start and end apart: 5 -> 5, of which waited for: 1 -> 1; matrix products, arithmetic and copies ran while one was open for 27% -> 26% of each run, Pallas kernels for 0% -> 0%
where the time goes in v12:
time: 44 us; the launch traced here: 43.5 us
  starting transfers between devices  16.2 us (37%)
  local copies, waits for them, and re-layouts  8.37 us (19%)
  Pallas kernels  7.34 us (17%)
  matrix products  4.22 us (10%)
  waiting for transfers between devices  4.01 us (9%)
  other arithmetic  3.13 us (7%)
    ppermute x5, starting transfers between devices, move(): return lax.ppermute(value, ('lat', 'lon'), pairs)  16.2 us
    pallas_call x1, Pallas kernels, shards(): pl.pallas_call(conv_mix_kernel, out_shape=jax.ShapeDtypeStruct((LAT_DEV *...  7.34 us
    ppermute x5, waiting for transfers between devices, move(): return lax.ppermute(value, ('lat', 'lon'), pairs)  4.01 us
    pad x3, local copies, waits for them, and re-layouts, shards(): pieces.append(jnp.pad(piece, ((0, need - piece.shape[0]), (0, 0))))  2.95 us
    transpose x3, other arithmetic, lon_major(): jnp.transpose(rows, (1, 0, 2, 3)).reshape(nlon * count, members * channels)  2.54 us
    dot_general x1, matrix products, band_coupling(): lax.dot_general(filter_hit, slot_hit, (((0,), (0,)), ((), ())), preferred...  2.42 us
    slice x1, local copies, waits for them, and re-layouts, gather_pieces(): above = move(x[:OVERHANG], -1, 0)  2.06 us
    dot_general x1, matrix products, band_coupling(): jnp.dot(coeffs.T, counts, precision=lax.Precision.HIGHEST, preferred_elem...  1.8 us
  transfers between devices with their start and end apart: 5, of which 1 were waited for; matrix products, arithmetic and copies ran while one was open for 26% of the time, Pallas kernels for 0%

profile of v12, /device:TPU:102, one launch (start us, length us, event | category | flops | bytes accessed | tf_op | source)
XLA Modules:
  0.0 43.5 jit_solution(17105399923576119842)
XLA Ops:
  0.0 2.1 %fusion.12 = (bf16[3,90,2,512]{3,2,1,0:T(2,128)(2,1)S(1)}, bf16[3,90,2,512]{3,2,1,0:T(2,128)(2,1)S(1)}) fusion(bf16[4,90,2,512]{3,2,1,0:T(2,128)(2,1)} %param.6), kind=kLoop, calls=%fused_computation.39 | loop fusion | bytes 2211840 | tf_op jit(solution)/shard_map/slice | solution.py:79
  2.1 5.0 %collective-permute-start.2 = (bf16[3,90,2,512]{3,2,1,0:T(2,128)(2,1)S(1)}, bf16[3,90,2,512]{3,2,1,0:T(2,128)(2,1)S(1)}, u32[]{:S(2)}, u32[]{:S(2)}) collective-permute-start(bf16[3,90,2,512]{3,2,1,0:T(2,128)(2,1)S(1)} %get-tuple-element.13), channel_id=1, source_target_pairs={{0,8},{1,9},{2,10},{3,11},{4,12},{5,13},{6,14},{7,15},{8,16},{9,17... | collective-permute-start | bytes 1658888 | tf_op jit(solution)/shard_map/ppermute | solution.py:76
  7.1 1.9 %collective-permute-start.4 = (bf16[3,90,2,512]{3,2,1,0:T(2,128)(2,1)S(1)}, bf16[3,90,2,512]{3,2,1,0:T(2,128)(2,1)S(1)}, u32[]{:S(2)}, u32[]{:S(2)}) collective-permute-start(bf16[3,90,2,512]{3,2,1,0:T(2,128)(2,1)S(1)} %get-tuple-element.12), channel_id=1, source_target_pairs={{8,0},{9,1},{10,2},{11,3},{12,4},{13,5},{14,6},{15,7},{16,8},{17,9... | collective-permute-start | bytes 1658888 | tf_op jit(solution)/shard_map/ppermute | solution.py:76
  9.1 0.6 %gather_fusion = s32[3,4,4,128]{3,2,1,0:T(4,128)S(1)} fusion(s32[32,4,4,128]{3,2,1,0:T(4,128)S(1)} %copy-done, s32[1024]{0:T(1024)S(1)} %pad_clamp_fusion), kind=kCustom, calls=%fused_computation | custom fusion | bytes 49164 | tf_op jit(solution)/shard_map/jit(_take)/gather | solution.py:22
  9.7 0.1 broadcast_select_fusion
  9.8 0.1 slice_reduce_fusion
  9.9 0.1 copy.11
  10.0 0.6 %gather_fusion.1 = s32[3,3]{1,0:T(4,128)S(1)} fusion(s32[32,3]{1,0:T(8,128)S(1)} %copy.11, s32[1024]{0:T(1024)S(1)} %pad_clamp_fusion), kind=kCustom, calls=%fused_computation.1 | custom fusion | bytes 84 | tf_op jit(solution)/shard_map/jit(_take)/gather | solution.py:23
  10.6 0.1 broadcast_select_fusion.1
  10.6 0.2 negate_reduce_fusion
  10.9 0.1 lt.89
  10.9 0.1 fusion.9
  11.0 0.1 and.97
  11.1 0.1 ge.73
  11.3 2.4 %fusion = f32[1024,512]{1,0:T(8,128)S(1)} fusion(s32[1536]{0:T(1024)S(1)} %eq.43, s32[1536]{0:T(1024)S(1)} %add_select_fusion), kind=kOutput, calls=%fused_computation.3 | convolution fusion | flops 1612972032 | bytes 2109440 | tf_op jit(solution)/shard_map/dot_general | solution.py:50
  13.8 1.8 %fusion.4.coupling_ref = f32[3,512]{1,0:T(4,128)} fusion(f32[1024,512]{1,0:T(8,128)S(1)} %fusion, f32[1024,3]{0,1:T(4,128)S(1)} %copy-done.2), kind=kOutput, calls=%fused_computation.9 | convolution fusion | flops 18877440 | bytes 2115584 | tf_op jit(solution)/shard_map/dot_general | solution.py:53
  15.6 7.2 %collective-permute-start.1 = (bf16[3,6,2,512]{3,2,1,0:T(2,128)(2,1)S(1)}, bf16[3,6,2,512]{3,2,1,0:T(2,128)(2,1)S(1)}, u32[]{:S(2)}, u32[]{:S(2)}) collective-permute-start(bf16[3,6,2,512]{3,2,1,0:T(2,128)(2,1)S(1)} %get-tuple-element.15), channel_id=1, source_target_pairs={{0,8},{1,9},{2,10},{3,11},{4,12},{5,13},{6,14},{7,15},{8,16},{9,17... | collective-permute-start | bytes 110600 | tf_op jit(solution)/shard_map/ppermute | solution.py:76
  22.9 1.0 %maximum_bitcast_fusion = bf16[96,4,2,512]{3,2,0,1:T(2,128)(2,1)S(1)} fusion(bf16[4,90,2,512]{3,2,1,0:T(2,128)(2,1)S(1)} %copy-done.1, bf16[4,6,2,512]{3,2,1,0:T(2,128)(2,1)S(1)} %collective-permute-done), kind=kLoop, calls=%fused_computation.10 | loop fusion | flops 393216 | bytes 1572864 | tf_op jit(solution)/shard_map/transpose | solution.py:61
  23.9 0.5 %copy.13 = bf16[96,4,2,512]{3,2,1,0:T(2,128)(2,1)S(1)} copy(bf16[96,4,2,512]{3,2,0,1:T(2,128)(2,1)S(1)} %maximum_bitcast_fusion) | data formatting | bytes 1572864 | tf_op jit(solution)/shard_map/transpose | solution.py:61
  24.4 0.1 copy.23
  24.6 2.1 %collective-permute-start.3 = (bf16[3,6,2,512]{3,2,1,0:T(2,128)(2,1)S(1)}, bf16[3,6,2,512]{3,2,1,0:T(2,128)(2,1)S(1)}, u32[]{:S(2)}, u32[]{:S(2)}) collective-permute-start(bf16[3,6,2,512]{3,2,1,0:T(2,128)(2,1)S(1)} %get-tuple-element.14), channel_id=1, source_target_pairs={{8,0},{9,1},{10,2},{11,3},{12,4},{13,5},{14,6},{15,7},{16,8},{17,9... | collective-permute-start | bytes 110600 | tf_op jit(solution)/shard_map/ppermute | solution.py:76
  26.7 1.1 %pad.12.own_ref = bf16[512,1024]{1,0:T(8,128)(2,1)} pad(bf16[384,1024]{1,0:T(8,128)(2,1)S(1)} %bitcast.36, bf16[]{:T(256)} %constant.37.clone.1), padding=0_128x0_0 | pad | bytes 1835010 | tf_op jit(solution)/shard_map/jit(_pad)/pad | solution.py:166
  27.8 0.8 %maximum_bitcast_fusion.1 = bf16[96,3,2,512]{3,2,0,1:T(2,128)(2,1)S(1)} fusion(bf16[3,90,2,512]{3,2,1,0:T(2,128)(2,1)S(1)} %collective-permute-done.2, bf16[3,6,2,512]{3,2,1,0:T(2,128)(2,1)S(1)} %collective-permute-done.1), kind=kLoop, calls=%fused_computation.11 | loop fusion | flops 294912 | bytes 1179648 | tf_op jit(solution)/shard_map/transpose | solution.py:61
  28.6 0.4 copy.12
  29.0 0.1 copy.22
  29.1 0.9 %pad.11.below_ref = bf16[320,1024]{1,0:T(8,128)(2,1)} pad(bf16[288,1024]{1,0:T(8,128)(2,1)S(1)} %bitcast.40, bf16[]{:T(256)} %constant.37.clone.1), padding=0_32x0_0 | pad | bytes 1245186 | tf_op jit(solution)/shard_map/jit(_pad)/pad | solution.py:166
  30.0 4.0 %collective-permute-done.3 = bf16[3,6,2,512]{3,2,1,0:T(2,128)(2,1)S(1)} collective-permute-done((bf16[3,6,2,512]{3,2,1,0:T(2,128)(2,1)S(1)}, bf16[3,6,2,512]{3,2,1,0:T(2,128)(2,1)S(1)}, u32[]{:S(2)}, u32[]{:S(2)}) %collective-permute-start.3) | collective-permute-done | bytes 36896 | tf_op jit(solution)/shard_map/ppermute | solution.py:76
  34.0 0.8 %maximum_bitcast_fusion.2 = bf16[96,3,2,512]{3,2,0,1:T(2,128)(2,1)S(1)} fusion(bf16[3,90,2,512]{3,2,1,0:T(2,128)(2,1)S(1)} %collective-permute-done.4, bf16[3,6,2,512]{3,2,1,0:T(2,128)(2,1)S(1)} %collective-permute-done.3), kind=kLoop, calls=%fused_computation.12 | loop fusion | flops 294912 | bytes 1179648 | tf_op jit(solution)/shard_map/transpose | solution.py:61
  34.8 0.4 copy.14
  35.2 0.1 copy.24
  35.3 0.9 %pad.13.above_ref = bf16[320,1024]{1,0:T(8,128)(2,1)} pad(bf16[288,1024]{1,0:T(8,128)(2,1)S(1)} %bitcast.38, bf16[]{:T(256)} %constant.37.clone.1), padding=0_32x0_0 | pad | bytes 1245186 | tf_op jit(solution)/shard_map/jit(_pad)/pad | solution.py:166
  36.2 7.3 %shard_map.64 = bf16[360,2,512]{2,1,0:T(2,128)(2,1)} custom-call(f32[3,512]{1,0:T(4,128)} %fusion.4.coupling_ref, bf16[320,1024]{1,0:T(8,128)(2,1)} %pad.11.below_ref, bf16[512,1024]{1,0:T(8,128)(2,1)} %pad.12.own_ref, bf16[320,1024]{1,0:T(8,128)(2,1)} %pad.13.above_ref, bf16[1536,512]{1,0:T(8,128)(2,1)} %weight_ref.1, bf16[512,512]{1,0:T(8,128)(2,1)} %mix_ref.1), custom_call_target="tpu_custom_call" | custom-call | flops 2717908992 | bytes 4980736 | tf_op jit(solution)/shard_map/pallas_call | solution.py:169
  (29 shorter events, 0.4 us)
Async XLA Ops:
  0.0 9.1 %copy-start = (s32[32,4,4,128]{3,2,1,0:T(4,128)S(1)}, s32[32,4,4,128]{3,2,1,0:T(4,128)}, u32[]{:S(2)}) copy-start(s32[32,4,4,128]{3,2,1,0:T(4,128)} %param.8) | copy-start | bytes 786436
  0.0 7.0 %copy-start.1 = (bf16[4,90,2,512]{3,2,1,0:T(2,128)(2,1)S(1)}, bf16[4,90,2,512]{3,2,1,0:T(2,128)(2,1)}, u32[]{:S(2)}) copy-start(bf16[4,90,2,512]{3,2,1,0:T(2,128)(2,1)} %param.6) | copy-start | bytes 2211844
  0.0 9.9 %copy-start.3 = (s32[32,3]{0,1:T(4,128)S(1)}, s32[32,3]{0,1:T(4,128)}, u32[]{:S(2)}) copy-start(s32[32,3]{0,1:T(4,128)} %param.9) | copy-start | bytes 1156
  2.1 25.7 %collective-permute-start.2 = (bf16[3,90,2,512]{3,2,1,0:T(2,128)(2,1)S(1)}, bf16[3,90,2,512]{3,2,1,0:T(2,128)(2,1)S(1)}, u32[]{:S(2)}, u32[]{:S(2)}) collective-permute-start(bf16[3,90,2,512]{3,2,1,0:T(2,128)(2,1)S(1)} %get-tuple-element.13), channel_id=1, source_target_pairs={{0,8},{1,9},{2,10},{3,11},{4,12},{5,13},{6,14},{7,15},{8,16},{9,17... | collective-permute-start | bytes 1658888 | tf_op jit(solution)/shard_map/ppermute | solution.py:76
  7.1 8.5 %collective-permute-start = (bf16[4,6,2,512]{3,2,1,0:T(2,128)(2,1)S(1)}, bf16[4,6,2,512]{3,2,1,0:T(2,128)(2,1)S(1)}, u32[]{:S(2)}, u32[]{:S(2)}) collective-permute-start(bf16[4,6,2,512]{3,2,1,0:T(2,128)(2,1)S(1)} %slice.46), channel_id=1, source_target_pairs={{0,1},{1,2},{2,3},{3,4},{4,5},{5,6},{6,7},{7,0},{8,9},{9,10},{10,1... | collective-permute-start | bytes 147464 | tf_op jit(solution)/shard_map/ppermute | solution.py:76
  7.1 26.9 %collective-permute-start.4 = (bf16[3,90,2,512]{3,2,1,0:T(2,128)(2,1)S(1)}, bf16[3,90,2,512]{3,2,1,0:T(2,128)(2,1)S(1)}, u32[]{:S(2)}, u32[]{:S(2)}) collective-permute-start(bf16[3,90,2,512]{3,2,1,0:T(2,128)(2,1)S(1)} %get-tuple-element.12), channel_id=1, source_target_pairs={{8,0},{9,1},{10,2},{11,3},{12,4},{13,5},{14,6},{15,7},{16,8},{17,9... | collective-permute-start | bytes 1658888 | tf_op jit(solution)/shard_map/ppermute | solution.py:76
  11.3 2.4 %copy-start.2 = (f32[1024,3]{0,1:T(4,128)S(1)}, f32[1024,3]{0,1:T(4,128)}, u32[]{:S(2)}) copy-start(f32[1024,3]{0,1:T(4,128)} %param.7) | copy-start | bytes 36868
  15.6 12.2 %collective-permute-start.1 = (bf16[3,6,2,512]{3,2,1,0:T(2,128)(2,1)S(1)}, bf16[3,6,2,512]{3,2,1,0:T(2,128)(2,1)S(1)}, u32[]{:S(2)}, u32[]{:S(2)}) collective-permute-start(bf16[3,6,2,512]{3,2,1,0:T(2,128)(2,1)S(1)} %get-tuple-element.15), channel_id=1, source_target_pairs={{0,8},{1,9},{2,10},{3,11},{4,12},{5,13},{6,14},{7,15},{8,16},{9,17... | collective-permute-start | bytes 110600 | tf_op jit(solution)/shard_map/ppermute | solution.py:76
  24.6 9.4 %collective-permute-start.3 = (bf16[3,6,2,512]{3,2,1,0:T(2,128)(2,1)S(1)}, bf16[3,6,2,512]{3,2,1,0:T(2,128)(2,1)S(1)}, u32[]{:S(2)}, u32[]{:S(2)}) collective-permute-start(bf16[3,6,2,512]{3,2,1,0:T(2,128)(2,1)S(1)} %get-tuple-element.14), channel_id=1, source_target_pairs={{8,0},{9,1},{10,2},{11,3},{12,4},{13,5},{14,6},{15,7},{16,8},{17,9... | collective-permute-start | bytes 110600 | tf_op jit(solution)/shard_map/ppermute | solution.py:76

commit v13 on v11

--- a/solution.py
+++ b/solution.py
@@ -91,14 +91,15 @@
 LON_PAD = 32
 TAPS = 128
 WIDTHS = (OVERHANG, LAT_DEV, OVERHANG)
-DEPTHS = (128, 256, 128)
+DEPTHS = (128, 160, 128)
+LANES = (128, 256, 128)
 
 
 def conv_mix_kernel(
     coupling_ref, below_ref, own_ref, above_ref, weight_ref, mix_ref, out_ref, feature_ref, *toeplitz_refs
 ):
     for p in range(3):
-        width, depth = WIDTHS[p], DEPTHS[p]
+        width, depth = WIDTHS[p], LANES[p]
         lane = lax.broadcasted_iota(jnp.int32, (1, TAPS), 1)
         for k in range(BASIS):
             for q in range(LAT_DEV):
@@ -123,7 +124,9 @@
         conv = None
         for p in range(3):
             window = row_refs[p][pl.ds(j * WINDOW * WIDTHS[p], DEPTHS[p]), :]
-            term = jnp.dot(toeplitz_refs[p][...], window, preferred_element_type=jnp.float32)
+            term = jnp.dot(
+                toeplitz_refs[p][:, : DEPTHS[p]], window, preferred_element_type=jnp.float32
+            )
             conv = term if conv is None else conv + term
         for k in range(BASIS):
             for q in range(LAT_DEV):
@@ -172,7 +175,7 @@
         in_specs=[pl.BlockSpec(memory_space=pltpu.VMEM)] * 6,
         out_specs=pl.BlockSpec(memory_space=pltpu.VMEM),
         scratch_shapes=[pltpu.VMEM((BASIS * CHANNELS // 128, out_rows, 128), jnp.float32)]
-        + [pltpu.VMEM((toeplitz_rows, depth), jnp.bfloat16) for depth in DEPTHS],
+        + [pltpu.VMEM((toeplitz_rows, lanes), jnp.bfloat16) for lanes in LANES],
         cost_estimate=pl.CostEstimate(
             flops=2 * toeplitz_rows * sum(DEPTHS) * 1024 * nwin
             + 2 * out_rows * CHANNELS * CHANNELS * (BASIS + 1),

time: 42.2 us -> 42.1 us (level)
  no operation moved by 1% of the time
where the time goes in v13:
time: 42.1 us; the launch traced here: 41.8 us
  starting transfers between devices  13.8 us (33%)
  local copies, waits for them, and re-layouts  8.21 us (20%)
  Pallas kernels  7.28 us (17%)
  waiting for transfers between devices  4.86 us (12%)
  matrix products  4.22 us (10%)
  other arithmetic  3.13 us (7%)
    ppermute x5, starting transfers between devices, move(): return lax.ppermute(value, ('lat', 'lon'), pairs)  13.8 us
    pallas_call x1, Pallas kernels, shards(): pl.pallas_call(conv_mix_kernel, out_shape=jax.ShapeDtypeStruct((LAT_DEV *...  7.28 us
    ppermute x5, waiting for transfers between devices, move(): return lax.ppermute(value, ('lat', 'lon'), pairs)  4.86 us
    pad x3, local copies, waits for them, and re-layouts, shards(): pieces.append(jnp.pad(piece, ((0, need - piece.shape[0]), (0, 0))))  2.8 us
    transpose x3, other arithmetic, lon_major(): jnp.transpose(rows, (1, 0, 2, 3)).reshape(nlon * count, members * channels)  2.54 us
    dot_general x1, matrix products, band_coupling(): lax.dot_general(filter_hit, slot_hit, (((0,), (0,)), ((), ())), preferred...  2.42 us
    slice x1, local copies, waits for them, and re-layouts, gather_pieces(): above = move(x[:OVERHANG], -1, 0)  2.06 us
    dot_general x1, matrix products, band_coupling(): jnp.dot(coeffs.T, counts, precision=lax.Precision.HIGHEST, preferred_elem...  1.8 us
  transfers between devices with their start and end apart: 5, of which 1 were waited for; matrix products, arithmetic and copies ran while one was open for 27% of the time, Pallas kernels for 0%

profile of v13, /device:TPU:102, one launch (start us, length us, event | category | flops | bytes accessed | tf_op | source)
XLA Modules:
  0.0 41.8 jit_solution(12974782274533771313)
XLA Ops:
  0.0 2.1 %fusion.13 = (bf16[3,90,2,512]{3,2,1,0:T(2,128)(2,1)S(1)}, bf16[3,90,2,512]{3,2,1,0:T(2,128)(2,1)S(1)}) fusion(bf16[4,90,2,512]{3,2,1,0:T(2,128)(2,1)} %param.6), kind=kLoop, calls=%fused_computation.40 | loop fusion | bytes 2211840 | tf_op jit(solution)/shard_map/slice | solution.py:79
  2.1 5.0 %collective-permute-start.1 = (bf16[3,90,2,512]{3,2,1,0:T(2,128)(2,1)S(1)}, bf16[3,90,2,512]{3,2,1,0:T(2,128)(2,1)S(1)}, u32[]{:S(2)}, u32[]{:S(2)}) collective-permute-start(bf16[3,90,2,512]{3,2,1,0:T(2,128)(2,1)S(1)} %get-tuple-element.15), channel_id=1, source_target_pairs={{0,8},{1,9},{2,10},{3,11},{4,12},{5,13},{6,14},{7,15},{8,16},{9,17... | collective-permute-start | bytes 1658888 | tf_op jit(solution)/shard_map/ppermute | solution.py:76
  7.1 2.6 %collective-permute-start = (bf16[3,6,2,512]{3,2,1,0:T(2,128)(2,1)S(1)}, bf16[3,6,2,512]{3,2,1,0:T(2,128)(2,1)S(1)}, u32[]{:S(2)}, u32[]{:S(2)}) collective-permute-start(bf16[3,6,2,512]{3,2,1,0:T(2,128)(2,1)S(1)} %get-tuple-element.13), channel_id=1, source_target_pairs={{0,9},{1,10},{2,11},{3,12},{4,13},{5,14},{6,15},{7,8},{8,17},{9,18... | collective-permute-start | bytes 110600 | tf_op jit(solution)/shard_map/ppermute | solution.py:76
  9.7 2.0 %collective-permute-start.2 = (bf16[4,6,2,512]{3,2,1,0:T(2,128)(2,1)S(1)}, bf16[4,6,2,512]{3,2,1,0:T(2,128)(2,1)S(1)}, u32[]{:S(2)}, u32[]{:S(2)}) collective-permute-start(bf16[4,6,2,512]{3,2,1,0:T(2,128)(2,1)S(1)} %slice.50), channel_id=1, source_target_pairs={{0,1},{1,2},{2,3},{3,4},{4,5},{5,6},{6,7},{7,0},{8,9},{9,10},{10,1... | collective-permute-start | bytes 147464 | tf_op jit(solution)/shard_map/ppermute | solution.py:76
  11.7 2.4 %collective-permute-start.4 = (bf16[3,90,2,512]{3,2,1,0:T(2,128)(2,1)S(1)}, bf16[3,90,2,512]{3,2,1,0:T(2,128)(2,1)S(1)}, u32[]{:S(2)}, u32[]{:S(2)}) collective-permute-start(bf16[3,90,2,512]{3,2,1,0:T(2,128)(2,1)S(1)} %get-tuple-element.14), channel_id=1, source_target_pairs={{8,0},{9,1},{10,2},{11,3},{12,4},{13,5},{14,6},{15,7},{16,8},{17,9... | collective-permute-start | bytes 1658888 | tf_op jit(solution)/shard_map/ppermute | solution.py:76
  14.1 1.9 %collective-permute-start.3 = (bf16[3,6,2,512]{3,2,1,0:T(2,128)(2,1)S(1)}, bf16[3,6,2,512]{3,2,1,0:T(2,128)(2,1)S(1)}, u32[]{:S(2)}, u32[]{:S(2)}) collective-permute-start(bf16[3,6,2,512]{3,2,1,0:T(2,128)(2,1)S(1)} %get-tuple-element.12), channel_id=1, source_target_pairs={{8,1},{9,2},{10,3},{11,4},{12,5},{13,6},{14,7},{15,0},{16,9},{17,1... | collective-permute-start | bytes 110600 | tf_op jit(solution)/shard_map/ppermute | solution.py:76
  16.1 0.6 %gather_fusion = s32[3,4,4,128]{3,2,1,0:T(4,128)S(1)} fusion(s32[32,4,4,128]{3,2,1,0:T(4,128)S(1)} %copy-done, s32[1024]{0:T(1024)S(1)} %pad_clamp_fusion), kind=kCustom, calls=%fused_computation | custom fusion | bytes 49164 | tf_op jit(solution)/shard_map/jit(_take)/gather | solution.py:22
  16.7 0.1 broadcast_select_fusion
  16.8 0.1 slice_reduce_fusion
  16.9 0.1 copy.11
  17.0 0.6 %gather_fusion.1 = s32[3,3]{1,0:T(4,128)S(1)} fusion(s32[32,3]{1,0:T(8,128)S(1)} %copy.11, s32[1024]{0:T(1024)S(1)} %pad_clamp_fusion), kind=kCustom, calls=%fused_computation.1 | custom fusion | bytes 84 | tf_op jit(solution)/shard_map/jit(_take)/gather | solution.py:23
  17.6 0.1 broadcast_select_fusion.1
  17.6 0.2 negate_reduce_fusion
  17.9 0.1 lt.89
  18.0 0.1 fusion.9
  18.0 0.1 and.97
  18.3 2.4 %fusion = f32[1024,512]{1,0:T(8,128)S(1)} fusion(s32[1536]{0:T(1024)S(1)} %eq.43, s32[1536]{0:T(1024)S(1)} %add_select_fusion), kind=kOutput, calls=%fused_computation.3 | convolution fusion | flops 1612972032 | bytes 2109440 | tf_op jit(solution)/shard_map/dot_general | solution.py:50
  20.8 1.8 %fusion.4.coupling_ref = f32[3,512]{1,0:T(4,128)} fusion(f32[1024,512]{1,0:T(8,128)S(1)} %fusion, f32[1024,3]{0,1:T(4,128)S(1)} %copy-done.2), kind=kOutput, calls=%fused_computation.9 | convolution fusion | flops 18877440 | bytes 2115584 | tf_op jit(solution)/shard_map/dot_general | solution.py:53
  22.6 1.0 %maximum_bitcast_fusion = bf16[96,4,2,512]{3,2,0,1:T(2,128)(2,1)S(1)} fusion(bf16[4,90,2,512]{3,2,1,0:T(2,128)(2,1)S(1)} %copy-done.1, bf16[4,6,2,512]{3,2,1,0:T(2,128)(2,1)S(1)} %collective-permute-done.2), kind=kLoop, calls=%fused_computation.10 | loop fusion | flops 393216 | bytes 1572864 | tf_op jit(solution)/shard_map/transpose | solution.py:61
  23.6 0.5 %copy.13 = bf16[96,4,2,512]{3,2,1,0:T(2,128)(2,1)S(1)} copy(bf16[96,4,2,512]{3,2,0,1:T(2,128)(2,1)S(1)} %maximum_bitcast_fusion) | data formatting | bytes 1572864 | tf_op jit(solution)/shard_map/transpose | solution.py:61
  24.1 0.1 copy.23
  24.3 1.0 %pad.12.own_ref = bf16[416,1024]{1,0:T(8,128)(2,1)} pad(bf16[384,1024]{1,0:T(8,128)(2,1)S(1)} %bitcast.37, bf16[]{:T(256)} %constant.37.clone.1), padding=0_32x0_0 | pad | bytes 1638402 | tf_op jit(solution)/shard_map/jit(_pad)/pad | solution.py:169
  25.3 0.8 %maximum_bitcast_fusion.1 = bf16[96,3,2,512]{3,2,0,1:T(2,128)(2,1)S(1)} fusion(bf16[3,90,2,512]{3,2,1,0:T(2,128)(2,1)S(1)} %collective-permute-done.1, bf16[3,6,2,512]{3,2,1,0:T(2,128)(2,1)S(1)} %collective-permute-done), kind=kLoop, calls=%fused_computation.11 | loop fusion | flops 294912 | bytes 1179648 | tf_op jit(solution)/shard_map/transpose | solution.py:61
  26.0 0.4 copy.12
  26.5 0.1 copy.22
  26.5 0.9 %pad.11.below_ref = bf16[320,1024]{1,0:T(8,128)(2,1)} pad(bf16[288,1024]{1,0:T(8,128)(2,1)S(1)} %bitcast.40, bf16[]{:T(256)} %constant.37.clone.1), padding=0_32x0_0 | pad | bytes 1245186 | tf_op jit(solution)/shard_map/jit(_pad)/pad | solution.py:169
  27.5 4.9 %collective-permute-done.3 = bf16[3,6,2,512]{3,2,1,0:T(2,128)(2,1)S(1)} collective-permute-done((bf16[3,6,2,512]{3,2,1,0:T(2,128)(2,1)S(1)}, bf16[3,6,2,512]{3,2,1,0:T(2,128)(2,1)S(1)}, u32[]{:S(2)}, u32[]{:S(2)}) %collective-permute-start.3) | collective-permute-done | bytes 36896 | tf_op jit(solution)/shard_map/ppermute | solution.py:76
  32.3 0.8 %maximum_bitcast_fusion.2 = bf16[96,3,2,512]{3,2,0,1:T(2,128)(2,1)S(1)} fusion(bf16[3,90,2,512]{3,2,1,0:T(2,128)(2,1)S(1)} %collective-permute-done.4, bf16[3,6,2,512]{3,2,1,0:T(2,128)(2,1)S(1)} %collective-permute-done.3), kind=kLoop, calls=%fused_computation.12 | loop fusion | flops 294912 | bytes 1179648 | tf_op jit(solution)/shard_map/transpose | solution.py:61
  33.1 0.4 copy.14
  33.5 0.1 copy.24
  33.6 0.9 %pad.13.above_ref = bf16[320,1024]{1,0:T(8,128)(2,1)} pad(bf16[288,1024]{1,0:T(8,128)(2,1)S(1)} %bitcast.38, bf16[]{:T(256)} %constant.37.clone.1), padding=0_32x0_0 | pad | bytes 1245186 | tf_op jit(solution)/shard_map/jit(_pad)/pad | solution.py:169
  34.5 7.3 %shard_map.64 = bf16[360,2,512]{2,1,0:T(2,128)(2,1)} custom-call(f32[3,512]{1,0:T(4,128)} %fusion.4.coupling_ref, bf16[320,1024]{1,0:T(8,128)(2,1)} %pad.11.below_ref, bf16[416,1024]{1,0:T(8,128)(2,1)} %pad.12.own_ref, bf16[320,1024]{1,0:T(8,128)(2,1)} %pad.13.above_ref, bf16[1536,512]{1,0:T(8,128)(2,1)} %weight_ref.1, bf16[512,512]{1,0:T(8,128)(2,1)} %mix_ref.1), custom_call_target="tpu_custom_call" | custom-call | flops 2491416576 | bytes 4784128 | tf_op jit(solution)/shard_map/pallas_call | solution.py:172
  (29 shorter events, 0.4 us)
Async XLA Ops:
  0.0 16.1 %copy-start = (s32[32,4,4,128]{3,2,1,0:T(4,128)S(1)}, s32[32,4,4,128]{3,2,1,0:T(4,128)}, u32[]{:S(2)}) copy-start(s32[32,4,4,128]{3,2,1,0:T(4,128)} %param.8) | copy-start | bytes 786436
  0.0 7.0 %copy-start.1 = (bf16[4,90,2,512]{3,2,1,0:T(2,128)(2,1)S(1)}, bf16[4,90,2,512]{3,2,1,0:T(2,128)(2,1)}, u32[]{:S(2)}) copy-start(bf16[4,90,2,512]{3,2,1,0:T(2,128)(2,1)} %param.6) | copy-start | bytes 2211844
  0.0 16.9 %copy-start.3 = (s32[32,3]{0,1:T(4,128)S(1)}, s32[32,3]{0,1:T(4,128)}, u32[]{:S(2)}) copy-start(s32[32,3]{0,1:T(4,128)} %param.9) | copy-start | bytes 1156
  2.1 23.2 %collective-permute-start.1 = (bf16[3,90,2,512]{3,2,1,0:T(2,128)(2,1)S(1)}, bf16[3,90,2,512]{3,2,1,0:T(2,128)(2,1)S(1)}, u32[]{:S(2)}, u32[]{:S(2)}) collective-permute-start(bf16[3,90,2,512]{3,2,1,0:T(2,128)(2,1)S(1)} %get-tuple-element.15), channel_id=1, source_target_pairs={{0,8},{1,9},{2,10},{3,11},{4,12},{5,13},{6,14},{7,15},{8,16},{9,17... | collective-permute-start | bytes 1658888 | tf_op jit(solution)/shard_map/ppermute | solution.py:76
  7.1 18.2 %collective-permute-start = (bf16[3,6,2,512]{3,2,1,0:T(2,128)(2,1)S(1)}, bf16[3,6,2,512]{3,2,1,0:T(2,128)(2,1)S(1)}, u32[]{:S(2)}, u32[]{:S(2)}) collective-permute-start(bf16[3,6,2,512]{3,2,1,0:T(2,128)(2,1)S(1)} %get-tuple-element.13), channel_id=1, source_target_pairs={{0,9},{1,10},{2,11},{3,12},{4,13},{5,14},{6,15},{7,8},{8,17},{9,18... | collective-permute-start | bytes 110600 | tf_op jit(solution)/shard_map/ppermute | solution.py:76
  9.7 12.9 %collective-permute-start.2 = (bf16[4,6,2,512]{3,2,1,0:T(2,128)(2,1)S(1)}, bf16[4,6,2,512]{3,2,1,0:T(2,128)(2,1)S(1)}, u32[]{:S(2)}, u32[]{:S(2)}) collective-permute-start(bf16[4,6,2,512]{3,2,1,0:T(2,128)(2,1)S(1)} %slice.50), channel_id=1, source_target_pairs={{0,1},{1,2},{2,3},{3,4},{4,5},{5,6},{6,7},{7,0},{8,9},{9,10},{10,1... | collective-permute-start | bytes 147464 | tf_op jit(solution)/shard_map/ppermute | solution.py:76
  11.7 20.6 %collective-permute-start.4 = (bf16[3,90,2,512]{3,2,1,0:T(2,128)(2,1)S(1)}, bf16[3,90,2,512]{3,2,1,0:T(2,128)(2,1)S(1)}, u32[]{:S(2)}, u32[]{:S(2)}) collective-permute-start(bf16[3,90,2,512]{3,2,1,0:T(2,128)(2,1)S(1)} %get-tuple-element.14), channel_id=1, source_target_pairs={{8,0},{9,1},{10,2},{11,3},{12,4},{13,5},{14,6},{15,7},{16,8},{17,9... | collective-permute-start | bytes 1658888 | tf_op jit(solution)/shard_map/ppermute | solution.py:76
  14.1 18.2 %collective-permute-start.3 = (bf16[3,6,2,512]{3,2,1,0:T(2,128)(2,1)S(1)}, bf16[3,6,2,512]{3,2,1,0:T(2,128)(2,1)S(1)}, u32[]{:S(2)}, u32[]{:S(2)}) collective-permute-start(bf16[3,6,2,512]{3,2,1,0:T(2,128)(2,1)S(1)} %get-tuple-element.12), channel_id=1, source_target_pairs={{8,1},{9,2},{10,3},{11,4},{12,5},{13,6},{14,7},{15,0},{16,9},{17,1... | collective-permute-start | bytes 110600 | tf_op jit(solution)/shard_map/ppermute | solution.py:76
  18.3 2.4 %copy-start.2 = (f32[1024,3]{0,1:T(4,128)S(1)}, f32[1024,3]{0,1:T(4,128)}, u32[]{:S(2)}) copy-start(f32[1024,3]{0,1:T(4,128)} %param.7) | copy-start | bytes 36868

commit v14 on v13

--- a/solution.py
+++ b/solution.py
@@ -95,9 +95,7 @@
 LANES = (128, 256, 128)
 
 
-def conv_mix_kernel(
-    coupling_ref, below_ref, own_ref, above_ref, weight_ref, mix_ref, out_ref, feature_ref, *toeplitz_refs
-):
+def toeplitz_kernel(coupling_ref, *toeplitz_refs):
     for p in range(3):
         width, depth = WIDTHS[p], LANES[p]
         lane = lax.broadcasted_iota(jnp.int32, (1, TAPS), 1)
@@ -117,6 +115,12 @@
                     toeplitz_refs[p][pl.ds((k * LAT_DEV + q) * LON_PAD + 8 * g, 8), :] = block.astype(
                         jnp.bfloat16
                     )
+
+
+def conv_mix_kernel(
+    below_t_ref, own_t_ref, above_t_ref, below_ref, own_ref, above_ref, weight_ref, mix_ref, out_ref, feature_ref
+):
+    toeplitz_refs = (below_t_ref, own_t_ref, above_t_ref)
     nlon = out_ref.shape[0] // LAT_DEV
     nwin = -(-nlon // WINDOW)
     row_refs = (below_ref, own_ref, above_ref)
@@ -169,20 +173,28 @@
         pieces.append(jnp.pad(piece, ((0, need - piece.shape[0]), (0, 0))))
     out_rows = members * nlon * LAT_DEV
     toeplitz_rows = BASIS * LAT_DEV * LON_PAD
+    toeplitz = pl.pallas_call(
+        toeplitz_kernel,
+        out_shape=[jax.ShapeDtypeStruct((toeplitz_rows, lanes), jnp.bfloat16) for lanes in LANES],
+        in_specs=[pl.BlockSpec(memory_space=pltpu.VMEM)],
+        out_specs=[pl.BlockSpec(memory_space=pltpu.VMEM)] * 3,
+        cost_estimate=pl.CostEstimate(
+            flops=0, transcendentals=0, bytes_accessed=toeplitz_rows * sum(LANES) * 2
+        ),
+    )(coupling)
     mixed = pl.pallas_call(
         conv_mix_kernel,
         out_shape=jax.ShapeDtypeStruct((LAT_DEV * nlon, members, CHANNELS), jnp.bfloat16),
-        in_specs=[pl.BlockSpec(memory_space=pltpu.VMEM)] * 6,
+        in_specs=[pl.BlockSpec(memory_space=pltpu.VMEM)] * 8,
         out_specs=pl.BlockSpec(memory_space=pltpu.VMEM),
-        scratch_shapes=[pltpu.VMEM((BASIS * CHANNELS // 128, out_rows, 128), jnp.float32)]
-        + [pltpu.VMEM((toeplitz_rows, lanes), jnp.bfloat16) for lanes in LANES],
+        scratch_shapes=[pltpu.VMEM((BASIS * CHANNELS // 128, out_rows, 128), jnp.float32)],
         cost_estimate=pl.CostEstimate(
             flops=2 * toeplitz_rows * sum(DEPTHS) * 1024 * nwin
             + 2 * out_rows * CHANNELS * CHANNELS * (BASIS + 1),
             transcendentals=out_rows * CHANNELS,
             bytes_accessed=sum(p.size for p in pieces) * 2 + (BASIS + 2) * CHANNELS * CHANNELS * 2,
         ),
-    )(coupling, *pieces, conv_weight, mix_weight)
+    )(*toeplitz, *pieces, conv_weight, mix_weight)
     return mixed.reshape(LAT_DEV, nlon, members, CHANNELS)
 
 

time: 42.1 us -> 43.1 us (1.024)
  the two profiles are of different devices: /device:TPU:102 before, /device:TPU:129 now
where the time goes in v14:
time: 43.1 us; the launch traced here: 42.8 us
  starting transfers between devices  17.4 us (40%)
  Pallas kernels  9.55 us (22%)
  local copies, waits for them, and re-layouts  8.27 us (19%)
  matrix products  4.22 us (10%)
  other arithmetic  3.13 us (7%)
    ppermute x5, starting transfers between devices, move(): return lax.ppermute(value, ('lat', 'lon'), pairs)  17.4 us
    pallas_call x1, Pallas kernels, shards(): pl.pallas_call(conv_mix_kernel, out_shape=jax.ShapeDtypeStruct((LAT_DEV *...  6.97 us
    pad x3, local copies, waits for them, and re-layouts, shards(): pieces.append(jnp.pad(piece, ((0, need - piece.shape[0]), (0, 0))))  2.8 us
    pallas_call x1, Pallas kernels, shards(): pl.pallas_call(toeplitz_kernel, out_shape=[jax.ShapeDtypeStruct((toeplitz...  2.57 us
    transpose x3, other arithmetic, lon_major(): jnp.transpose(rows, (1, 0, 2, 3)).reshape(nlon * count, members * channels)  2.54 us
    dot_general x1, matrix products, band_coupling(): lax.dot_general(filter_hit, slot_hit, (((0,), (0,)), ((), ())), preferred...  2.42 us
    slice x1, local copies, waits for them, and re-layouts, gather_pieces(): above = move(x[:OVERHANG], -1, 0)  2.12 us
    dot_general x1, matrix products, band_coupling(): jnp.dot(coeffs.T, counts, precision=lax.Precision.HIGHEST, preferred_elem...  1.8 us
  transfers between devices with their start and end apart: 5, of which 0 were waited for; matrix products, arithmetic and copies ran while one was open for 26% of the time, Pallas kernels for 6%

profile of v14, /device:TPU:129, one launch (start us, length us, event | category | flops | bytes accessed | tf_op | source)
XLA Modules:
  0.0 42.8 jit_solution(5738544808146916394)
XLA Ops:
  0.0 2.1 %fusion.13 = (bf16[3,90,2,512]{3,2,1,0:T(2,128)(2,1)S(1)}, bf16[3,90,2,512]{3,2,1,0:T(2,128)(2,1)S(1)}) fusion(bf16[4,90,2,512]{3,2,1,0:T(2,128)(2,1)} %param.6), kind=kLoop, calls=%fused_computation.40 | loop fusion | bytes 2211840 | tf_op jit(solution)/shard_map/slice | solution.py:79
  2.1 3.1 %collective-permute-start.1 = (bf16[3,90,2,512]{3,2,1,0:T(2,128)(2,1)S(1)}, bf16[3,90,2,512]{3,2,1,0:T(2,128)(2,1)S(1)}, u32[]{:S(2)}, u32[]{:S(2)}) collective-permute-start(bf16[3,90,2,512]{3,2,1,0:T(2,128)(2,1)S(1)} %get-tuple-element.21), channel_id=1, source_target_pairs={{0,8},{1,9},{2,10},{3,11},{4,12},{5,13},{6,14},{7,15},{8,16},{9,17... | collective-permute-start | bytes 1658888 | tf_op jit(solution)/shard_map/ppermute | solution.py:76
  5.3 5.0 %collective-permute-start = (bf16[3,6,2,512]{3,2,1,0:T(2,128)(2,1)S(1)}, bf16[3,6,2,512]{3,2,1,0:T(2,128)(2,1)S(1)}, u32[]{:S(2)}, u32[]{:S(2)}) collective-permute-start(bf16[3,6,2,512]{3,2,1,0:T(2,128)(2,1)S(1)} %get-tuple-element.19), channel_id=1, source_target_pairs={{0,9},{1,10},{2,11},{3,12},{4,13},{5,14},{6,15},{7,8},{8,17},{9,18... | collective-permute-start | bytes 110600 | tf_op jit(solution)/shard_map/ppermute | solution.py:76
  10.4 5.5 %collective-permute-start.4 = (bf16[3,90,2,512]{3,2,1,0:T(2,128)(2,1)S(1)}, bf16[3,90,2,512]{3,2,1,0:T(2,128)(2,1)S(1)}, u32[]{:S(2)}, u32[]{:S(2)}) collective-permute-start(bf16[3,90,2,512]{3,2,1,0:T(2,128)(2,1)S(1)} %get-tuple-element.20), channel_id=1, source_target_pairs={{8,0},{9,1},{10,2},{11,3},{12,4},{13,5},{14,6},{15,7},{16,8},{17,9... | collective-permute-start | bytes 1658888 | tf_op jit(solution)/shard_map/ppermute | solution.py:76
  15.9 3.8 %collective-permute-start.3 = (bf16[3,6,2,512]{3,2,1,0:T(2,128)(2,1)S(1)}, bf16[3,6,2,512]{3,2,1,0:T(2,128)(2,1)S(1)}, u32[]{:S(2)}, u32[]{:S(2)}) collective-permute-start(bf16[3,6,2,512]{3,2,1,0:T(2,128)(2,1)S(1)} %get-tuple-element.18), channel_id=1, source_target_pairs={{8,1},{9,2},{10,3},{11,4},{12,5},{13,6},{14,7},{15,0},{16,9},{17,1... | collective-permute-start | bytes 110600 | tf_op jit(solution)/shard_map/ppermute | solution.py:76
  19.8 0.6 %gather_fusion = s32[3,4,4,128]{3,2,1,0:T(4,128)S(1)} fusion(s32[32,4,4,128]{3,2,1,0:T(4,128)S(1)} %copy-done, s32[1024]{0:T(1024)S(1)} %pad_clamp_fusion), kind=kCustom, calls=%fused_computation | custom fusion | bytes 49164 | tf_op jit(solution)/shard_map/jit(_take)/gather | solution.py:22
  20.4 0.1 broadcast_select_fusion
  20.4 0.1 slice_reduce_fusion
  20.6 0.1 copy.11
  20.7 0.6 %gather_fusion.1 = s32[3,3]{1,0:T(4,128)S(1)} fusion(s32[32,3]{1,0:T(8,128)S(1)} %copy.11, s32[1024]{0:T(1024)S(1)} %pad_clamp_fusion), kind=kCustom, calls=%fused_computation.1 | custom fusion | bytes 84 | tf_op jit(solution)/shard_map/jit(_take)/gather | solution.py:23
  21.2 0.1 broadcast_select_fusion.1
  21.3 0.2 negate_reduce_fusion
  21.5 0.1 lt.89
  21.6 0.1 fusion.9
  21.7 0.1 and.97
  21.8 0.1 ge.73
  22.0 2.4 %fusion = f32[1024,512]{1,0:T(8,128)S(1)} fusion(s32[1536]{0:T(1024)S(1)} %eq.43, s32[1536]{0:T(1024)S(1)} %add_select_fusion), kind=kOutput, calls=%fused_computation.3 | convolution fusion | flops 1612972032 | bytes 2109440 | tf_op jit(solution)/shard_map/dot_general | solution.py:50
  24.4 1.8 %fusion.4.coupling_ref = f32[3,512]{1,0:T(4,128)} fusion(f32[1024,512]{1,0:T(8,128)S(1)} %fusion, f32[1024,3]{0,1:T(4,128)S(1)} %copy-done.2), kind=kOutput, calls=%fused_computation.9 | convolution fusion | flops 18877440 | bytes 2115584 | tf_op jit(solution)/shard_map/dot_general | solution.py:53
  26.2 2.6 %shard_map.64 = (bf16[384,128]{1,0:T(8,128)(2,1)}, bf16[384,256]{1,0:T(8,128)(2,1)}, bf16[384,128]{1,0:T(8,128)(2,1)}) custom-call(f32[3,512]{1,0:T(4,128)} %fusion.4.coupling_ref), custom_call_target="tpu_custom_call" | custom-call | bytes 393216 | tf_op jit(solution)/shard_map/pallas_call | solution.py:176
  28.8 1.0 %maximum_bitcast_fusion = bf16[96,4,2,512]{3,2,0,1:T(2,128)(2,1)S(1)} fusion(bf16[4,90,2,512]{3,2,1,0:T(2,128)(2,1)S(1)} %copy-done.1, bf16[4,6,2,512]{3,2,1,0:T(2,128)(2,1)S(1)} %collective-permute-done.2), kind=kLoop, calls=%fused_computation.10 | loop fusion | flops 393216 | bytes 1572864 | tf_op jit(solution)/shard_map/transpose | solution.py:61
  29.8 0.5 %copy.13 = bf16[96,4,2,512]{3,2,1,0:T(2,128)(2,1)S(1)} copy(bf16[96,4,2,512]{3,2,0,1:T(2,128)(2,1)S(1)} %maximum_bitcast_fusion) | data formatting | bytes 1572864 | tf_op jit(solution)/shard_map/transpose | solution.py:61
  30.4 0.1 copy.23
  30.5 1.0 %pad.12.own_ref = bf16[416,1024]{1,0:T(8,128)(2,1)} pad(bf16[384,1024]{1,0:T(8,128)(2,1)S(1)} %bitcast.37, bf16[]{:T(256)} %constant.37.clone.1), padding=0_32x0_0 | pad | bytes 1638402 | tf_op jit(solution)/shard_map/jit(_pad)/pad | solution.py:173
  31.5 0.8 %maximum_bitcast_fusion.1 = bf16[96,3,2,512]{3,2,0,1:T(2,128)(2,1)S(1)} fusion(bf16[3,90,2,512]{3,2,1,0:T(2,128)(2,1)S(1)} %collective-permute-done.1, bf16[3,6,2,512]{3,2,1,0:T(2,128)(2,1)S(1)} %collective-permute-done), kind=kLoop, calls=%fused_computation.11 | loop fusion | flops 294912 | bytes 1179648 | tf_op jit(solution)/shard_map/transpose | solution.py:61
  32.3 0.4 copy.12
  32.7 0.1 copy.22
  32.8 0.9 %pad.11.below_ref = bf16[320,1024]{1,0:T(8,128)(2,1)} pad(bf16[288,1024]{1,0:T(8,128)(2,1)S(1)} %bitcast.40, bf16[]{:T(256)} %constant.37.clone.1), padding=0_32x0_0 | pad | bytes 1245186 | tf_op jit(solution)/shard_map/jit(_pad)/pad | solution.py:173
  33.7 0.8 %maximum_bitcast_fusion.2 = bf16[96,3,2,512]{3,2,0,1:T(2,128)(2,1)S(1)} fusion(bf16[3,90,2,512]{3,2,1,0:T(2,128)(2,1)S(1)} %collective-permute-done.4, bf16[3,6,2,512]{3,2,1,0:T(2,128)(2,1)S(1)} %collective-permute-done.3), kind=kLoop, calls=%fused_computation.12 | loop fusion | flops 294912 | bytes 1179648 | tf_op jit(solution)/shard_map/transpose | solution.py:61
  34.5 0.4 copy.14
  34.9 0.1 copy.24
  35.0 0.9 %pad.13.above_ref = bf16[320,1024]{1,0:T(8,128)(2,1)} pad(bf16[288,1024]{1,0:T(8,128)(2,1)S(1)} %bitcast.38, bf16[]{:T(256)} %constant.37.clone.1), padding=0_32x0_0 | pad | bytes 1245186 | tf_op jit(solution)/shard_map/jit(_pad)/pad | solution.py:173
  35.9 7.0 %shard_map.65 = bf16[360,2,512]{2,1,0:T(2,128)(2,1)} custom-call(bf16[384,128]{1,0:T(8,128)(2,1)} %get-tuple-element.8.below_t_ref, bf16[384,256]{1,0:T(8,128)(2,1)} %get-tuple-element.9.own_t_ref, bf16[384,128]{1,0:T(8,128)(2,1)} %get-tuple-element.10.above_t_ref, bf16[320,1024]{1,0:T(8,128)(2,1)} %pad.11.below_ref, bf16[416,1024]{1,0:T(8,128)(2,1)} %pad.12.own_ref, ...), custom_call_target="tpu_custom_call" | custom-call | flops 2491416576 | bytes 4784128 | tf_op jit(solution)/shard_map/pallas_call | solution.py:185
  (30 shorter events, 0.4 us)
Async XLA Ops:
  0.0 19.8 %copy-start = (s32[32,4,4,128]{3,2,1,0:T(4,128)S(1)}, s32[32,4,4,128]{3,2,1,0:T(4,128)}, u32[]{:S(2)}) copy-start(s32[32,4,4,128]{3,2,1,0:T(4,128)} %param.8) | copy-start | bytes 786436
  0.0 5.3 %copy-start.1 = (bf16[4,90,2,512]{3,2,1,0:T(2,128)(2,1)S(1)}, bf16[4,90,2,512]{3,2,1,0:T(2,128)(2,1)}, u32[]{:S(2)}) copy-start(bf16[4,90,2,512]{3,2,1,0:T(2,128)(2,1)} %param.6) | copy-start | bytes 2211844
  0.0 20.6 %copy-start.3 = (s32[32,3]{0,1:T(4,128)S(1)}, s32[32,3]{0,1:T(4,128)}, u32[]{:S(2)}) copy-start(s32[32,3]{0,1:T(4,128)} %param.9) | copy-start | bytes 1156
  2.1 29.3 %collective-permute-start.1 = (bf16[3,90,2,512]{3,2,1,0:T(2,128)(2,1)S(1)}, bf16[3,90,2,512]{3,2,1,0:T(2,128)(2,1)S(1)}, u32[]{:S(2)}, u32[]{:S(2)}) collective-permute-start(bf16[3,90,2,512]{3,2,1,0:T(2,128)(2,1)S(1)} %get-tuple-element.21), channel_id=1, source_target_pairs={{0,8},{1,9},{2,10},{3,11},{4,12},{5,13},{6,14},{7,15},{8,16},{9,17... | collective-permute-start | bytes 1658888 | tf_op jit(solution)/shard_map/ppermute | solution.py:76
  5.3 26.2 %collective-permute-start = (bf16[3,6,2,512]{3,2,1,0:T(2,128)(2,1)S(1)}, bf16[3,6,2,512]{3,2,1,0:T(2,128)(2,1)S(1)}, u32[]{:S(2)}, u32[]{:S(2)}) collective-permute-start(bf16[3,6,2,512]{3,2,1,0:T(2,128)(2,1)S(1)} %get-tuple-element.19), channel_id=1, source_target_pairs={{0,9},{1,10},{2,11},{3,12},{4,13},{5,14},{6,15},{7,8},{8,17},{9,18... | collective-permute-start | bytes 110600 | tf_op jit(solution)/shard_map/ppermute | solution.py:76
  10.4 18.4 %collective-permute-start.2 = (bf16[4,6,2,512]{3,2,1,0:T(2,128)(2,1)S(1)}, bf16[4,6,2,512]{3,2,1,0:T(2,128)(2,1)S(1)}, u32[]{:S(2)}, u32[]{:S(2)}) collective-permute-start(bf16[4,6,2,512]{3,2,1,0:T(2,128)(2,1)S(1)} %slice.50), channel_id=1, source_target_pairs={{0,1},{1,2},{2,3},{3,4},{4,5},{5,6},{6,7},{7,0},{8,9},{9,10},{10,1... | collective-permute-start | bytes 147464 | tf_op jit(solution)/shard_map/ppermute | solution.py:76
  10.4 23.3 %collective-permute-start.4 = (bf16[3,90,2,512]{3,2,1,0:T(2,128)(2,1)S(1)}, bf16[3,90,2,512]{3,2,1,0:T(2,128)(2,1)S(1)}, u32[]{:S(2)}, u32[]{:S(2)}) collective-permute-start(bf16[3,90,2,512]{3,2,1,0:T(2,128)(2,1)S(1)} %get-tuple-element.20), channel_id=1, source_target_pairs={{8,0},{9,1},{10,2},{11,3},{12,4},{13,5},{14,6},{15,7},{16,8},{17,9... | collective-permute-start | bytes 1658888 | tf_op jit(solution)/shard_map/ppermute | solution.py:76
  15.9 17.8 %collective-permute-start.3 = (bf16[3,6,2,512]{3,2,1,0:T(2,128)(2,1)S(1)}, bf16[3,6,2,512]{3,2,1,0:T(2,128)(2,1)S(1)}, u32[]{:S(2)}, u32[]{:S(2)}) collective-permute-start(bf16[3,6,2,512]{3,2,1,0:T(2,128)(2,1)S(1)} %get-tuple-element.18), channel_id=1, source_target_pairs={{8,1},{9,2},{10,3},{11,4},{12,5},{13,6},{14,7},{15,0},{16,9},{17,1... | collective-permute-start | bytes 110600 | tf_op jit(solution)/shard_map/ppermute | solution.py:76
  22.0 2.4 %copy-start.2 = (f32[1024,3]{0,1:T(4,128)S(1)}, f32[1024,3]{0,1:T(4,128)}, u32[]{:S(2)}) copy-start(f32[1024,3]{0,1:T(4,128)} %param.7) | copy-start | bytes 36868

commit v15 on v13

--- a/solution.py
+++ b/solution.py
@@ -65,26 +65,12 @@
     nlat = lax.axis_size("lat")
     nlon = lax.axis_size("lon")
     lo = SHIFTS - 1
-    tail = x[:, x.shape[1] - lo :]
-
-    def move(value, dlat, dlon):
-        pairs = []
-        for b in range(nlat):
-            if 0 <= b + dlat < nlat:
-                for j in range(nlon):
-                    pairs.append((b * nlon + j, (b + dlat) * nlon + (j + dlon) % nlon))
-        return lax.ppermute(value, ("lat", "lon"), pairs)
-
-    below = move(x[LAT_DEV - OVERHANG :], 1, 0)
-    above = move(x[:OVERHANG], -1, 0)
-    below_left = move(tail[LAT_DEV - OVERHANG :], 1, 1)
-    above_left = move(tail[:OVERHANG], -1, 1)
-    left = move(tail, 0, 1)
-    return (
-        lon_major(jnp.concatenate([below_left, below], axis=1)),
-        lon_major(jnp.concatenate([left, x], axis=1)),
-        lon_major(jnp.concatenate([above_left, above], axis=1)),
-    )
+    left = lax.ppermute(x[:, x.shape[1] - lo :], "lon", [(j, (j + 1) % nlon) for j in range(nlon)])
+    ext = jnp.concatenate([left, x], axis=1)
+    down = [(b, b + 1) for b in range(nlat - 1)]
+    below = lax.ppermute(ext[LAT_DEV - OVERHANG :], "lat", down)
+    above = lax.ppermute(ext[:OVERHANG], "lat", [(t, s) for s, t in down])
+    return lon_major(below), lon_major(ext), lon_major(above)
 
 
 WINDOW = 32

time: 42.1 us -> 42.1 us (level)
  waiting for transfers between devices: 4.86 us -> 12.6 us
  starting transfers between devices: 13.8 us -> 6.89 us
  other arithmetic: 3.13 us -> 0.58 us
  local copies, waits for them, and re-layouts: 8.21 us -> 10 us
    ppermute x5 -> x3, waiting for transfers between devices: 4.86 us -> 12.6 us  [the longest x1 6.03 us: gather_pieces(): above = lax.ppermute(ext[:OVERHANG], 'lat', [(t, s) for s, t in down])]
    ppermute x5 -> x3, starting transfers between devices: 13.8 us -> 6.89 us  [the longest x1 4.95 us: gather_pieces(): below = lax.ppermute(ext[LAT_DEV - OVERHANG:], 'lat', down)]
    transpose x3 -> x0, other arithmetic: 2.54 us -> none  [lon_major(): jnp.transpose(rows, (1, 0, 2, 3)).reshape(nlon * count, members * channels)]
    concatenate x0 -> x1, local copies, waits for them, and re-layouts: none -> 1.69 us  [gather_pieces(): ext = jnp.concatenate([left, x], axis=1)]
    unnamed x12 -> x9, local copies, waits for them, and re-layouts: 0.4 us -> 1.1 us
    slice x3 -> x2, local copies, waits for them, and re-layouts: 2.15 us -> 1.55 us  [the longest x1 0.88 us: gather_pieces(): x[:, x.shape[1] - lo:]]
  transfers between devices with their start and end apart: 5 -> 3, of which waited for: 1 -> 3; matrix products, arithmetic and copies ran while one was open for 27% -> 24% of each run, Pallas kernels for 0% -> 0%
where the time goes in v15:
time: 42.1 us; the launch traced here: 41.7 us
  waiting for transfers between devices  12.6 us (30%)
  local copies, waits for them, and re-layouts  10 us (24%)
  Pallas kernels  7.27 us (17%)
  starting transfers between devices  6.89 us (16%)
  matrix products  4.22 us (10%)
  other arithmetic  0.58 us (1%)
    pallas_call x1, Pallas kernels, shards(): pl.pallas_call(conv_mix_kernel, out_shape=jax.ShapeDtypeStruct((LAT_DEV *...  7.27 us
    ppermute x1, waiting for transfers between devices, gather_pieces(): above = lax.ppermute(ext[:OVERHANG], 'lat', [(t, s) for s, t in down])  6.03 us
    ppermute x1, starting transfers between devices, gather_pieces(): below = lax.ppermute(ext[LAT_DEV - OVERHANG:], 'lat', down)  4.95 us
    ppermute x1, waiting for transfers between devices, gather_pieces(): below = lax.ppermute(ext[LAT_DEV - OVERHANG:], 'lat', down)  4.79 us
    pad x3, local copies, waits for them, and re-layouts, shards(): pieces.append(jnp.pad(piece, ((0, need - piece.shape[0]), (0, 0))))  2.8 us
    dot_general x1, matrix products, band_coupling(): lax.dot_general(filter_hit, slot_hit, (((0,), (0,)), ((), ())), preferred...  2.42 us
    ppermute x1, starting transfers between devices, gather_pieces(): above = lax.ppermute(ext[:OVERHANG], 'lat', [(t, s) for s, t in down])  1.92 us
    dot_general x1, matrix products, band_coupling(): jnp.dot(coeffs.T, counts, precision=lax.Precision.HIGHEST, preferred_elem...  1.8 us
  transfers between devices with their start and end apart: 3, of which 3 were waited for; matrix products, arithmetic and copies ran while one was open for 24% of the time, Pallas kernels for 0%

profile of v15, /device:TPU:102, one launch (start us, length us, event | category | flops | bytes accessed | tf_op | source)
XLA Modules:
  0.0 41.7 jit_solution(13455318328413497723)
XLA Ops:
  0.0 0.9 %slice.40 = bf16[4,6,2,512]{3,2,1,0:T(2,128)(2,1)S(1)} slice(bf16[4,90,2,512]{3,2,1,0:T(2,128)(2,1)} %param.6), slice={[0:4], [84:90], [0:2], [0:512]} | slice | bytes 98304 | tf_op jit(solution)/shard_map/slice | solution.py:68
  1.0 0.6 %gather_fusion = s32[3,4,4,128]{3,2,1,0:T(4,128)S(1)} fusion(s32[32,4,4,128]{3,2,1,0:T(4,128)S(1)} %copy-done, s32[1024]{0:T(1024)S(1)} %pad_clamp_fusion), kind=kCustom, calls=%fused_computation | custom fusion | bytes 49164 | tf_op jit(solution)/shard_map/jit(_take)/gather | solution.py:22
  1.6 0.1 broadcast_select_fusion
  1.6 0.1 slice_reduce_fusion
  1.8 0.8 %copy.11 = s32[32,3]{1,0:T(8,128)S(1)} copy(s32[32,3]{0,1:T(4,128)} %param.9) | data formatting | bytes 768 | tf_op args[3]
  2.5 0.6 %gather_fusion.1 = s32[3,3]{1,0:T(4,128)S(1)} fusion(s32[32,3]{1,0:T(8,128)S(1)} %copy.11, s32[1024]{0:T(1024)S(1)} %pad_clamp_fusion), kind=kCustom, calls=%fused_computation.1 | custom fusion | bytes 84 | tf_op jit(solution)/shard_map/jit(_take)/gather | solution.py:23
  3.1 0.1 broadcast_select_fusion.1
  3.2 0.2 negate_reduce_fusion
  3.4 0.1 lt.89
  3.5 0.1 fusion.9
  3.5 0.1 and.97
  3.6 0.1 ge.73
  3.7 0.1 sub.60
  3.8 1.8 %collective-permute-done = bf16[4,6,2,512]{3,2,1,0:T(2,128)(2,1)S(1)} collective-permute-done((bf16[4,6,2,512]{3,2,1,0:T(2,128)(2,1)S(1)}, bf16[4,6,2,512]{3,2,1,0:T(2,128)(2,1)S(1)}, u32[]{:S(2)}, u32[]{:S(2)}) %collective-permute-start) | collective-permute-done | bytes 49184 | tf_op jit(solution)/shard_map/ppermute | solution.py:68
  5.7 1.7 %constant_dynamic-update-slice_fusion = bf16[4,96,2,512]{3,2,1,0:T(2,128)(2,1)S(1)} fusion(bf16[4,96,2,512]{3,2,1,0:T(2,128)(2,1)S(1)} %constant_dynamic-update-slice_fusion.1, bf16[4,90,2,512]{3,2,1,0:T(2,128)(2,1)} %param.6), kind=kLoop, calls=%fused_computation.22 | loop fusion | bytes 1474560 | tf_op jit(solution)/shard_map/concatenate | solution.py:69
  7.3 0.7 %fusion.12 = (bf16[3,96,2,512]{3,2,1,0:T(2,128)(2,1)S(1)}, bf16[3,96,2,512]{3,2,1,0:T(2,128)(2,1)S(1)}) fusion(bf16[4,96,2,512]{3,2,1,0:T(2,128)(2,1)S(1)} %constant_dynamic-update-slice_fusion), kind=kLoop, calls=%fused_computation.38 | loop fusion | bytes 2359296 | tf_op jit(solution)/shard_map/slice | solution.py:72
  8.0 5.0 %collective-permute-start.1 = (bf16[3,96,2,512]{3,2,1,0:T(2,128)(2,1)S(1)}, bf16[3,96,2,512]{3,2,1,0:T(2,128)(2,1)S(1)}, u32[]{:S(2)}, u32[]{:S(2)}) collective-permute-start(bf16[3,96,2,512]{3,2,1,0:T(2,128)(2,1)S(1)} %get-tuple-element.13), channel_id=1, source_target_pairs={{0,8},{8,16},{16,24},{24,32},{32,40},{40,48},{48,56},{56,64},{64,7... | collective-permute-start | bytes 1769480 | tf_op jit(solution)/shard_map/ppermute | solution.py:71
  13.0 1.9 %collective-permute-start.2 = (bf16[3,96,2,512]{3,2,1,0:T(2,128)(2,1)S(1)}, bf16[3,96,2,512]{3,2,1,0:T(2,128)(2,1)S(1)}, u32[]{:S(2)}, u32[]{:S(2)}) collective-permute-start(bf16[3,96,2,512]{3,2,1,0:T(2,128)(2,1)S(1)} %get-tuple-element.12), channel_id=1, source_target_pairs={{8,0},{16,8},{24,16},{32,24},{40,32},{48,40},{56,48},{64,56},{72,6... | collective-permute-start | bytes 1769480 | tf_op jit(solution)/shard_map/ppermute | solution.py:72
  14.9 2.4 %fusion = f32[1024,512]{1,0:T(8,128)S(1)} fusion(s32[1536]{0:T(1024)S(1)} %eq.43, s32[1536]{0:T(1024)S(1)} %add_select_fusion), kind=kOutput, calls=%fused_computation.3 | convolution fusion | flops 1612972032 | bytes 2109440 | tf_op jit(solution)/shard_map/dot_general | solution.py:50
  17.4 1.8 %fusion.4.coupling_ref = f32[3,512]{1,0:T(4,128)} fusion(f32[1024,512]{1,0:T(8,128)S(1)} %fusion, f32[1024,3]{0,1:T(4,128)S(1)} %copy-done.1), kind=kOutput, calls=%fused_computation.9 | convolution fusion | flops 18877440 | bytes 2115584 | tf_op jit(solution)/shard_map/dot_general | solution.py:53
  19.2 0.5 %copy.13 = bf16[96,4,2,512]{3,2,1,0:T(2,128)(2,1)S(1)} copy(bf16[96,4,2,512]{3,2,0,1:T(2,128)(2,1)S(1)} %bitcast.33) | data formatting | bytes 1572864 | tf_op jit(solution)/shard_map/transpose | solution.py:61
  19.7 0.1 copy.23
  19.8 1.0 %pad.12.own_ref = bf16[416,1024]{1,0:T(8,128)(2,1)} pad(bf16[384,1024]{1,0:T(8,128)(2,1)S(1)} %bitcast.35, bf16[]{:T(256)} %constant.37.clone.1), padding=0_32x0_0 | pad | bytes 1638402 | tf_op jit(solution)/shard_map/jit(_pad)/pad | solution.py:155
  20.8 4.8 %collective-permute-done.1 = bf16[3,96,2,512]{3,2,1,0:T(2,128)(2,1)S(1)} collective-permute-done((bf16[3,96,2,512]{3,2,1,0:T(2,128)(2,1)S(1)}, bf16[3,96,2,512]{3,2,1,0:T(2,128)(2,1)S(1)}, u32[]{:S(2)}, u32[]{:S(2)}) %collective-permute-start.1) | collective-permute-done | bytes 589856 | tf_op jit(solution)/shard_map/ppermute | solution.py:71
  25.6 0.4 copy.12
  26.0 0.1 copy.22
  26.1 0.9 %pad.11.below_ref = bf16[320,1024]{1,0:T(8,128)(2,1)} pad(bf16[288,1024]{1,0:T(8,128)(2,1)S(1)} %bitcast.38, bf16[]{:T(256)} %constant.37.clone.1), padding=0_32x0_0 | pad | bytes 1245186 | tf_op jit(solution)/shard_map/jit(_pad)/pad | solution.py:155
  27.0 6.0 %collective-permute-done.2 = bf16[3,96,2,512]{3,2,1,0:T(2,128)(2,1)S(1)} collective-permute-done((bf16[3,96,2,512]{3,2,1,0:T(2,128)(2,1)S(1)}, bf16[3,96,2,512]{3,2,1,0:T(2,128)(2,1)S(1)}, u32[]{:S(2)}, u32[]{:S(2)}) %collective-permute-start.2) | collective-permute-done | bytes 589856 | tf_op jit(solution)/shard_map/ppermute | solution.py:72
  33.1 0.4 copy.14
  33.5 0.1 copy.24
  33.6 0.9 %pad.13.above_ref = bf16[320,1024]{1,0:T(8,128)(2,1)} pad(bf16[288,1024]{1,0:T(8,128)(2,1)S(1)} %bitcast.36, bf16[]{:T(256)} %constant.37.clone.1), padding=0_32x0_0 | pad | bytes 1245186 | tf_op jit(solution)/shard_map/jit(_pad)/pad | solution.py:155
  34.5 7.3 %shard_map.64 = bf16[360,2,512]{2,1,0:T(2,128)(2,1)} custom-call(f32[3,512]{1,0:T(4,128)} %fusion.4.coupling_ref, bf16[320,1024]{1,0:T(8,128)(2,1)} %pad.11.below_ref, bf16[416,1024]{1,0:T(8,128)(2,1)} %pad.12.own_ref, bf16[320,1024]{1,0:T(8,128)(2,1)} %pad.13.above_ref, bf16[1536,512]{1,0:T(8,128)(2,1)} %weight_ref.1, bf16[512,512]{1,0:T(8,128)(2,1)} %mix_ref.1), custom_call_target="tpu_custom_call" | custom-call | flops 2491416576 | bytes 4784128 | tf_op jit(solution)/shard_map/pallas_call | solution.py:158
  (19 shorter events, 0.2 us)
Async XLA Ops:
  0.0 1.0 %copy-start = (s32[32,4,4,128]{3,2,1,0:T(4,128)S(1)}, s32[32,4,4,128]{3,2,1,0:T(4,128)}, u32[]{:S(2)}) copy-start(s32[32,4,4,128]{3,2,1,0:T(4,128)} %param.8) | copy-start | bytes 786436
  0.9 4.7 %collective-permute-start = (bf16[4,6,2,512]{3,2,1,0:T(2,128)(2,1)S(1)}, bf16[4,6,2,512]{3,2,1,0:T(2,128)(2,1)S(1)}, u32[]{:S(2)}, u32[]{:S(2)}) collective-permute-start(bf16[4,6,2,512]{3,2,1,0:T(2,128)(2,1)S(1)} %slice.40), channel_id=1, source_target_pairs={{0,1},{1,2},{2,3},{3,4},{4,5},{5,6},{6,7},{7,0},{8,9},{9,10},{10,1... | collective-permute-start | bytes 147464 | tf_op jit(solution)/shard_map/ppermute | solution.py:68
  8.0 17.6 %collective-permute-start.1 = (bf16[3,96,2,512]{3,2,1,0:T(2,128)(2,1)S(1)}, bf16[3,96,2,512]{3,2,1,0:T(2,128)(2,1)S(1)}, u32[]{:S(2)}, u32[]{:S(2)}) collective-permute-start(bf16[3,96,2,512]{3,2,1,0:T(2,128)(2,1)S(1)} %get-tuple-element.13), channel_id=1, source_target_pairs={{0,8},{8,16},{16,24},{24,32},{32,40},{40,48},{48,56},{56,64},{64,7... | collective-permute-start | bytes 1769480 | tf_op jit(solution)/shard_map/ppermute | solution.py:71
  13.0 4.4 %copy-start.1 = (f32[1024,3]{0,1:T(4,128)S(1)}, f32[1024,3]{0,1:T(4,128)}, u32[]{:S(2)}) copy-start(f32[1024,3]{0,1:T(4,128)} %param.7) | copy-start | bytes 36868
  13.0 20.1 %collective-permute-start.2 = (bf16[3,96,2,512]{3,2,1,0:T(2,128)(2,1)S(1)}, bf16[3,96,2,512]{3,2,1,0:T(2,128)(2,1)S(1)}, u32[]{:S(2)}, u32[]{:S(2)}) collective-permute-start(bf16[3,96,2,512]{3,2,1,0:T(2,128)(2,1)S(1)} %get-tuple-element.12), channel_id=1, source_target_pairs={{8,0},{16,8},{24,16},{32,24},{40,32},{48,40},{56,48},{64,56},{72,6... | collective-permute-start | bytes 1769480 | tf_op jit(solution)/shard_map/ppermute | solution.py:72
